TPU v7x, 768 devices: a whole 4x8x12 slice. The times are simulated.
768 devices in a mesh: band: 6 (over z_lo), pw: 128 (over z_hi, x, y, core).
Axes of the slice: x: 4, y: 8, z: 12 (z_hi: 2, z_lo: 6; z = z_hi * 6 + z_lo), core: 2. Of those that a mesh axis runs over, the one named last changes fastest.
Arguments:
- states: bfloat16 [18, 884736], P('band', 'pw'), may hold values from -12 to 12
- slot_map: int32 [884736], P('pw'), may hold values from 0 to 9215, as said below
- potential: float32 [128, 128, 128], P('pw'), may hold values from -5 to 5
- projectors: bfloat16 [512, 884736], P(None, 'pw'), may hold values from -6 to 6
- species: int32 [64], replicated, may hold values from 0 to 3
- coupling: float32 [4, 8, 8], replicated, may hold values from -2.4 to 2.4
Outputs:
- applied: float32 [18, 884736], P('band', 'pw')
- subspace: float32 [18, 18], P('band')
Inputs may be any that keep to these rules, and one draw needn't show every extreme that they name: `slot_map`: within each aligned block of 6912 entries the values are distinct, and each block holds the value 72 * 128 - 1.
All inputs are finite; a program needn't handle non-finite values.
Results may differ from a plain program's by a relative error of at most 0.0019.
Values may be sent and summed in bfloat16 or wider, within the bound.
No kernel may reach another device: no remote copies, remote signals or barrier semaphores. Data moves between devices by JAX's collectives and lax.ppermute only.
A program may use at most 64 MiB of HBM per device.

v0:
```python
import functools
import math

import jax
import jax.numpy as jnp
from jax import lax
from jax.sharding import Mesh
from jax.sharding import PartitionSpec as P

NSIDE = 96
NG = 884736
PW = ("pw_0", "pw_1", "pw_2", "pw_3")


def cut_along(x, dim, length):
    shape = x.shape
    pieces = x.reshape(*shape[:dim], length, shape[dim] // length, *shape[dim + 1 :])
    return jnp.moveaxis(pieces, dim, 0)


def joined_along(pieces, dim):
    pieces = jnp.moveaxis(pieces, 0, dim)
    shape = pieces.shape
    return pieces.reshape(*shape[:dim], shape[dim] * shape[dim + 1], *shape[dim + 2 :])


def moved_by_axis(pieces, axes, order):
    inside = pieces.shape[1:]
    whole = pieces.reshape(*(lax.axis_size(a) for a in axes), *inside)
    for k in order:
        whole = lax.all_to_all(whole, axes[k], k, k, tiled=True)
    return whole.reshape(-1, *inside)


def exchange_by_chip(x, groups, order, split_dim, concat_dim):
    length = lax.axis_size(groups[0]) * lax.axis_size(groups[1])
    pieces = cut_along(x, split_dim, length)
    return joined_along(moved_by_axis(pieces, groups, order), concat_dim)


def one_axis_at_a_time(x, axes):
    return functools.reduce(lax.psum, axes, x)


def from_everyone(x, axis):
    length = lax.axis_size(axis)
    return lax.all_to_all(jnp.broadcast_to(x[None], (length, *x.shape)), axis, 0, 0, tiled=True)


def collect(x, axis, dim):
    return joined_along(from_everyone(x, axis), dim)


def cas_table(frequency, length):
    columns = jnp.arange(length)
    phases = frequency[:, None] * columns[None, :] % length
    angles = phases.astype(jnp.float32) * (2.0 * math.pi / length)
    return (jnp.cos(angles) + jnp.sin(angles)) / math.sqrt(length)


def side_frequency(indices):
    halves = (indices + 1) // 2
    return jnp.where(indices % 2 == 1, halves, -halves)


def kinetic(slot_map, first_stick, stick_count, length, side):
    sticks = first_stick + slot_map % stick_count
    plane_index = slot_map // stick_count
    along_z = jnp.where(plane_index < length // 2, plane_index, plane_index - length)
    along_x = side_frequency(sticks // side)
    along_y = side_frequency(sticks % side)
    squared = along_x * along_x + along_y * along_y + along_z * along_z
    return squared.astype(jnp.float32) * (1.0 / (0.5 * side * side + 0.25 * length * length))


def local(states, slot_map, potential, projectors, species, coupling):
    highest = lax.Precision.HIGHEST
    bands = states.shape[0]
    planes = potential.shape[0]
    length = potential.shape[1]
    side = NSIDE
    stick_count = side * side // lax.axis_size(PW)
    owner = lax.axis_index(PW)
    wide = states.astype(jnp.float32)
    dense = jnp.zeros((bands, length * stick_count), jnp.float32).at[:, slot_map].set(wide)
    dense = dense.reshape(bands, length, stick_count)
    z_table = cas_table(jnp.arange(length), length)
    side_table = cas_table(side_frequency(jnp.arange(side)), length)
    columns = jnp.einsum("bks,kz->bzs", dense, z_table, precision=highest)
    piece = lax.all_to_all(columns, PW, split_axis=1, concat_axis=2, tiled=True)
    count = piece.shape[0]
    grid = piece.reshape(count, planes, side, side)
    half = jnp.einsum("bzjk,jx->bzxk", grid, side_table, precision=highest)
    real_space = jnp.einsum("bzxk,ky->bzxy", half, side_table, precision=highest)
    weighted = real_space * potential[None]
    back_half = jnp.einsum("bzxy,ky->bzxk", weighted, side_table, precision=highest)
    back_grid = jnp.einsum("bzxk,jx->bzjk", back_half, side_table, precision=highest)
    returned = exchange_by_chip(
        back_grid.reshape(count, planes, side * side),
        (("pw_0", "pw_1", "pw_2"), "pw_3"),
        (1, 0),
        2,
        1,
    )
    spectral = jnp.einsum("bzs,kz->bks", returned, z_table, precision=highest)
    local_term = spectral.reshape(bands, length * stick_count)[:, slot_map]
    energies = kinetic(slot_map, owner * stick_count, stick_count, length, side)
    partial_value = lax.dot_general(
        projectors, states, (((1,), (1,)), ((), ())), preferred_element_type=jnp.float32
    )
    correlations = one_axis_at_a_time(partial_value, PW) / math.sqrt(NG)
    atoms = species.shape[0]
    per_atom = coupling.shape[1]
    kinds = coupling.shape[0]
    symmetric = 0.5 * (coupling + jnp.swapaxes(coupling, 1, 2))
    onehot = (species[:, None] == jnp.arange(kinds)[None, :]).astype(jnp.float32)
    chosen = jnp.einsum("as,smn->amn", onehot, symmetric, precision=highest)
    weights = jnp.einsum(
        "amn,anb->amb", chosen, correlations.reshape(atoms, per_atom, bands), precision=highest
    )
    weights = weights.reshape(atoms * per_atom, bands).astype(jnp.bfloat16)
    nonlocal_term = lax.dot_general(
        weights, projectors, (((0,), (0,)), ((), ())), preferred_element_type=jnp.float32
    ) / math.sqrt(atoms * per_atom)
    applied = energies[None, :] * wide + local_term + nonlocal_term
    block = lax.dot_general(
        wide,
        collect(applied.astype(jnp.bfloat16), "band", 0).astype(applied.dtype),
        (((1,), (1,)), ((), ())),
        precision=highest,
        preferred_element_type=jnp.float32,
    )
    subspace = one_axis_at_a_time(block, PW) / float(NG)
    return (applied, subspace)


def solution(mesh):
    split = Mesh(
        mesh.devices.reshape(mesh.shape["band"], 2, 4, 8, 2),
        ("band", "pw_0", "pw_1", "pw_2", "pw_3"),
    )
    return jax.shard_map(
        local,
        mesh=split,
        in_specs=(P("band", PW), P(PW), P(PW, None, None), P(None, PW), P(), P()),
        out_specs=(P("band", PW), P("band", None)),
        check_vma=False,
    )
```

profile of v0, /device:TPU:1, one launch (start us, length us, event | category | flops | bytes accessed | tf_op | source)
XLA Modules:
  0.0 242.8 jit_solution(18308723643729804434)
XLA Ops:
  0.6 1.4 compare_select_fusion
  2.0 1.5 convert_bitcast_fusion
  3.5 1.9 copy.25
  5.4 0.0 copy-start.5
  5.4 28.5 %scatter_custom_fusion = f32[3,9216]{0,1:T(8,128)} fusion(s32[6912]{0:T(1024)} %compare_select_fusion, f32[6912,3]{1,0:T(8,128)S(1)} %copy.25, f32[]{:T(128)} %constant.150.clone.1), kind=kCustom, calls=%fused_computation.4 | custom fusion | bytes 111104 | tf_op jit(solution)/shard_map/scatter | solution.py:85
  33.9 0.0 copy-start.6
  33.9 3.4 %copy.26 = f32[3,128,72]{1,2,0:T(8,128)S(1)} copy(f32[3,128,72]{0,2,1:T(8,128)} %bitcast.80) | data formatting | bytes 221184 | tf_op jit(solution)/shard_map/reshape | solution.py:86
  37.3 0.6 fusion.22
  37.9 0.1 copy.27
  38.1 0.9 reshape.120
  39.0 25.1 %all-to-all-start = ((f32[128,1,216]{2,1,0:T(1,128)}), f32[128,1,216]{2,1,0:T(1,128)S(1)}, u32[]{:S(2)}, u32[]{:S(2)}) async-start(f32[128,1,216]{2,1,0:T(1,128)} %reshape.120), calls=%async_computation | async-start | bytes 262144 | tf_op jit(solution)/shard_map/all_to_all | solution.py:90
  64.1 0.0 copy-done.5
  64.1 0.1 copy.37
  64.1 0.0 copy-done.6
  64.1 0.2 fusion.45
  64.4 0.1 copy.39
  64.5 0.0 copy-done
  64.5 0.0 copy-start.4
  64.5 0.0 copy-start.3
  64.6 5.0 %fusion.82 = f32[512,3]{0,1:T(4,128)S(1)} fusion(bf16[512,6912]{1,0:T(8,128)(2,1)} %param.9, bf16[3,6912]{1,0:T(4,128)(2,1)S(1)} %copy-done), kind=kOutput, calls=%fused_computation.138 | convolution fusion | flops 21233664 | bytes 7125504 | tf_op jit(solution)/shard_map/dot_general | solution.py:108
  69.5 10.7 %psum.56 = f32[512,3]{0,1:T(4,128)S(1)} all-reduce(f32[512,3]{0,1:T(4,128)S(1)} %fusion.82), channel_id=1, replica_groups=mesh['band'=6,'pw_0'=2,'pw_1'=4,'pw_2'=8,'pw_3'=2] {'pw_0'}, use_global_device_ids=true, to_apply=%region_1.2 | all-reduce | flops 1536 | bytes 12288 | tf_op jit(solution)/shard_map/psum | solution.py:42
  80.2 8.8 %psum.57 = f32[512,3]{0,1:T(4,128)S(1)} all-reduce(f32[512,3]{0,1:T(4,128)S(1)} %psum.56), channel_id=1, replica_groups=mesh['band'=6,'pw_0'=2,'pw_1'=4,'pw_2'=8,'pw_3'=2] {'pw_1'}, use_global_device_ids=true, to_apply=%region_2.3 | all-reduce | flops 1536 | bytes 12288 | tf_op jit(solution)/shard_map/psum | solution.py:42
  89.0 13.4 %psum.58 = f32[512,3]{0,1:T(4,128)S(1)} all-reduce(f32[512,3]{0,1:T(4,128)S(1)} %psum.57), channel_id=1, replica_groups=mesh['band'=6,'pw_0'=2,'pw_1'=4,'pw_2'=8,'pw_3'=2] {'pw_2'}, use_global_device_ids=true, to_apply=%region_3.4 | all-reduce | flops 1536 | bytes 12288 | tf_op jit(solution)/shard_map/psum | solution.py:42
  102.5 9.0 %psum.59 = f32[512,3]{0,1:T(4,128)S(1)} all-reduce(f32[512,3]{0,1:T(4,128)S(1)} %psum.58), channel_id=1, replica_groups=mesh['band'=6,'pw_0'=2,'pw_1'=4,'pw_2'=8,'pw_3'=2] {'pw_3'}, use_global_device_ids=true, to_apply=%region_4.5 | all-reduce | flops 1536 | bytes 12288 | tf_op jit(solution)/shard_map/psum | solution.py:42
  111.5 0.1 reshape.90
  111.6 0.6 convolution_convert_fusion
  112.2 0.1 convert_element_type.36
  112.4 0.0 all-to-all-done
  112.4 0.5 broadcast.143
  112.9 1.0 reduce
  113.9 0.2 reshape.121
  114.1 0.1 reshape.84
  114.2 0.1 copy.29
  114.3 0.6 fusion.43
  114.9 0.0 copy-done.4
  114.9 0.6 convolution_multiply_fusion.1
  115.5 0.7 fusion.15
  116.2 0.6 convolution_bitcast_fusion
  116.8 0.1 reshape_reshape.3
  117.0 3.9 %all_to_all.24 = f32[64,2,3,1,72]{4,0,2,3,1:T(8,128)S(1)} all-to-all(f32[64,2,3,1,72]{4,0,2,3,1:T(8,128)S(1)} %copy.30), channel_id=1, replica_groups=mesh['band'=6,'pw_0'=2,'pw_1'=4,'pw_2'=8,'pw_3'=2] {'pw_3'}, dimensions={1} | all-to-all | bytes 221184 | tf_op jit(solution)/shard_map/all_to_all | solution.py:31
  120.9 0.8 copy.31
  121.7 13.3 %all-to-all-start.2 = ((f32[64,2,3,1,72]{4,1,2,3,0:T(2,128)}), f32[64,2,3,1,72]{4,1,2,3,0:T(2,128)S(1)}, u32[]{:S(2)}, u32[]{:S(2)}) async-start(f32[64,2,3,1,72]{4,1,2,3,0:T(2,128)} %copy.31), calls=%async_computation.2 | async-start | bytes 393216 | tf_op jit(solution)/shard_map/all_to_all | solution.py:31
  135.0 0.0 copy-done.3
  135.0 0.6 pad_clamp_fusion
  135.6 0.0 copy-done.2
  135.6 0.7 fusion.31
  136.4 15.1 %all-to-all-done.2 = f32[64,2,3,1,72]{4,1,2,3,0:T(2,128)S(1)} async-done(((f32[64,2,3,1,72]{4,1,2,3,0:T(2,128)}), f32[64,2,3,1,72]{4,1,2,3,0:T(2,128)S(1)}, u32[]{:S(2)}, u32[]{:S(2)}) %all-to-all-start.2) | async-done | bytes 110624 | tf_op jit(solution)/shard_map/all_to_all | solution.py:31
  151.5 0.1 copy.32
  151.5 0.1 copy.33
  151.7 0.6 fusion.21
  152.3 3.1 %copy.42 = f32[3,128,72]{0,2,1:T(8,128)} copy(f32[3,128,72]{1,2,0:T(8,128)S(1)} %bitcast.91) | data formatting | bytes 221184 | tf_op jit(solution)/shard_map/reshape | solution.py:106
  155.3 15.1 %gather_fusion = f32[6912,3]{1,0:T(8,128)S(1)} fusion(f32[3,9216]{0,1:T(8,128)} %bitcast.81, s32[7168]{0:T(1024)} %pad_clamp_fusion), kind=kCustom, calls=%fused_computation | custom fusion | bytes 193536 | tf_op jit(solution)/shard_map/gather | solution.py:106
  170.5 2.0 copy.36
  172.4 4.8 %fusion.81 = (bf16[3,6912]{1,0:T(4,128)(2,1)S(1)}, f32[3,6912]{1,0:T(4,128)}) fusion(bf16[512,3]{0,1:T(4,128)(2,1)S(1)} %convert_element_type.36, bf16[512,6912]{1,0:T(8,128)(2,1)} %param.9, f32[6912,3]{0,1:T(4,128)} %copy.36, bf16[3,6912]{1,0:T(4,128)(2,1)} %param.6, f32[6912]{0:T(1024)} %fusion.31), kind=kOutput, calls=%fused_computation.137 | convolution fusion | flops 21358080 | bytes 7357440 | tf_op jit(solution)/shard_map/dot_general | solution.py:122
  177.2 0.1 broadcast_in_dim.8
  177.3 25.5 %all_to_all.25 = bf16[6,3,6912]{2,1,0:T(4,128)(2,1)S(1)} all-to-all(bf16[6,3,6912]{2,1,0:T(4,128)(2,1)S(1)} %broadcast_in_dim.8), channel_id=1, replica_groups=mesh['band'=6,'pw_0'=2,'pw_1'=4,'pw_2'=8,'pw_3'=2] {'band'}, dimensions={0} | all-to-all | bytes 497664 | tf_op jit(solution)/shard_map/all_to_all | solution.py:47
  202.8 0.2 reshape.91
  203.1 0.0 copy-done.1
  203.1 0.2 convolution_bitcast_fusion.1
  203.3 10.1 %psum.60 = f32[3,18]{1,0:T(4,128)S(1)} all-reduce(f32[3,18]{1,0:T(4,128)S(1)} %convolution_bitcast_fusion.1), channel_id=1, replica_groups=mesh['band'=6,'pw_0'=2,'pw_1'=4,'pw_2'=8,'pw_3'=2] {'pw_0'}, use_global_device_ids=true, to_apply=%region_5.6 | all-reduce | flops 54 | bytes 432 | tf_op jit(solution)/shard_map/psum | solution.py:42
  213.4 7.5 %psum.61 = f32[3,18]{1,0:T(4,128)S(1)} all-reduce(f32[3,18]{1,0:T(4,128)S(1)} %psum.60), channel_id=1, replica_groups=mesh['band'=6,'pw_0'=2,'pw_1'=4,'pw_2'=8,'pw_3'=2] {'pw_1'}, use_global_device_ids=true, to_apply=%region_6.7 | all-reduce | flops 54 | bytes 432 | tf_op jit(solution)/shard_map/psum | solution.py:42
  220.9 10.8 %psum.62 = f32[3,18]{1,0:T(4,128)S(1)} all-reduce(f32[3,18]{1,0:T(4,128)S(1)} %psum.61), channel_id=1, replica_groups=mesh['band'=6,'pw_0'=2,'pw_1'=4,'pw_2'=8,'pw_3'=2] {'pw_2'}, use_global_device_ids=true, to_apply=%region_7.8 | all-reduce | flops 54 | bytes 432 | tf_op jit(solution)/shard_map/psum | solution.py:42
  231.7 10.5 %psum.63 = f32[3,18]{1,0:T(4,128)S(1)} all-reduce(f32[3,18]{1,0:T(4,128)S(1)} %psum.62), channel_id=1, replica_groups=mesh['band'=6,'pw_0'=2,'pw_1'=4,'pw_2'=8,'pw_3'=2] {'pw_3'}, use_global_device_ids=true, to_apply=%region_8.9 | all-reduce | flops 54 | bytes 432 | tf_op jit(solution)/shard_map/psum | solution.py:42
  242.2 0.6 broadcast_multiply_fusion.1
  (9 shorter events, 0.1 us)
Async XLA Ops:
  5.4 58.7 %copy-start.5 = (f32[4,8,8]{2,1,0:T(8,128)S(1)}, f32[4,8,8]{2,1,0:T(8,128)}, u32[]{:S(2)}) copy-start(f32[4,8,8]{2,1,0:T(8,128)} %param.11) | copy-start | bytes 3076
  33.9 30.2 %copy-start.6 = (s32[64]{0:T(128)S(1)}, s32[64]{0:T(128)}, u32[]{:S(2)}) copy-start(s32[64]{0:T(128)} %param.10) | copy-start | bytes 772
  33.9 30.6 %copy-start = (bf16[3,6912]{1,0:T(4,128)(2,1)S(1)}, bf16[3,6912]{1,0:T(4,128)(2,1)}, u32[]{:S(2)}) copy-start(bf16[3,6912]{1,0:T(4,128)(2,1)} %param.6) | copy-start | bytes 124420
  39.0 73.4 %all-to-all-start = ((f32[128,1,216]{2,1,0:T(1,128)}), f32[128,1,216]{2,1,0:T(1,128)S(1)}, u32[]{:S(2)}, u32[]{:S(2)}) async-start(f32[128,1,216]{2,1,0:T(1,128)} %reshape.120), calls=%async_computation | async-start | bytes 262144 | tf_op jit(solution)/shard_map/all_to_all | solution.py:90
  64.5 50.3 %copy-start.4 = (f32[1,128,128]{2,1,0:T(8,128)S(1)}, f32[1,128,128]{2,1,0:T(8,128)}, u32[]{:S(2)}) copy-start(f32[1,128,128]{2,1,0:T(8,128)} %param.8) | copy-start | bytes 196612
  64.5 70.5 %copy-start.3 = (s32[6912]{0:T(1024)S(1)}, s32[6912]{0:T(1024)}, u32[]{:S(2)}) copy-start(s32[6912]{0:T(1024)} %compare_select_fusion) | copy-start | bytes 82948
  69.5 66.1 %copy-start.2 = (s32[6912]{0:T(1024)S(1)}, s32[6912]{0:T(1024)}, u32[]{:S(2)}) copy-start(s32[6912]{0:T(1024)} %param.7) | copy-start | bytes 82948
  121.7 29.8 %all-to-all-start.2 = ((f32[64,2,3,1,72]{4,1,2,3,0:T(2,128)}), f32[64,2,3,1,72]{4,1,2,3,0:T(2,128)S(1)}, u32[]{:S(2)}, u32[]{:S(2)}) async-start(f32[64,2,3,1,72]{4,1,2,3,0:T(2,128)} %copy.31), calls=%async_computation.2 | async-start | bytes 393216 | tf_op jit(solution)/shard_map/all_to_all | solution.py:31
  172.4 30.6 %copy-start.1 = (bf16[3,6912]{1,0:T(4,128)(2,1)S(1)}, bf16[3,6912]{1,0:T(4,128)(2,1)}, u32[]{:S(2)}) copy-start(bf16[3,6912]{1,0:T(4,128)(2,1)} %param.6) | copy-start | bytes 124420
where the time goes:
time: 244 us; the launch traced here: 243 us
  blocking collectives  110 us (45%)
  local copies, waits for them, and re-layouts  57.9 us (24%)
  starting transfers between devices  38.4 us (16%)
  waiting for transfers between devices  15.1 us (6%)
  matrix products  14.4 us (6%)
  other arithmetic  5.73 us (2%)
    psum x8, blocking collectives, one_axis_at_a_time(): return functools.reduce(lax.psum, axes, x)  80.9 us
    scatter x1, local copies, waits for them, and re-layouts, local(): jnp.zeros((bands, length * stick_count), jnp.float32).at[:, slot_map]  28.5 us
    all_to_all x1, blocking collectives, from_everyone(): lax.all_to_all(jnp.broadcast_to(x[None], (length, *x.shape)), axis, 0, 0,...  25.5 us
    all_to_all x1, starting transfers between devices, local(): piece = lax.all_to_all(columns, PW, split_axis=1, concat_axis=2, tiled=True)  25.1 us
    gather x2, local copies, waits for them, and re-layouts, local(): local_term = spectral.reshape(bands, length * stick_count)[:, slot_map]  17.1 us
    all_to_all x1, waiting for transfers between devices, moved_by_axis(): whole = lax.all_to_all(whole, axes[k], k, k, tiled=True)  15.1 us
    all_to_all x1, starting transfers between devices, moved_by_axis(): whole = lax.all_to_all(whole, axes[k], k, k, tiled=True)  13.3 us
    dot_general x1, matrix products, local(): lax.dot_general(projectors, states, (((1,), (1,)), ((), ())), preferred_e...  4.95 us
  transfers between devices with their start and end apart: 2, of which 1 were waited for; matrix products, arithmetic and copies ran while one was open for 3% of the time, Pallas kernels for 0%

commit v1 on v0

--- a/solution.py
+++ b/solution.py
@@ -95,12 +95,8 @@
     weighted = real_space * potential[None]
     back_half = jnp.einsum("bzxy,ky->bzxk", weighted, side_table, precision=highest)
     back_grid = jnp.einsum("bzxk,jx->bzjk", back_half, side_table, precision=highest)
-    returned = exchange_by_chip(
-        back_grid.reshape(count, planes, side * side),
-        (("pw_0", "pw_1", "pw_2"), "pw_3"),
-        (1, 0),
-        2,
-        1,
+    returned = lax.all_to_all(
+        back_grid.reshape(count, planes, side * side), PW, split_axis=2, concat_axis=1, tiled=True
     )
     spectral = jnp.einsum("bzs,kz->bks", returned, z_table, precision=highest)
     local_term = spectral.reshape(bands, length * stick_count)[:, slot_map]
@@ -108,7 +104,7 @@
     partial_value = lax.dot_general(
         projectors, states, (((1,), (1,)), ((), ())), preferred_element_type=jnp.float32
     )
-    correlations = one_axis_at_a_time(partial_value, PW) / math.sqrt(NG)
+    correlations = lax.psum(partial_value, PW) / math.sqrt(NG)
     atoms = species.shape[0]
     per_atom = coupling.shape[1]
     kinds = coupling.shape[0]
@@ -123,14 +119,21 @@
         weights, projectors, (((0,), (0,)), ((), ())), preferred_element_type=jnp.float32
     ) / math.sqrt(atoms * per_atom)
     applied = energies[None, :] * wide + local_term + nonlocal_term
+    group = lax.axis_index("band")
+    every_state = lax.all_gather(states, "band", axis=0, tiled=True).astype(jnp.float32)
     block = lax.dot_general(
-        wide,
-        collect(applied.astype(jnp.bfloat16), "band", 0).astype(applied.dtype),
+        every_state,
+        applied,
         (((1,), (1,)), ((), ())),
         precision=highest,
         preferred_element_type=jnp.float32,
     )
-    subspace = one_axis_at_a_time(block, PW) / float(NG)
+    total = every_state.shape[0]
+    placed = lax.dynamic_update_slice(
+        jnp.zeros((total, total), jnp.float32), block, (0, group * bands)
+    )
+    whole = lax.psum(placed, ("band",) + PW) / float(NG)
+    subspace = lax.dynamic_slice(whole, (group * bands, 0), (bands, total))
     return (applied, subspace)
 
 

time: 244 us -> 818 us (3.35)
  blocking collectives: 110 us -> 612 us
  other arithmetic: 5.73 us -> 49.6 us
  local copies, waits for them, and re-layouts: 57.9 us -> 77 us
  starting transfers between devices: 38.4 us -> 47 us
    psum x8 -> x2, blocking collectives: 80.9 us -> 586 us  [the longest x1 482 us: local(): correlations = lax.psum(partial_value, PW) / math.sqrt(NG)]
    unnamed x0 -> x1, other arithmetic: none -> 42.9 us
    all_to_all x2 -> x0, blocking collectives: 29.4 us -> none  [the longest x1 25.5 us: from_everyone(): lax.all_to_all(jnp.broadcast_to(x[None], (length, *x.shape)), axis, 0, 0,...]
    all_gather x0 -> x1, blocking collectives: none -> 25.8 us  [local(): lax.all_gather(states, 'band', axis=0, tiled=True).astype(jnp.float32)]
    unnamed x17 -> x22, local copies, waits for them, and re-layouts: 1.15 us -> 15.1 us
    all_to_all x1, starting transfers between devices: 13.3 us -> 22 us  [local(): lax.all_to_all(back_grid.reshape(count, planes, side * side), PW, split_a...]
  transfers between devices with their start and end apart: 2 -> 2, of which waited for: 1 -> 1; matrix products, arithmetic and copies ran while one was open for 3% -> 1% of each run, Pallas kernels for 0% -> 0%
where the time goes in v1:
time: 818 us; the launch traced here: 817 us
  blocking collectives  612 us (75%)
  local copies, waits for them, and re-layouts  77 us (9%)
  other arithmetic  49.6 us (6%)
  starting transfers between devices  47 us (6%)
  waiting for transfers between devices  16 us (2%)
  matrix products  13.9 us (2%)
    psum x1, blocking collectives, local(): correlations = lax.psum(partial_value, PW) / math.sqrt(NG)  482 us
    psum x1, blocking collectives, local(): whole = lax.psum(placed, ('band',) + PW) / float(NG)  104 us
    unnamed x1, other arithmetic  42.9 us
    scatter x1, local copies, waits for them, and re-layouts, local(): jnp.zeros((bands, length * stick_count), jnp.float32).at[:, slot_map]  28.5 us
    all_gather x1, blocking collectives, local(): lax.all_gather(states, 'band', axis=0, tiled=True).astype(jnp.float32)  25.8 us
    all_to_all x1, starting transfers between devices, local(): piece = lax.all_to_all(columns, PW, split_axis=1, concat_axis=2, tiled=True)  25.1 us
    all_to_all x1, starting transfers between devices, local(): lax.all_to_all(back_grid.reshape(count, planes, side * side), PW, split_a...  22 us
    gather x2, local copies, waits for them, and re-layouts, local(): local_term = spectral.reshape(bands, length * stick_count)[:, slot_map]  17.1 us
  transfers between devices with their start and end apart: 2, of which 1 were waited for; matrix products, arithmetic and copies ran while one was open for 1% of the time, Pallas kernels for 0%

profile of v1, /device:TPU:1, one launch (start us, length us, event | category | flops | bytes accessed | tf_op | source)
XLA Modules:
  0.0 816.7 jit_solution(2165809134190573856)
XLA Ops:
  0.6 1.4 compare_select_fusion
  2.0 1.5 convert_bitcast_fusion
  3.5 1.9 copy.43
  5.4 0.0 copy-start.6
  5.4 28.5 %scatter_custom_fusion = f32[3,9216]{0,1:T(8,128)} fusion(s32[6912]{0:T(1024)} %compare_select_fusion, f32[6912,3]{1,0:T(8,128)S(1)} %copy.43, f32[]{:T(128)} %constant.157.clone.1), kind=kCustom, calls=%fused_computation.4 | custom fusion | bytes 111104 | tf_op jit(solution)/shard_map/scatter | solution.py:85
  33.9 0.0 copy-start.7
  34.0 0.0 copy-start.1
  34.0 3.4 copy.44
  37.3 0.6 fusion.22
  37.9 0.1 copy.45
  38.1 0.9 reshape.112
  39.0 25.1 %all-to-all-start = ((f32[128,1,216]{2,1,0:T(1,128)}), f32[128,1,216]{2,1,0:T(1,128)S(1)}, u32[]{:S(2)}, u32[]{:S(2)}) async-start(f32[128,1,216]{2,1,0:T(1,128)} %reshape.112), calls=%async_computation | async-start | bytes 262144 | tf_op jit(solution)/shard_map/all_to_all | solution.py:90
  64.1 0.0 copy-done.6
  64.1 0.1 copy.54
  64.1 0.0 copy-done.7
  64.1 0.2 fusion.45
  64.4 0.1 copy.56
  64.5 0.0 copy-done.1
  64.5 0.0 copy-start.5
  64.5 5.0 fusion.81
  69.5 482.1 %psum.14 = f32[512,3]{0,1:T(4,128)S(1)} all-reduce(f32[512,3]{0,1:T(4,128)S(1)} %fusion.81), channel_id=1, replica_groups=mesh['band'=6,'pw_0'=2,'pw_1'=4,'pw_2'=8,'pw_3'=2] {'pw_0','pw_1','pw_2'..., use_global_device_ids=true, to_apply=%region_1.2 | all-reduce | flops 1536 | bytes 12288 | tf_op jit(solution)/shard_map/psum | solution.py:107
  551.6 0.1 reshape.81
  551.7 0.6 convolution_convert_fusion
  552.3 0.1 convert_element_type.33
  552.4 25.8 %all-gather = bf16[6,3,6912]{2,1,0:T(4,128)(2,1)S(1)} all-gather(bf16[1,3,6912]{2,1,0:T(4,128)(2,1)S(1)} %bitcast.79), channel_id=1, replica_groups=mesh['band'=6,'pw_0'=2,'pw_1'=4,'pw_2'=8,'pw_3'=2] {'band'}, dimensions={0}, use_global_device_ids=true | all-gather | bytes 290304 | tf_op jit(solution)/shard_map/all_gather | solution.py:123
  578.3 0.9 reshape.101
  579.2 0.0 all-to-all-done
  579.2 0.5 broadcast.142
  579.7 1.0 reduce
  580.7 0.2 reshape.113
  580.9 0.1 reshape.77
  581.0 0.1 copy.47
  581.1 0.6 fusion.43
  581.7 0.0 copy-done.5
  581.7 0.6 convolution_multiply_fusion.1
  582.4 0.7 fusion.15
  583.0 0.6 convolution_bitcast_fusion
  583.7 3.0 copy.60
  586.6 42.9 %reduce.1 = f32[9216,3]{1,0:T(8,128)} reduce(f32[9216,1,3]{2,1,0:T(1,128)} %bitcast.74, f32[]{:T(128)} %broadcast.142), dimensions={1}, to_apply=%bitcast.58.reduce_sub_computation | reduce | bytes 221188
  629.5 0.0 copy-start.4
  629.5 0.0 copy-start.3
  629.5 5.0 reshape.114
  634.5 22.0 %all-to-all-start.1 = ((f32[128,1,216]{2,1,0:T(1,128)}), f32[128,1,216]{2,1,0:T(1,128)S(1)}, u32[]{:S(2)}, u32[]{:S(2)}) async-start(f32[128,1,216]{2,1,0:T(1,128)} %reshape.114), calls=%async_computation.1 | async-start | bytes 262144 | tf_op jit(solution)/shard_map/all_to_all | solution.py:98
  656.5 0.0 copy-done.4
  656.5 0.6 pad_clamp_fusion
  657.1 0.0 copy-done.3
  657.1 0.7 fusion.31
  657.8 16.0 %all-to-all-done.1 = f32[128,1,216]{2,1,0:T(1,128)S(1)} async-done(((f32[128,1,216]{2,1,0:T(1,128)}), f32[128,1,216]{2,1,0:T(1,128)S(1)}, u32[]{:S(2)}, u32[]{:S(2)}) %all-to-all-start.1) | async-done | bytes 110624 | tf_op jit(solution)/shard_map/all_to_all | solution.py:98
  673.8 1.0 reduce.2
  674.8 8.0 reshape.115
  682.8 3.3 copy.50
  686.2 0.6 fusion.21
  686.8 3.1 copy.63
  689.9 15.1 %gather_fusion = f32[6912,3]{1,0:T(8,128)S(1)} fusion(f32[3,9216]{0,1:T(8,128)} %bitcast.76, s32[7168]{0:T(1024)} %pad_clamp_fusion), kind=kCustom, calls=%fused_computation | custom fusion | bytes 193536 | tf_op jit(solution)/shard_map/gather | solution.py:102
  705.0 2.0 copy.53
  707.0 4.1 fusion
  711.1 0.0 copy-done
  711.1 0.0 copy-start.2
  711.1 0.4 convolution_bitcast_fusion.1
  711.5 0.1 copy.59
  711.6 0.2 dynamic_update_slice.3
  711.8 104.3 %psum.15 = f32[18,18]{1,0:T(8,128)S(1)} all-reduce(f32[18,18]{1,0:T(8,128)S(1)} %dynamic_update_slice.3), channel_id=1, replica_groups=mesh['band'=6,'pw_0'=2,'pw_1'=4,'pw_2'=8,'pw_3'=2] {'band','pw_0','pw_1'..., use_global_device_ids=true, to_apply=%region_2.3 | all-reduce | flops 324 | bytes 2592 | tf_op jit(solution)/shard_map/psum | solution.py:135
  816.1 0.6 dynamic-slice_multiply_fusion
  816.7 0.0 copy-done.2
  (7 shorter events, 0.0 us)
Async XLA Ops:
  5.4 58.6 %copy-start.6 = (f32[4,8,8]{2,1,0:T(8,128)S(1)}, f32[4,8,8]{2,1,0:T(8,128)}, u32[]{:S(2)}) copy-start(f32[4,8,8]{2,1,0:T(8,128)} %param.11) | copy-start | bytes 3076
  33.9 30.2 %copy-start.7 = (s32[64]{0:T(128)S(1)}, s32[64]{0:T(128)}, u32[]{:S(2)}) copy-start(s32[64]{0:T(128)} %param.10) | copy-start | bytes 772
  34.0 30.6 %copy-start.1 = (bf16[3,6912]{1,0:T(4,128)(2,1)S(1)}, bf16[3,6912]{1,0:T(4,128)(2,1)}, u32[]{:S(2)}) copy-start(bf16[3,6912]{1,0:T(4,128)(2,1)} %param.6) | copy-start | bytes 124420
  39.0 540.2 %all-to-all-start = ((f32[128,1,216]{2,1,0:T(1,128)}), f32[128,1,216]{2,1,0:T(1,128)S(1)}, u32[]{:S(2)}, u32[]{:S(2)}) async-start(f32[128,1,216]{2,1,0:T(1,128)} %reshape.112), calls=%async_computation | async-start | bytes 262144 | tf_op jit(solution)/shard_map/all_to_all | solution.py:90
  64.5 517.2 %copy-start.5 = (f32[1,128,128]{2,1,0:T(8,128)S(1)}, f32[1,128,128]{2,1,0:T(8,128)}, u32[]{:S(2)}) copy-start(f32[1,128,128]{2,1,0:T(8,128)} %param.8) | copy-start | bytes 196612
  629.5 26.9 %copy-start.4 = (s32[6912]{0:T(1024)S(1)}, s32[6912]{0:T(1024)}, u32[]{:S(2)}) copy-start(s32[6912]{0:T(1024)} %compare_select_fusion) | copy-start | bytes 82948
  629.5 27.6 %copy-start.3 = (s32[6912]{0:T(1024)S(1)}, s32[6912]{0:T(1024)}, u32[]{:S(2)}) copy-start(s32[6912]{0:T(1024)} %param.7) | copy-start | bytes 82948
  634.5 39.3 %all-to-all-start.1 = ((f32[128,1,216]{2,1,0:T(1,128)}), f32[128,1,216]{2,1,0:T(1,128)S(1)}, u32[]{:S(2)}, u32[]{:S(2)}) async-start(f32[128,1,216]{2,1,0:T(1,128)} %reshape.114), calls=%async_computation.1 | async-start | bytes 262144 | tf_op jit(solution)/shard_map/all_to_all | solution.py:98
  707.0 4.1 copy-start
  711.1 105.6 %copy-start.2 = (f32[3,6912]{1,0:T(4,128)}, f32[3,6912]{1,0:T(4,128)S(1)}, u32[]{:S(2)}) copy-start(f32[3,6912]{1,0:T(4,128)S(1)} %fusion) | copy-start | bytes 248836

commit v2 on v0

v2 whole, which is shorter than its diff:
```python
import math

import jax
import jax.numpy as jnp
from jax import lax
from jax.sharding import Mesh
from jax.sharding import PartitionSpec as P

NSIDE = 96
NG = 884736
PW = ("pw_0", "pw_1", "pw_2", "pw_3")


def one_axis_at_a_time(x, axes):
    for a in axes:
        x = lax.psum(x, a)
    return x


def cas_table(frequency, length):
    columns = jnp.arange(length)
    phases = frequency[:, None] * columns[None, :] % length
    angles = phases.astype(jnp.float32) * (2.0 * math.pi / length)
    return (jnp.cos(angles) + jnp.sin(angles)) / math.sqrt(length)


def side_frequency(indices):
    halves = (indices + 1) // 2
    return jnp.where(indices % 2 == 1, halves, -halves)


def kinetic(slot_map, first_stick, stick_count, length, side):
    sticks = first_stick + slot_map % stick_count
    plane_index = slot_map // stick_count
    along_z = jnp.where(plane_index < length // 2, plane_index, plane_index - length)
    along_x = side_frequency(sticks // side)
    along_y = side_frequency(sticks % side)
    squared = along_x * along_x + along_y * along_y + along_z * along_z
    return squared.astype(jnp.float32) * (1.0 / (0.5 * side * side + 0.25 * length * length))


def gathered_bands(states, axis):
    n = lax.axis_size(axis)
    blocks = [states]
    for k in range(1, n):
        blocks.append(lax.ppermute(states, axis, [(i, (i + k) % n) for i in range(n)]))
    return jnp.concatenate(blocks, axis=0)


def local(states, slot_map, potential, projectors, species, coupling):
    highest = lax.Precision.HIGHEST
    bands = states.shape[0]
    planes = potential.shape[0]
    length = potential.shape[1]
    side = NSIDE
    npw = lax.axis_size(PW)
    stick_count = side * side // npw
    owner = lax.axis_index(PW)
    group = lax.axis_index("band")
    ngroup = lax.axis_size("band")
    every = gathered_bands(states, "band")
    total = every.shape[0]
    wide = states.astype(jnp.float32)
    dense = jnp.zeros((bands, length * stick_count), jnp.float32).at[:, slot_map].set(wide)
    dense = dense.reshape(bands, length, stick_count)
    z_table = cas_table(jnp.arange(length), length)
    side_table = cas_table(side_frequency(jnp.arange(side)), length)
    columns = jnp.einsum("bks,kz->zbs", dense, z_table, precision=highest)
    sent = columns.reshape(npw, planes * bands * stick_count)
    piece = lax.all_to_all(sent, PW, 0, 0, tiled=True)
    piece = piece.reshape(npw, planes, bands, stick_count)
    grid = jnp.transpose(piece, (2, 1, 0, 3)).reshape(bands, planes, side, side)
    half = jnp.einsum("bzjk,jx->bzxk", grid, side_table, precision=highest)
    real_space = jnp.einsum("bzxk,ky->bzxy", half, side_table, precision=highest)
    weighted = real_space * potential[None]
    back_half = jnp.einsum("bzxy,ky->bzxk", weighted, side_table, precision=highest)
    back_grid = jnp.einsum("bzxk,jx->bzjk", back_half, side_table, precision=highest)
    back = back_grid.reshape(bands, planes, npw, stick_count)
    back = jnp.transpose(back, (2, 1, 0, 3)).reshape(npw, planes * bands * stick_count)
    returned = lax.all_to_all(back, PW, 0, 0, tiled=True)
    returned = returned.reshape(npw * planes, bands, stick_count)
    spectral = jnp.einsum("zbs,kz->bks", returned, z_table, precision=highest)
    local_term = spectral.reshape(bands, length * stick_count)[:, slot_map]
    energies = kinetic(slot_map, owner * stick_count, stick_count, length, side)
    diagonal = energies[None, :] * wide + local_term
    partial_corr = lax.dot_general(
        projectors, every, (((1,), (1,)), ((), ())), preferred_element_type=jnp.float32
    )
    partial_gram = lax.dot_general(
        diagonal,
        every.astype(jnp.float32),
        (((1,), (1,)), ((), ())),
        precision=highest,
        preferred_element_type=jnp.float32,
    )
    nproj = partial_corr.shape[0]
    packed = jnp.concatenate([partial_corr.reshape(-1), partial_gram.reshape(-1)])
    reduced = one_axis_at_a_time(packed, PW)
    correlations = reduced[: nproj * total].reshape(nproj, total) / math.sqrt(NG)
    gram = reduced[nproj * total :].reshape(bands, total)
    atoms = species.shape[0]
    per_atom = coupling.shape[1]
    kinds = coupling.shape[0]
    symmetric = 0.5 * (coupling + jnp.swapaxes(coupling, 1, 2))
    onehot = (species[:, None] == jnp.arange(kinds)[None, :]).astype(jnp.float32)
    chosen = jnp.einsum("as,smn->amn", onehot, symmetric, precision=highest)
    weights = jnp.einsum(
        "amn,anb->amb", chosen, correlations.reshape(atoms, per_atom, total), precision=highest
    )
    weights = weights.reshape(atoms * per_atom, total).astype(jnp.bfloat16)
    nonlocal_term = lax.dot_general(
        weights[:, :bands], projectors, (((0,), (0,)), ((), ())), preferred_element_type=jnp.float32
    ) / math.sqrt(atoms * per_atom)
    applied = diagonal + nonlocal_term
    cross = lax.dot_general(
        correlations[:, :bands],
        weights.astype(jnp.float32),
        (((0,), (0,)), ((), ())),
        precision=highest,
        preferred_element_type=jnp.float32,
    ) / (math.sqrt(atoms * per_atom) * math.sqrt(NG))
    rotated = (gram / float(NG) + cross).reshape(bands, ngroup, bands)
    order = (group - jnp.arange(ngroup)) % ngroup
    subspace = jnp.take(rotated, order, axis=1).reshape(bands, total)
    return (applied, subspace)


def solution(mesh):
    split = Mesh(
        mesh.devices.reshape(mesh.shape["band"], 2, 4, 8, 2),
        ("band", "pw_0", "pw_1", "pw_2", "pw_3"),
    )
    return jax.shard_map(
        local,
        mesh=split,
        in_specs=(P("band", PW), P(PW), P(PW, None, None), P(None, PW), P(), P()),
        out_specs=(P("band", PW), P("band", None)),
        check_vma=False,
    )
```

time: 244 us -> 229 us (0.939)
  blocking collectives: 110 us -> 62.2 us
  starting transfers between devices: 38.4 us -> 56.1 us
  local copies, waits for them, and re-layouts: 57.9 us -> 65.1 us
  waiting for transfers between devices: 15.1 us -> 20.5 us
  matrix products: 14.4 us -> 17 us
    all_to_all x2 -> x0, blocking collectives: 29.4 us -> none  [the longest x1 25.5 us: from_everyone(): lax.all_to_all(jnp.broadcast_to(x[None], (length, *x.shape)), axis, 0, 0,...]
    ppermute x0 -> x5, starting transfers between devices: none -> 25.7 us  [gathered_bands(): lax.ppermute(states, axis, [(i, (i + k) % n) for i in range(n)])]
    psum x8 -> x4, blocking collectives: 80.9 us -> 62.2 us  [one_axis_at_a_time(): x = lax.psum(x, a)]
    all_to_all x2, starting transfers between devices: 38.4 us -> 30.4 us  [the longest x1 20.8 us: local(): piece = lax.all_to_all(sent, PW, 0, 0, tiled=True)]
    all_to_all x2, waiting for transfers between devices: 15.1 us -> 20.5 us  [the longest x1 11.3 us: local(): returned = lax.all_to_all(back, PW, 0, 0, tiled=True)]
    concatenate x0 -> x1, local copies, waits for them, and re-layouts: none -> 5.25 us  [gathered_bands(): return jnp.concatenate(blocks, axis=0)]
    dot_general x3 -> x5, matrix products: 9.91 us -> 12.2 us  [the longest x1 4.96 us: local(): lax.dot_general(projectors, every, (((1,), (1,)), ((), ())), preferred_el...]
  transfers between devices with their start and end apart: 2 -> 7, of which waited for: 1 -> 2; matrix products, arithmetic and copies ran while one was open for 3% -> 23% of each run, Pallas kernels for 0% -> 0%
where the time goes in v2:
time: 229 us; the launch traced here: 228 us
  local copies, waits for them, and re-layouts  65.1 us (28%)
  blocking collectives  62.2 us (27%)
  starting transfers between devices  56.1 us (24%)
  waiting for transfers between devices  20.5 us (9%)
  matrix products  17 us (7%)
  other arithmetic  5.65 us (2%)
    psum x4, blocking collectives, one_axis_at_a_time(): x = lax.psum(x, a)  62.2 us
    scatter x1, local copies, waits for them, and re-layouts, local(): jnp.zeros((bands, length * stick_count), jnp.float32).at[:, slot_map]  28.5 us
    ppermute x5, starting transfers between devices, gathered_bands(): lax.ppermute(states, axis, [(i, (i + k) % n) for i in range(n)])  25.7 us
    all_to_all x1, starting transfers between devices, local(): piece = lax.all_to_all(sent, PW, 0, 0, tiled=True)  20.8 us
    gather x2, local copies, waits for them, and re-layouts, local(): local_term = spectral.reshape(bands, length * stick_count)[:, slot_map]  17.1 us
    all_to_all x1, waiting for transfers between devices, local(): returned = lax.all_to_all(back, PW, 0, 0, tiled=True)  11.3 us
    all_to_all x1, starting transfers between devices, local(): returned = lax.all_to_all(back, PW, 0, 0, tiled=True)  9.59 us
    all_to_all x1, waiting for transfers between devices, local(): piece = lax.all_to_all(sent, PW, 0, 0, tiled=True)  9.19 us
  transfers between devices with their start and end apart: 7, of which 2 were waited for; matrix products, arithmetic and copies ran while one was open for 23% of the time, Pallas kernels for 0%

profile of v2, /device:TPU:1, one launch (start us, length us, event | category | flops | bytes accessed | tf_op | source)
XLA Modules:
  0.0 227.5 jit_solution(9273060306293420398)
XLA Ops:
  0.6 4.8 %collective-permute-start = (bf16[3,6912]{1,0:T(4,128)(2,1)}, bf16[3,6912]{1,0:T(4,128)(2,1)}, u32[]{:S(2)}, u32[]{:S(2)}) collective-permute-start(bf16[3,6912]{1,0:T(4,128)(2,1)} %param.6), channel_id=1, source_target_pairs={{0,128},{128,256},{256,384},{384,512},{512,640},{640,0},{1,129},{1... | collective-permute-start | bytes 124424 | tf_op jit(solution)/shard_map/ppermute | solution.py:46
  5.5 5.8 %collective-permute-start.1 = (bf16[3,6912]{1,0:T(4,128)(2,1)}, bf16[3,6912]{1,0:T(4,128)(2,1)}, u32[]{:S(2)}, u32[]{:S(2)}) collective-permute-start(bf16[3,6912]{1,0:T(4,128)(2,1)} %param.6), channel_id=1, source_target_pairs={{0,256},{128,384},{256,512},{384,640},{512,0},{640,128},{1,257},{1... | collective-permute-start | bytes 124424 | tf_op jit(solution)/shard_map/ppermute | solution.py:46
  11.3 6.8 %collective-permute-start.2 = (bf16[3,6912]{1,0:T(4,128)(2,1)}, bf16[3,6912]{1,0:T(4,128)(2,1)}, u32[]{:S(2)}, u32[]{:S(2)}) collective-permute-start(bf16[3,6912]{1,0:T(4,128)(2,1)} %param.6), channel_id=1, source_target_pairs={{0,384},{128,512},{256,640},{384,0},{512,128},{640,256},{1,385},{1... | collective-permute-start | bytes 124424 | tf_op jit(solution)/shard_map/ppermute | solution.py:46
  18.0 4.6 %collective-permute-start.3 = (bf16[3,6912]{1,0:T(4,128)(2,1)}, bf16[3,6912]{1,0:T(4,128)(2,1)}, u32[]{:S(2)}, u32[]{:S(2)}) collective-permute-start(bf16[3,6912]{1,0:T(4,128)(2,1)} %param.6), channel_id=1, source_target_pairs={{0,512},{128,640},{256,0},{384,128},{512,256},{640,384},{1,513},{1... | collective-permute-start | bytes 124424 | tf_op jit(solution)/shard_map/ppermute | solution.py:46
  22.6 3.7 %collective-permute-start.4 = (bf16[3,6912]{1,0:T(4,128)(2,1)}, bf16[3,6912]{1,0:T(4,128)(2,1)}, u32[]{:S(2)}, u32[]{:S(2)}) collective-permute-start(bf16[3,6912]{1,0:T(4,128)(2,1)} %param.6), channel_id=1, source_target_pairs={{0,640},{128,0},{256,128},{384,256},{512,384},{640,512},{1,641},{1... | collective-permute-start | bytes 124424 | tf_op jit(solution)/shard_map/ppermute | solution.py:46
  26.4 1.5 convert_bitcast_fusion
  27.8 1.4 compare_select_fusion
  29.2 1.9 copy.40
  31.2 0.0 copy-start.5
  31.2 28.5 %scatter_custom_fusion = f32[3,9216]{0,1:T(8,128)} fusion(s32[6912]{0:T(1024)} %compare_select_fusion, f32[6912,3]{1,0:T(8,128)S(1)} %copy.40, f32[]{:T(128)} %constant.177.clone.1), kind=kCustom, calls=%fused_computation.5 | custom fusion | bytes 111104 | tf_op jit(solution)/shard_map/scatter | solution.py:64
  59.7 0.0 copy-start.4
  59.7 3.5 %copy.41 = f32[3,128,72]{1,2,0:T(8,128)S(1)} copy(f32[3,128,72]{0,2,1:T(8,128)} %bitcast.83) | data formatting | bytes 221184 | tf_op jit(solution)/shard_map/reshape | solution.py:65
  63.2 0.6 convolution_bitcast_fusion.1
  63.8 0.7 copy.42
  64.5 20.8 %all-to-all-start = ((f32[128,1,216]{2,1,0:T(1,128)}), f32[128,1,216]{2,1,0:T(1,128)S(1)}, u32[]{:S(2)}, u32[]{:S(2)}) async-start(f32[128,1,216]{2,1,0:T(1,128)} %copy.42), calls=%async_computation | async-start | bytes 262144 | tf_op jit(solution)/shard_map/all_to_all | solution.py:70
  85.4 0.6 pad_clamp_fusion
  86.0 0.7 fusion.37
  86.7 0.1 copy.52
  86.8 0.2 fusion.51
  87.1 0.8 copy.55
  87.9 0.1 broadcast_in_dim.31
  88.0 0.1 broadcast_in_dim.32
  88.1 0.0 collective-permute-done.1
  88.1 0.0 collective-permute-done.2
  88.1 5.2 %concatenate.6 = bf16[18,6912]{1,0:T(8,128)(2,1)S(1)} concatenate(bf16[3,6912]{1,0:T(4,128)(2,1)S(1)} %copy-done.1, bf16[3,6912]{1,0:T(4,128)(2,1)} %collective-permute-done, bf16[3,6912]{1,0:T(4,128)(2,1)} %collective-permute-done.1, bf16[3,6912]{1,0:T(4,128)(2,1)} %collective-permute-done.2, bf16[3,6912]{1,0:T(4,128)(2,1)} %collective-permute-done.3, ...), dimensions={0} | concatenate | bytes 497664 | tf_op jit(solution)/shard_map/concatenate | solution.py:47
  93.4 9.2 %all-to-all-done = f32[128,1,216]{2,1,0:T(1,128)S(1)} async-done(((f32[128,1,216]{2,1,0:T(1,128)}), f32[128,1,216]{2,1,0:T(1,128)S(1)}, u32[]{:S(2)}, u32[]{:S(2)}) %all-to-all-start) | async-done | bytes 110624 | tf_op jit(solution)/shard_map/all_to_all | solution.py:70
  102.6 0.1 copy.43
  102.7 0.1 copy.44
  102.8 0.1 reshape.161
  103.0 0.1 copy.45
  103.1 0.6 fusion.49
  103.7 0.6 convolution_multiply_fusion.1
  104.3 0.7 fusion.23
  105.0 0.6 convolution_bitcast_fusion
  105.6 0.1 reshape.163
  105.7 0.1 copy.46
  105.8 0.8 copy.47
  106.6 9.6 %all-to-all-start.1 = ((f32[128,1,216]{2,1,0:T(1,128)}), f32[128,1,216]{2,1,0:T(1,128)S(1)}, u32[]{:S(2)}, u32[]{:S(2)}) async-start(f32[128,1,216]{2,1,0:T(1,128)} %copy.47), calls=%async_computation.1 | async-start | bytes 262144 | tf_op jit(solution)/shard_map/all_to_all | solution.py:80
  116.2 5.0 %convolution_bitcast_fusion.2 = f32[512,18]{0,1:T(8,128)S(1)} fusion(bf16[18,6912]{1,0:T(8,128)(2,1)S(1)} %concatenate.6, bf16[512,6912]{1,0:T(8,128)(2,1)} %param.9), kind=kOutput, calls=%fused_computation.12 | convolution fusion | flops 127401984 | bytes 7363584 | tf_op jit(solution)/shard_map/dot_general | solution.py:86
  121.2 0.2 copy.54
  121.3 0.8 reshape.166
  122.1 11.3 %all-to-all-done.1 = f32[128,1,216]{2,1,0:T(1,128)S(1)} async-done(((f32[128,1,216]{2,1,0:T(1,128)}), f32[128,1,216]{2,1,0:T(1,128)S(1)}, u32[]{:S(2)}, u32[]{:S(2)}) %all-to-all-start.1) | async-done | bytes 110624 | tf_op jit(solution)/shard_map/all_to_all | solution.py:80
  133.4 0.1 copy.48
  133.6 0.6 fusion.8
  134.2 3.1 %copy.58 = f32[3,128,72]{0,2,1:T(8,128)} copy(f32[3,128,72]{1,2,0:T(8,128)S(1)} %bitcast.91) | data formatting | bytes 221184 | tf_op jit(solution)/shard_map/reshape | solution.py:83
  137.3 15.1 %gather_fusion = f32[6912,3]{1,0:T(8,128)S(1)} fusion(f32[3,9216]{0,1:T(8,128)} %bitcast.84, s32[7168]{0:T(1024)} %pad_clamp_fusion), kind=kCustom, calls=%fused_computation | custom fusion | bytes 193536 | tf_op jit(solution)/shard_map/gather | solution.py:83
  152.4 2.0 copy.51
  154.4 1.5 fusion.16
  155.9 0.1 reshape.167
  155.9 0.8 pad_maximum_fusion
  156.7 12.5 %psum.28 = f32[9270]{0:T(1024)S(1)} all-reduce(f32[9270]{0:T(1024)S(1)} %pad_maximum_fusion), channel_id=1, replica_groups=mesh['band'=6,'pw_0'=2,'pw_1'=4,'pw_2'=8,'pw_3'=2] {'pw_0'}, use_global_device_ids=true, to_apply=%region_1.2 | all-reduce | flops 9270 | bytes 74160 | tf_op jit(solution)/shard_map/psum | solution.py:16
  169.2 11.8 %psum.29 = f32[9270]{0:T(1024)S(1)} all-reduce(f32[9270]{0:T(1024)S(1)} %psum.28), channel_id=1, replica_groups=mesh['band'=6,'pw_0'=2,'pw_1'=4,'pw_2'=8,'pw_3'=2] {'pw_1'}, use_global_device_ids=true, to_apply=%region_2.3 | all-reduce | flops 9270 | bytes 74160 | tf_op jit(solution)/shard_map/psum | solution.py:16
  181.1 21.5 %psum.30 = f32[9270]{0:T(1024)S(1)} all-reduce(f32[9270]{0:T(1024)S(1)} %psum.29), channel_id=1, replica_groups=mesh['band'=6,'pw_0'=2,'pw_1'=4,'pw_2'=8,'pw_3'=2] {'pw_2'}, use_global_device_ids=true, to_apply=%region_3.4 | all-reduce | flops 9270 | bytes 74160 | tf_op jit(solution)/shard_map/psum | solution.py:16
  202.6 16.4 %psum.31 = f32[9270]{0:T(1024)S(1)} all-reduce(f32[9270]{0:T(1024)S(1)} %psum.30), channel_id=1, replica_groups=mesh['band'=6,'pw_0'=2,'pw_1'=4,'pw_2'=8,'pw_3'=2] {'pw_3'}, use_global_device_ids=true, to_apply=%region_4.5 | all-reduce | flops 9270 | bytes 74160 | tf_op jit(solution)/shard_map/psum | solution.py:16
  219.0 0.2 div.121
  219.2 0.2 div.127
  219.5 0.1 div.126
  219.5 1.5 fusion.3
  221.1 4.8 %fusion = f32[3,6912]{1,0:T(4,128)} fusion(bf16[512,6912]{1,0:T(8,128)(2,1)} %param.9, bf16[512,18]{1,0:T(8,128)(2,1)S(1)} %fusion.3, f32[6912,3]{0,1:T(4,128)} %copy.51, bf16[3,6912]{1,0:T(4,128)(2,1)} %param.6, f32[6912]{0:T(1024)} %fusion.37), kind=kOutput, calls=%fused_computation.4 | convolution fusion | flops 21337344 | bytes 7331328 | tf_op jit(solution)/shard_map/dot_general | solution.py:111
  225.9 0.3 fusion.4
  226.2 0.1 reshape.168
  226.3 0.6 gather_fusion.1
  226.9 0.1 gather.11
  227.0 0.6 broadcast_select_fusion
  (24 shorter events, 0.1 us)
Async XLA Ops:
  0.6 87.5 %collective-permute-start = (bf16[3,6912]{1,0:T(4,128)(2,1)}, bf16[3,6912]{1,0:T(4,128)(2,1)}, u32[]{:S(2)}, u32[]{:S(2)}) collective-permute-start(bf16[3,6912]{1,0:T(4,128)(2,1)} %param.6), channel_id=1, source_target_pairs={{0,128},{128,256},{256,384},{384,512},{512,640},{640,0},{1,129},{1... | collective-permute-start | bytes 124424 | tf_op jit(solution)/shard_map/ppermute | solution.py:46
  5.5 82.6 %collective-permute-start.1 = (bf16[3,6912]{1,0:T(4,128)(2,1)}, bf16[3,6912]{1,0:T(4,128)(2,1)}, u32[]{:S(2)}, u32[]{:S(2)}) collective-permute-start(bf16[3,6912]{1,0:T(4,128)(2,1)} %param.6), channel_id=1, source_target_pairs={{0,256},{128,384},{256,512},{384,640},{512,0},{640,128},{1,257},{1... | collective-permute-start | bytes 124424 | tf_op jit(solution)/shard_map/ppermute | solution.py:46
  11.3 76.8 %collective-permute-start.2 = (bf16[3,6912]{1,0:T(4,128)(2,1)}, bf16[3,6912]{1,0:T(4,128)(2,1)}, u32[]{:S(2)}, u32[]{:S(2)}) collective-permute-start(bf16[3,6912]{1,0:T(4,128)(2,1)} %param.6), channel_id=1, source_target_pairs={{0,384},{128,512},{256,640},{384,0},{512,128},{640,256},{1,385},{1... | collective-permute-start | bytes 124424 | tf_op jit(solution)/shard_map/ppermute | solution.py:46
  18.0 70.1 %collective-permute-start.3 = (bf16[3,6912]{1,0:T(4,128)(2,1)}, bf16[3,6912]{1,0:T(4,128)(2,1)}, u32[]{:S(2)}, u32[]{:S(2)}) collective-permute-start(bf16[3,6912]{1,0:T(4,128)(2,1)} %param.6), channel_id=1, source_target_pairs={{0,512},{128,640},{256,0},{384,128},{512,256},{640,384},{1,513},{1... | collective-permute-start | bytes 124424 | tf_op jit(solution)/shard_map/ppermute | solution.py:46
  22.6 65.5 %collective-permute-start.4 = (bf16[3,6912]{1,0:T(4,128)(2,1)}, bf16[3,6912]{1,0:T(4,128)(2,1)}, u32[]{:S(2)}, u32[]{:S(2)}) collective-permute-start(bf16[3,6912]{1,0:T(4,128)(2,1)} %param.6), channel_id=1, source_target_pairs={{0,640},{128,0},{256,128},{384,256},{512,384},{640,512},{1,641},{1... | collective-permute-start | bytes 124424 | tf_op jit(solution)/shard_map/ppermute | solution.py:46
  31.2 55.6 %copy-start.5 = (f32[4,8,8]{2,1,0:T(8,128)S(1)}, f32[4,8,8]{2,1,0:T(8,128)}, u32[]{:S(2)}) copy-start(f32[4,8,8]{2,1,0:T(8,128)} %param.11) | copy-start | bytes 3076
  59.7 25.7 %copy-start.3 = (s32[6912]{0:T(1024)S(1)}, s32[6912]{0:T(1024)}, u32[]{:S(2)}) copy-start(s32[6912]{0:T(1024)} %compare_select_fusion) | copy-start | bytes 82948
  59.7 26.3 %copy-start.2 = (s32[6912]{0:T(1024)S(1)}, s32[6912]{0:T(1024)}, u32[]{:S(2)}) copy-start(s32[6912]{0:T(1024)} %param.7) | copy-start | bytes 82948
  59.7 27.2 %copy-start.6 = (s32[64]{0:T(128)S(1)}, s32[64]{0:T(128)}, u32[]{:S(2)}) copy-start(s32[64]{0:T(128)} %param.10) | copy-start | bytes 772
  59.7 28.4 %copy-start.1 = (bf16[3,6912]{1,0:T(4,128)(2,1)S(1)}, bf16[3,6912]{1,0:T(4,128)(2,1)}, u32[]{:S(2)}) copy-start(bf16[3,6912]{1,0:T(4,128)(2,1)} %param.6) | copy-start | bytes 124420
  59.7 44.0 %copy-start.4 = (f32[1,128,128]{2,1,0:T(8,128)S(1)}, f32[1,128,128]{2,1,0:T(8,128)}, u32[]{:S(2)}) copy-start(f32[1,128,128]{2,1,0:T(8,128)} %param.8) | copy-start | bytes 196612
  64.5 38.0 %all-to-all-start = ((f32[128,1,216]{2,1,0:T(1,128)}), f32[128,1,216]{2,1,0:T(1,128)S(1)}, u32[]{:S(2)}, u32[]{:S(2)}) async-start(f32[128,1,216]{2,1,0:T(1,128)} %copy.42), calls=%async_computation | async-start | bytes 262144 | tf_op jit(solution)/shard_map/all_to_all | solution.py:70
  93.4 27.8 %copy-start = (bf16[18,6912]{1,0:T(8,128)(2,1)}, bf16[18,6912]{1,0:T(8,128)(2,1)S(1)}, u32[]{:S(2)}) copy-start(bf16[18,6912]{1,0:T(8,128)(2,1)S(1)} %concatenate.6) | copy-start | bytes 746500
  106.6 26.8 %all-to-all-start.1 = ((f32[128,1,216]{2,1,0:T(1,128)}), f32[128,1,216]{2,1,0:T(1,128)S(1)}, u32[]{:S(2)}, u32[]{:S(2)}) async-start(f32[128,1,216]{2,1,0:T(1,128)} %copy.47), calls=%async_computation.1 | async-start | bytes 262144 | tf_op jit(solution)/shard_map/all_to_all | solution.py:80

commit v3 on v2

--- a/solution.py
+++ b/solution.py
@@ -14,6 +14,16 @@
 def one_axis_at_a_time(x, axes):
     for a in axes:
         x = lax.psum(x, a)
+    return x
+
+
+def butterfly(x, axes):
+    for a in axes:
+        n = lax.axis_size(a)
+        d = 1
+        while d < n:
+            x = x + lax.ppermute(x, a, [(i, i ^ d) for i in range(n)])
+            d *= 2
     return x
 
 
@@ -61,8 +71,14 @@
     every = gathered_bands(states, "band")
     total = every.shape[0]
     wide = states.astype(jnp.float32)
-    dense = jnp.zeros((bands, length * stick_count), jnp.float32).at[:, slot_map].set(wide)
-    dense = dense.reshape(bands, length, stick_count)
+    plane_of = slot_map // stick_count
+    stick_of = slot_map % stick_count
+    on_stick = (stick_of[:, None] == jnp.arange(stick_count)[None, :]).astype(jnp.bfloat16)
+    on_plane = jnp.arange(length)[:, None] == plane_of[None, :]
+    spread = jnp.where(on_plane[None], states[:, None, :], jnp.zeros((), states.dtype))
+    dense = jnp.dot(
+        spread.reshape(bands * length, -1), on_stick, preferred_element_type=jnp.float32
+    ).reshape(bands, length, stick_count)
     z_table = cas_table(jnp.arange(length), length)
     side_table = cas_table(side_frequency(jnp.arange(side)), length)
     columns = jnp.einsum("bks,kz->zbs", dense, z_table, precision=highest)
@@ -80,7 +96,13 @@
     returned = lax.all_to_all(back, PW, 0, 0, tiled=True)
     returned = returned.reshape(npw * planes, bands, stick_count)
     spectral = jnp.einsum("zbs,kz->bks", returned, z_table, precision=highest)
-    local_term = spectral.reshape(bands, length * stick_count)[:, slot_map]
+    picked = jnp.dot(
+        spectral.reshape(bands * length, stick_count),
+        on_stick.T.astype(jnp.float32),
+        precision=highest,
+        preferred_element_type=jnp.float32,
+    ).reshape(bands, length, -1)
+    local_term = jnp.sum(jnp.where(on_plane[None], picked, 0.0), axis=1)
     energies = kinetic(slot_map, owner * stick_count, stick_count, length, side)
     diagonal = energies[None, :] * wide + local_term
     partial_corr = lax.dot_general(
@@ -95,7 +117,7 @@
     )
     nproj = partial_corr.shape[0]
     packed = jnp.concatenate([partial_corr.reshape(-1), partial_gram.reshape(-1)])
-    reduced = one_axis_at_a_time(packed, PW)
+    reduced = butterfly(packed, PW)
     correlations = reduced[: nproj * total].reshape(nproj, total) / math.sqrt(NG)
     gram = reduced[nproj * total :].reshape(bands, total)
     atoms = species.shape[0]

time: 229 us -> 164 us (0.72)
  blocking collectives: 62.2 us -> 0 us
  local copies, waits for them, and re-layouts: 65.1 us -> 5.37 us
  waiting for transfers between devices: 20.5 us -> 54.2 us
  starting transfers between devices: 56.1 us -> 76.8 us
  matrix products: 17 us -> 23 us
  other arithmetic: 5.65 us -> 2.08 us
    psum x4 -> x0, blocking collectives: 62.2 us -> none  [one_axis_at_a_time(): x = lax.psum(x, a)]
    scatter x1 -> x0, local copies, waits for them, and re-layouts: 28.5 us -> none  [local(): jnp.zeros((bands, length * stick_count), jnp.float32).at[:, slot_map]]
    ppermute x0 -> x7, waiting for transfers between devices: none -> 26.1 us  [butterfly(): x = x + lax.ppermute(x, a, [(i, i ^ d) for i in range(n)])]
    ppermute x0 -> x7, starting transfers between devices: none -> 24.7 us  [butterfly(): x = x + lax.ppermute(x, a, [(i, i ^ d) for i in range(n)])]
    gather x2 -> x0, local copies, waits for them, and re-layouts: 17.1 us -> none  [local(): local_term = spectral.reshape(bands, length * stick_count)[:, slot_map]]
    dot_general x1 -> x2, matrix products: 0.61 us -> 8.13 us  [the longest x1 5.51 us: local(): jnp.dot(spectral.reshape(bands * length, stick_count), on_stick.T.astype(...]
    all_to_all x1, waiting for transfers between devices: 9.19 us -> 16.1 us  [local(): piece = lax.all_to_all(sent, PW, 0, 0, tiled=True)]
    reshape x4 -> x3, local copies, waits for them, and re-layouts: 6.8 us -> 0.48 us  [the longest x1 3.46 us: local(): dense = dense.reshape(bands, length, stick_count)]
  transfers between devices with their start and end apart: 7 -> 14, of which waited for: 2 -> 9; matrix products, arithmetic and copies ran while one was open for 23% -> 8% of each run, Pallas kernels for 0% -> 0%
where the time goes in v3:
time: 164 us; the launch traced here: 163 us
  starting transfers between devices  76.8 us (47%)
  waiting for transfers between devices  54.2 us (33%)
  matrix products  23 us (14%)
  local copies, waits for them, and re-layouts  5.37 us (3%)
  other arithmetic  2.08 us (1%)
    ppermute x7, waiting for transfers between devices, butterfly(): x = x + lax.ppermute(x, a, [(i, i ^ d) for i in range(n)])  26.1 us
    ppermute x5, starting transfers between devices, gathered_bands(): lax.ppermute(states, axis, [(i, (i + k) % n) for i in range(n)])  25.7 us
    ppermute x7, starting transfers between devices, butterfly(): x = x + lax.ppermute(x, a, [(i, i ^ d) for i in range(n)])  24.7 us
    all_to_all x1, starting transfers between devices, local(): piece = lax.all_to_all(sent, PW, 0, 0, tiled=True)  20.8 us
    all_to_all x1, waiting for transfers between devices, local(): piece = lax.all_to_all(sent, PW, 0, 0, tiled=True)  16.1 us
    all_to_all x1, waiting for transfers between devices, local(): returned = lax.all_to_all(back, PW, 0, 0, tiled=True)  12 us
    all_to_all x1, starting transfers between devices, local(): returned = lax.all_to_all(back, PW, 0, 0, tiled=True)  5.58 us
    dot_general x1, matrix products, local(): jnp.dot(spectral.reshape(bands * length, stick_count), on_stick.T.astype(...  5.51 us
  transfers between devices with their start and end apart: 14, of which 9 were waited for; matrix products, arithmetic and copies ran while one was open for 8% of the time, Pallas kernels for 0%

profile of v3, /device:TPU:1, one launch (start us, length us, event | category | flops | bytes accessed | tf_op | source)
XLA Modules:
  0.0 162.6 jit_solution(4710755069930577879)
XLA Ops:
  0.6 4.8 %collective-permute-start = (bf16[3,6912]{1,0:T(4,128)(2,1)}, bf16[3,6912]{1,0:T(4,128)(2,1)S(1)}, u32[]{:S(2)}, u32[]{:S(2)}) collective-permute-start(bf16[3,6912]{1,0:T(4,128)(2,1)} %param.6), channel_id=1, source_target_pairs={{0,128},{128,256},{256,384},{384,512},{512,640},{640,0},{1,129},{1... | collective-permute-start | bytes 124424 | tf_op jit(solution)/shard_map/ppermute | solution.py:56
  5.5 5.8 %collective-permute-start.1 = (bf16[3,6912]{1,0:T(4,128)(2,1)}, bf16[3,6912]{1,0:T(4,128)(2,1)S(1)}, u32[]{:S(2)}, u32[]{:S(2)}) collective-permute-start(bf16[3,6912]{1,0:T(4,128)(2,1)} %param.6), channel_id=1, source_target_pairs={{0,256},{128,384},{256,512},{384,640},{512,0},{640,128},{1,257},{1... | collective-permute-start | bytes 124424 | tf_op jit(solution)/shard_map/ppermute | solution.py:56
  11.3 6.8 %collective-permute-start.2 = (bf16[3,6912]{1,0:T(4,128)(2,1)}, bf16[3,6912]{1,0:T(4,128)(2,1)S(1)}, u32[]{:S(2)}, u32[]{:S(2)}) collective-permute-start(bf16[3,6912]{1,0:T(4,128)(2,1)} %param.6), channel_id=1, source_target_pairs={{0,384},{128,512},{256,640},{384,0},{512,128},{640,256},{1,385},{1... | collective-permute-start | bytes 124424 | tf_op jit(solution)/shard_map/ppermute | solution.py:56
  18.0 4.6 %collective-permute-start.3 = (bf16[3,6912]{1,0:T(4,128)(2,1)}, bf16[3,6912]{1,0:T(4,128)(2,1)S(1)}, u32[]{:S(2)}, u32[]{:S(2)}) collective-permute-start(bf16[3,6912]{1,0:T(4,128)(2,1)} %param.6), channel_id=1, source_target_pairs={{0,512},{128,640},{256,0},{384,128},{512,256},{640,384},{1,513},{1... | collective-permute-start | bytes 124424 | tf_op jit(solution)/shard_map/ppermute | solution.py:56
  22.6 3.7 %collective-permute-start.4 = (bf16[3,6912]{1,0:T(4,128)(2,1)}, bf16[3,6912]{1,0:T(4,128)(2,1)S(1)}, u32[]{:S(2)}, u32[]{:S(2)}) collective-permute-start(bf16[3,6912]{1,0:T(4,128)(2,1)} %param.6), channel_id=1, source_target_pairs={{0,640},{128,0},{256,128},{384,256},{512,384},{640,512},{1,641},{1... | collective-permute-start | bytes 124424 | tf_op jit(solution)/shard_map/ppermute | solution.py:56
  26.4 0.8 add_select_fusion.9
  27.1 0.5 iota_compare_fusion
  27.6 2.6 %fusion.1 = f32[3,128,72]{1,2,0:T(8,128)S(1)} fusion(pred[128,6912]{1,0:T(8,128)(4,1)S(1)} %iota_compare_fusion, bf16[3,6912]{1,0:T(4,128)(2,1)} %param.6, s32[6912]{0:T(1024)S(1)} %get-tuple-element.2), kind=kOutput, calls=%fused_computation.4 | convolution fusion | flops 385357824 | bytes 1064448 | tf_op jit(solution)/shard_map/dot_general | solution.py:79
  30.3 0.6 convolution_bitcast_fusion.1
  30.9 0.8 copy.24
  31.6 20.8 %all-to-all-start = ((f32[128,1,216]{2,1,0:T(1,128)}), f32[128,1,216]{2,1,0:T(1,128)S(1)}, u32[]{:S(2)}, u32[]{:S(2)}) async-start(f32[128,1,216]{2,1,0:T(1,128)} %copy.24), calls=%async_computation | async-start | bytes 262144 | tf_op jit(solution)/shard_map/all_to_all | solution.py:86
  52.5 0.1 fusion.41
  52.7 0.9 concatenate.6
  53.6 16.1 %all-to-all-done = f32[128,1,216]{2,1,0:T(1,128)S(1)} async-done(((f32[128,1,216]{2,1,0:T(1,128)}), f32[128,1,216]{2,1,0:T(1,128)S(1)}, u32[]{:S(2)}, u32[]{:S(2)}) %all-to-all-start) | async-done | bytes 110624 | tf_op jit(solution)/shard_map/all_to_all | solution.py:86
  69.7 0.1 copy.25
  69.8 0.1 copy.26
  69.9 0.1 reshape.186
  70.1 0.1 copy.27
  70.2 0.6 fusion.53
  70.8 0.6 convolution_multiply_fusion.1
  71.4 0.7 fusion.28
  72.1 0.6 convolution_bitcast_fusion
  72.7 0.1 reshape.188
  72.8 0.1 copy.28
  73.0 0.8 copy.29
  73.7 5.6 %all-to-all-start.1 = ((f32[128,1,216]{2,1,0:T(1,128)}), f32[128,1,216]{2,1,0:T(1,128)S(1)}, u32[]{:S(2)}, u32[]{:S(2)}) async-start(f32[128,1,216]{2,1,0:T(1,128)} %copy.29), calls=%async_computation.1 | async-start | bytes 262144 | tf_op jit(solution)/shard_map/all_to_all | solution.py:96
  79.3 5.0 %convolution_bitcast_fusion.2 = f32[512,18]{0,1:T(8,128)S(1)} fusion(bf16[18,6912]{1,0:T(8,128)(2,1)S(1)} %concatenate.6, bf16[512,6912]{1,0:T(8,128)(2,1)} %param.9), kind=kOutput, calls=%fused_computation.17 | convolution fusion | flops 127401984 | bytes 7363584 | tf_op jit(solution)/shard_map/dot_general | solution.py:108
  84.3 0.2 copy.33
  84.4 0.2 reshape.190
  84.6 12.0 %all-to-all-done.1 = f32[128,1,216]{2,1,0:T(1,128)S(1)} async-done(((f32[128,1,216]{2,1,0:T(1,128)}), f32[128,1,216]{2,1,0:T(1,128)S(1)}, u32[]{:S(2)}, u32[]{:S(2)}) %all-to-all-start.1) | async-done | bytes 110624 | tf_op jit(solution)/shard_map/all_to_all | solution.py:96
  96.7 0.1 copy.30
  96.8 0.6 fusion.14
  97.4 5.5 %select_reduce_fusion = f32[3,6912]{1,0:T(4,128)S(1)} fusion(f32[3,128,72]{1,2,0:T(8,128)S(1)} %bitcast.88, pred[128,6912]{1,0:T(8,128)(4,1)S(1)} %iota_compare_fusion, s32[6912]{0:T(1024)S(1)} %get-tuple-element.2), kind=kOutput, calls=%fused_computation.1 | convolution fusion | flops 2299021056 | bytes 1105920 | tf_op jit(solution)/shard_map/dot_general | solution.py:99
  102.9 0.4 fusion.22
  103.3 0.1 reshape.191
  103.4 2.8 %collective-permute-start.5 = (f32[9270]{0:T(1024)S(1)}, f32[9270]{0:T(1024)S(1)}, u32[]{:S(2)}, u32[]{:S(2)}) collective-permute-start(f32[9270]{0:T(1024)S(1)} %constant_dynamic-update-slice_fusion), channel_id=1, source_target_pairs={{0,64},{64,0},{1,65},{65,1},{2,66},{66,2},{3,67},{67,3},{4,68},{68... | collective-permute-start | bytes 111248 | tf_op jit(solution)/shard_map/ppermute | solution.py:25
  106.3 8.2 %collective-permute-done.5 = f32[9270]{0:T(1024)S(1)} collective-permute-done((f32[9270]{0:T(1024)S(1)}, f32[9270]{0:T(1024)S(1)}, u32[]{:S(2)}, u32[]{:S(2)}) %collective-permute-start.5) | collective-permute-done | bytes 37112 | tf_op jit(solution)/shard_map/ppermute | solution.py:25
  114.5 2.3 %collective-permute-start.6 = (f32[9270]{0:T(1024)S(1)}, f32[9270]{0:T(1024)S(1)}, u32[]{:S(2)}, u32[]{:S(2)}) collective-permute-start(f32[9270]{0:T(1024)S(1)} %add.206), channel_id=1, source_target_pairs={{0,16},{16,0},{32,48},{48,32},{1,17},{17,1},{33,49},{49,33},{2,18}... | collective-permute-start | bytes 111248 | tf_op jit(solution)/shard_map/ppermute | solution.py:25
  116.8 0.1 copy.31
  116.9 2.3 %collective-permute-done.6 = f32[9270]{0:T(1024)S(1)} collective-permute-done((f32[9270]{0:T(1024)S(1)}, f32[9270]{0:T(1024)S(1)}, u32[]{:S(2)}, u32[]{:S(2)}) %collective-permute-start.6) | collective-permute-done | bytes 37112 | tf_op jit(solution)/shard_map/ppermute | solution.py:25
  119.2 3.2 %collective-permute-start.7 = (f32[9270]{0:T(1024)S(1)}, f32[9270]{0:T(1024)S(1)}, u32[]{:S(2)}, u32[]{:S(2)}) collective-permute-start(f32[9270]{0:T(1024)S(1)} %add.207), channel_id=1, source_target_pairs={{0,32},{16,48},{32,0},{48,16},{1,33},{17,49},{33,1},{49,17},{2,34}... | collective-permute-start | bytes 111248 | tf_op jit(solution)/shard_map/ppermute | solution.py:25
  122.5 3.0 %collective-permute-done.7 = f32[9270]{0:T(1024)S(1)} collective-permute-done((f32[9270]{0:T(1024)S(1)}, f32[9270]{0:T(1024)S(1)}, u32[]{:S(2)}, u32[]{:S(2)}) %collective-permute-start.7) | collective-permute-done | bytes 37112 | tf_op jit(solution)/shard_map/ppermute | solution.py:25
  125.5 2.5 %collective-permute-start.8 = (f32[9270]{0:T(1024)S(1)}, f32[9270]{0:T(1024)S(1)}, u32[]{:S(2)}, u32[]{:S(2)}) collective-permute-start(f32[9270]{0:T(1024)S(1)} %add.208), channel_id=1, source_target_pairs={{0,2},{2,0},{4,6},{6,4},{8,10},{10,8},{12,14},{14,12},{1,3},{3,1},... | collective-permute-start | bytes 111248 | tf_op jit(solution)/shard_map/ppermute | solution.py:25
  128.0 0.2 fusion.55
  128.2 2.0 %collective-permute-done.8 = f32[9270]{0:T(1024)S(1)} collective-permute-done((f32[9270]{0:T(1024)S(1)}, f32[9270]{0:T(1024)S(1)}, u32[]{:S(2)}, u32[]{:S(2)}) %collective-permute-start.8) | collective-permute-done | bytes 37112 | tf_op jit(solution)/shard_map/ppermute | solution.py:25
  130.2 2.6 %collective-permute-start.9 = (f32[9270]{0:T(1024)S(1)}, f32[9270]{0:T(1024)S(1)}, u32[]{:S(2)}, u32[]{:S(2)}) collective-permute-start(f32[9270]{0:T(1024)S(1)} %add.209), channel_id=1, source_target_pairs={{0,4},{2,6},{4,0},{6,2},{8,12},{10,14},{12,8},{14,10},{1,5},{3,7},... | collective-permute-start | bytes 111248 | tf_op jit(solution)/shard_map/ppermute | solution.py:25
  132.9 3.4 %collective-permute-done.9 = f32[9270]{0:T(1024)S(1)} collective-permute-done((f32[9270]{0:T(1024)S(1)}, f32[9270]{0:T(1024)S(1)}, u32[]{:S(2)}, u32[]{:S(2)}) %collective-permute-start.9) | collective-permute-done | bytes 37112 | tf_op jit(solution)/shard_map/ppermute | solution.py:25
  136.3 2.2 %collective-permute-start.10 = (f32[9270]{0:T(1024)S(1)}, f32[9270]{0:T(1024)S(1)}, u32[]{:S(2)}, u32[]{:S(2)}) collective-permute-start(f32[9270]{0:T(1024)S(1)} %add.210), channel_id=1, source_target_pairs={{0,8},{2,10},{4,12},{6,14},{8,0},{10,2},{12,4},{14,6},{1,9},{3,11}... | collective-permute-start | bytes 111248 | tf_op jit(solution)/shard_map/ppermute | solution.py:25
  138.6 6.5 %collective-permute-done.10 = f32[9270]{0:T(1024)S(1)} collective-permute-done((f32[9270]{0:T(1024)S(1)}, f32[9270]{0:T(1024)S(1)}, u32[]{:S(2)}, u32[]{:S(2)}) %collective-permute-start.10) | collective-permute-done | bytes 37112 | tf_op jit(solution)/shard_map/ppermute | solution.py:25
  145.1 9.1 %collective-permute-start.11 = (f32[9270]{0:T(1024)S(1)}, f32[9270]{0:T(1024)S(1)}, u32[]{:S(2)}, u32[]{:S(2)}) collective-permute-start(f32[9270]{0:T(1024)S(1)} %add.211), channel_id=1, source_target_pairs={{0,1},{1,0},{2,3},{3,2},{4,5},{5,4},{6,7},{7,6},{8,9},{9,8},{10,11... | collective-permute-start | bytes 111248 | tf_op jit(solution)/shard_map/ppermute | solution.py:25
  154.2 0.1 copy.34
  154.4 0.1 broadcast_in_dim.63
  154.4 0.1 broadcast_in_dim.64
  154.5 0.5 collective-permute-done.11
  155.1 0.2 reshape.192
  155.3 0.2 div.126
  155.5 0.6 fusion.9
  156.1 4.7 %fusion = f32[3,6912]{1,0:T(4,128)} fusion(bf16[512,6912]{1,0:T(8,128)(2,1)} %param.9, bf16[512,18]{1,0:T(8,128)(2,1)S(1)} %fusion.9, f32[3,6912]{1,0:T(4,128)S(1)} %select_reduce_fusion, bf16[3,6912]{1,0:T(4,128)(2,1)S(1)} %copy-done, f32[6912]{0:T(1024)S(1)} %fusion.41), kind=kOutput, calls=%fused_computation.3 | convolution fusion | flops 21337344 | bytes 7331328 | tf_op jit(solution)/shard_map/dot_general | solution.py:133
  160.8 0.3 convolution_multiply_fusion.2
  161.2 0.1 div.125
  161.3 0.1 reshape.193
  161.3 0.6 gather_fusion
  162.0 0.1 gather.7
  162.0 0.6 broadcast_select_fusion
  (34 shorter events, 0.2 us)
Async XLA Ops:
  0.6 52.0 %collective-permute-start = (bf16[3,6912]{1,0:T(4,128)(2,1)}, bf16[3,6912]{1,0:T(4,128)(2,1)S(1)}, u32[]{:S(2)}, u32[]{:S(2)}) collective-permute-start(bf16[3,6912]{1,0:T(4,128)(2,1)} %param.6), channel_id=1, source_target_pairs={{0,128},{128,256},{256,384},{384,512},{512,640},{640,0},{1,129},{1... | collective-permute-start | bytes 124424 | tf_op jit(solution)/shard_map/ppermute | solution.py:56
  5.5 47.2 %collective-permute-start.1 = (bf16[3,6912]{1,0:T(4,128)(2,1)}, bf16[3,6912]{1,0:T(4,128)(2,1)S(1)}, u32[]{:S(2)}, u32[]{:S(2)}) collective-permute-start(bf16[3,6912]{1,0:T(4,128)(2,1)} %param.6), channel_id=1, source_target_pairs={{0,256},{128,384},{256,512},{384,640},{512,0},{640,128},{1,257},{1... | collective-permute-start | bytes 124424 | tf_op jit(solution)/shard_map/ppermute | solution.py:56
  11.3 41.4 %collective-permute-start.2 = (bf16[3,6912]{1,0:T(4,128)(2,1)}, bf16[3,6912]{1,0:T(4,128)(2,1)S(1)}, u32[]{:S(2)}, u32[]{:S(2)}) collective-permute-start(bf16[3,6912]{1,0:T(4,128)(2,1)} %param.6), channel_id=1, source_target_pairs={{0,384},{128,512},{256,640},{384,0},{512,128},{640,256},{1,385},{1... | collective-permute-start | bytes 124424 | tf_op jit(solution)/shard_map/ppermute | solution.py:56
  18.0 34.6 %collective-permute-start.3 = (bf16[3,6912]{1,0:T(4,128)(2,1)}, bf16[3,6912]{1,0:T(4,128)(2,1)S(1)}, u32[]{:S(2)}, u32[]{:S(2)}) collective-permute-start(bf16[3,6912]{1,0:T(4,128)(2,1)} %param.6), channel_id=1, source_target_pairs={{0,512},{128,640},{256,0},{384,128},{512,256},{640,384},{1,513},{1... | collective-permute-start | bytes 124424 | tf_op jit(solution)/shard_map/ppermute | solution.py:56
  22.6 30.0 %collective-permute-start.4 = (bf16[3,6912]{1,0:T(4,128)(2,1)}, bf16[3,6912]{1,0:T(4,128)(2,1)S(1)}, u32[]{:S(2)}, u32[]{:S(2)}) collective-permute-start(bf16[3,6912]{1,0:T(4,128)(2,1)} %param.6), channel_id=1, source_target_pairs={{0,640},{128,0},{256,128},{384,256},{512,384},{640,512},{1,641},{1... | collective-permute-start | bytes 124424 | tf_op jit(solution)/shard_map/ppermute | solution.py:56
  27.6 24.8 %copy-start.1 = (s32[6912]{0:T(1024)S(1)}, s32[6912]{0:T(1024)}, u32[]{:S(2)}) copy-start(s32[6912]{0:T(1024)} %param.7) | copy-start | bytes 82948
  27.6 25.1 %copy-start = (bf16[3,6912]{1,0:T(4,128)(2,1)S(1)}, bf16[3,6912]{1,0:T(4,128)(2,1)}, u32[]{:S(2)}) copy-start(bf16[3,6912]{1,0:T(4,128)(2,1)} %param.6) | copy-start | bytes 124420
  27.6 43.1 %copy-start.2 = (f32[1,128,128]{2,1,0:T(8,128)S(1)}, f32[1,128,128]{2,1,0:T(8,128)}, u32[]{:S(2)}) copy-start(f32[1,128,128]{2,1,0:T(8,128)} %param.8) | copy-start | bytes 196612
  31.6 38.1 %all-to-all-start = ((f32[128,1,216]{2,1,0:T(1,128)}), f32[128,1,216]{2,1,0:T(1,128)S(1)}, u32[]{:S(2)}, u32[]{:S(2)}) async-start(f32[128,1,216]{2,1,0:T(1,128)} %copy.24), calls=%async_computation | async-start | bytes 262144 | tf_op jit(solution)/shard_map/all_to_all | solution.py:86
  73.7 23.0 %all-to-all-start.1 = ((f32[128,1,216]{2,1,0:T(1,128)}), f32[128,1,216]{2,1,0:T(1,128)S(1)}, u32[]{:S(2)}, u32[]{:S(2)}) async-start(f32[128,1,216]{2,1,0:T(1,128)} %copy.29), calls=%async_computation.1 | async-start | bytes 262144 | tf_op jit(solution)/shard_map/all_to_all | solution.py:96
  97.4 19.4 %copy-start.3 = (f32[4,8,8]{2,1,0:T(8,128)S(1)}, f32[4,8,8]{2,1,0:T(8,128)}, u32[]{:S(2)}) copy-start(f32[4,8,8]{2,1,0:T(8,128)} %param.11) | copy-start | bytes 3076
  97.4 30.6 %copy-start.4 = (s32[64]{0:T(128)S(1)}, s32[64]{0:T(128)}, u32[]{:S(2)}) copy-start(s32[64]{0:T(128)} %param.10) | copy-start | bytes 772
  103.4 11.1 %collective-permute-start.5 = (f32[9270]{0:T(1024)S(1)}, f32[9270]{0:T(1024)S(1)}, u32[]{:S(2)}, u32[]{:S(2)}) collective-permute-start(f32[9270]{0:T(1024)S(1)} %constant_dynamic-update-slice_fusion), channel_id=1, source_target_pairs={{0,64},{64,0},{1,65},{65,1},{2,66},{66,2},{3,67},{67,3},{4,68},{68... | collective-permute-start | bytes 111248 | tf_op jit(solution)/shard_map/ppermute | solution.py:25
  114.5 4.7 %collective-permute-start.6 = (f32[9270]{0:T(1024)S(1)}, f32[9270]{0:T(1024)S(1)}, u32[]{:S(2)}, u32[]{:S(2)}) collective-permute-start(f32[9270]{0:T(1024)S(1)} %add.206), channel_id=1, source_target_pairs={{0,16},{16,0},{32,48},{48,32},{1,17},{17,1},{33,49},{49,33},{2,18}... | collective-permute-start | bytes 111248 | tf_op jit(solution)/shard_map/ppermute | solution.py:25
  119.2 6.2 %collective-permute-start.7 = (f32[9270]{0:T(1024)S(1)}, f32[9270]{0:T(1024)S(1)}, u32[]{:S(2)}, u32[]{:S(2)}) collective-permute-start(f32[9270]{0:T(1024)S(1)} %add.207), channel_id=1, source_target_pairs={{0,32},{16,48},{32,0},{48,16},{1,33},{17,49},{33,1},{49,17},{2,34}... | collective-permute-start | bytes 111248 | tf_op jit(solution)/shard_map/ppermute | solution.py:25
  125.5 4.7 %collective-permute-start.8 = (f32[9270]{0:T(1024)S(1)}, f32[9270]{0:T(1024)S(1)}, u32[]{:S(2)}, u32[]{:S(2)}) collective-permute-start(f32[9270]{0:T(1024)S(1)} %add.208), channel_id=1, source_target_pairs={{0,2},{2,0},{4,6},{6,4},{8,10},{10,8},{12,14},{14,12},{1,3},{3,1},... | collective-permute-start | bytes 111248 | tf_op jit(solution)/shard_map/ppermute | solution.py:25
  130.2 6.1 %collective-permute-start.9 = (f32[9270]{0:T(1024)S(1)}, f32[9270]{0:T(1024)S(1)}, u32[]{:S(2)}, u32[]{:S(2)}) collective-permute-start(f32[9270]{0:T(1024)S(1)} %add.209), channel_id=1, source_target_pairs={{0,4},{2,6},{4,0},{6,2},{8,12},{10,14},{12,8},{14,10},{1,5},{3,7},... | collective-permute-start | bytes 111248 | tf_op jit(solution)/shard_map/ppermute | solution.py:25
  136.3 8.8 %collective-permute-start.10 = (f32[9270]{0:T(1024)S(1)}, f32[9270]{0:T(1024)S(1)}, u32[]{:S(2)}, u32[]{:S(2)}) collective-permute-start(f32[9270]{0:T(1024)S(1)} %add.210), channel_id=1, source_target_pairs={{0,8},{2,10},{4,12},{6,14},{8,0},{10,2},{12,4},{14,6},{1,9},{3,11}... | collective-permute-start | bytes 111248 | tf_op jit(solution)/shard_map/ppermute | solution.py:25
  145.1 9.9 %collective-permute-start.11 = (f32[9270]{0:T(1024)S(1)}, f32[9270]{0:T(1024)S(1)}, u32[]{:S(2)}, u32[]{:S(2)}) collective-permute-start(f32[9270]{0:T(1024)S(1)} %add.211), channel_id=1, source_target_pairs={{0,1},{1,0},{2,3},{3,2},{4,5},{5,4},{6,7},{7,6},{8,9},{9,8},{10,11... | collective-permute-start | bytes 111248 | tf_op jit(solution)/shard_map/ppermute | solution.py:25

commit v4 on v3

--- a/solution.py
+++ b/solution.py
@@ -70,31 +70,71 @@
     ngroup = lax.axis_size("band")
     every = gathered_bands(states, "band")
     total = every.shape[0]
+    count = states.shape[1]
     wide = states.astype(jnp.float32)
     plane_of = slot_map // stick_count
     stick_of = slot_map % stick_count
-    on_stick = (stick_of[:, None] == jnp.arange(stick_count)[None, :]).astype(jnp.bfloat16)
+    on_stick = stick_of[:, None] == jnp.arange(stick_count)[None, :]
     on_plane = jnp.arange(length)[:, None] == plane_of[None, :]
-    spread = jnp.where(on_plane[None], states[:, None, :], jnp.zeros((), states.dtype))
+    spread = jnp.where(on_stick[:, None, :], every.T[:, :, None], jnp.zeros((), every.dtype))
     dense = jnp.dot(
-        spread.reshape(bands * length, -1), on_stick, preferred_element_type=jnp.float32
-    ).reshape(bands, length, stick_count)
+        on_plane.astype(jnp.bfloat16),
+        spread.reshape(count, total * stick_count),
+        preferred_element_type=jnp.float32,
+    )
     z_table = cas_table(jnp.arange(length), length)
     side_table = cas_table(side_frequency(jnp.arange(side)), length)
-    columns = jnp.einsum("bks,kz->zbs", dense, z_table, precision=highest)
-    sent = columns.reshape(npw, planes * bands * stick_count)
-    piece = lax.all_to_all(sent, PW, 0, 0, tiled=True)
-    piece = piece.reshape(npw, planes, bands, stick_count)
-    grid = jnp.transpose(piece, (2, 1, 0, 3)).reshape(bands, planes, side, side)
+    columns = jnp.dot(z_table.T, dense, precision=highest, preferred_element_type=jnp.float32)
+    energies = kinetic(slot_map, owner * stick_count, stick_count, length, side)
+    partial_corr = lax.dot_general(
+        projectors, every, (((1,), (1,)), ((), ())), preferred_element_type=jnp.float32
+    )
+    partial_kin = lax.dot_general(
+        energies[None, :] * wide,
+        every.astype(jnp.float32),
+        (((1,), (1,)), ((), ())),
+        precision=highest,
+        preferred_element_type=jnp.float32,
+    )
+    nproj = partial_corr.shape[0]
+    packed = jnp.concatenate([partial_corr.reshape(-1), partial_kin.reshape(-1)])
+    width = -(-packed.shape[0] // npw)
+    packed = jnp.pad(packed, (0, width * npw - packed.shape[0])).reshape(npw, width)
+    sent = jnp.concatenate([columns.reshape(npw, planes * total * stick_count), packed], axis=1)
+    got = lax.all_to_all(sent, PW, 0, 0, tiled=True)
+    piece = got[:, : planes * total * stick_count].reshape(npw, total, stick_count)
+    owned = jnp.sum(got[:, planes * total * stick_count :], axis=0)
+    grid = jnp.transpose(piece[:, :bands, :], (1, 0, 2)).reshape(bands, planes, side, side)
     half = jnp.einsum("bzjk,jx->bzxk", grid, side_table, precision=highest)
     real_space = jnp.einsum("bzxk,ky->bzxy", half, side_table, precision=highest)
     weighted = real_space * potential[None]
     back_half = jnp.einsum("bzxy,ky->bzxk", weighted, side_table, precision=highest)
     back_grid = jnp.einsum("bzxk,jx->bzjk", back_half, side_table, precision=highest)
-    back = back_grid.reshape(bands, planes, npw, stick_count)
-    back = jnp.transpose(back, (2, 1, 0, 3)).reshape(npw, planes * bands * stick_count)
-    returned = lax.all_to_all(back, PW, 0, 0, tiled=True)
-    returned = returned.reshape(npw * planes, bands, stick_count)
+    back_own = back_grid.reshape(bands, side * side)
+    plane_gram = lax.dot_general(
+        back_own,
+        jnp.transpose(piece, (1, 0, 2)).reshape(total, side * side),
+        (((1,), (1,)), ((), ())),
+        precision=highest,
+        preferred_element_type=jnp.float32,
+    )
+    back = jnp.transpose(back_own.reshape(bands, npw, stick_count), (1, 0, 2))
+    ret_sent = jnp.concatenate(
+        [
+            back.reshape(npw, bands * stick_count),
+            jnp.broadcast_to(plane_gram.reshape(1, -1), (npw, bands * total)),
+            jnp.broadcast_to(owned[None, :], (npw, width)),
+        ],
+        axis=1,
+    )
+    ret = lax.all_to_all(ret_sent, PW, 0, 0, tiled=True)
+    returned = ret[:, : bands * stick_count].reshape(npw * planes, bands, stick_count)
+    gram_local = jnp.sum(
+        ret[:, bands * stick_count : bands * stick_count + bands * total], axis=0
+    ).reshape(bands, total)
+    reduced = ret[:, bands * stick_count + bands * total :].reshape(-1)
+    correlations = reduced[: nproj * total].reshape(nproj, total) / math.sqrt(NG)
+    gram_kin = reduced[nproj * total : nproj * total + bands * total].reshape(bands, total)
     spectral = jnp.einsum("zbs,kz->bks", returned, z_table, precision=highest)
     picked = jnp.dot(
         spectral.reshape(bands * length, stick_count),
@@ -103,23 +143,6 @@
         preferred_element_type=jnp.float32,
     ).reshape(bands, length, -1)
     local_term = jnp.sum(jnp.where(on_plane[None], picked, 0.0), axis=1)
-    energies = kinetic(slot_map, owner * stick_count, stick_count, length, side)
-    diagonal = energies[None, :] * wide + local_term
-    partial_corr = lax.dot_general(
-        projectors, every, (((1,), (1,)), ((), ())), preferred_element_type=jnp.float32
-    )
-    partial_gram = lax.dot_general(
-        diagonal,
-        every.astype(jnp.float32),
-        (((1,), (1,)), ((), ())),
-        precision=highest,
-        preferred_element_type=jnp.float32,
-    )
-    nproj = partial_corr.shape[0]
-    packed = jnp.concatenate([partial_corr.reshape(-1), partial_gram.reshape(-1)])
-    reduced = butterfly(packed, PW)
-    correlations = reduced[: nproj * total].reshape(nproj, total) / math.sqrt(NG)
-    gram = reduced[nproj * total :].reshape(bands, total)
     atoms = species.shape[0]
     per_atom = coupling.shape[1]
     kinds = coupling.shape[0]
@@ -133,7 +156,7 @@
     nonlocal_term = lax.dot_general(
         weights[:, :bands], projectors, (((0,), (0,)), ((), ())), preferred_element_type=jnp.float32
     ) / math.sqrt(atoms * per_atom)
-    applied = diagonal + nonlocal_term
+    applied = energies[None, :] * wide + local_term + nonlocal_term
     cross = lax.dot_general(
         correlations[:, :bands],
         weights.astype(jnp.float32),
@@ -141,7 +164,7 @@
         precision=highest,
         preferred_element_type=jnp.float32,
     ) / (math.sqrt(atoms * per_atom) * math.sqrt(NG))
-    rotated = (gram / float(NG) + cross).reshape(bands, ngroup, bands)
+    rotated = ((gram_kin + gram_local) / float(NG) + cross).reshape(bands, ngroup, bands)
     order = (group - jnp.arange(ngroup)) % ngroup
     subspace = jnp.take(rotated, order, axis=1).reshape(bands, total)
     return (applied, subspace)

time: 164 us -> 153 us (0.933)
  the two profiles are of different devices: /device:TPU:1 before, /device:TPU:65 now
where the time goes in v4:
time: 153 us
  waiting for transfers between devices  55.6 us (36%)
  starting transfers between devices  50.4 us (33%)
  matrix products  28.2 us (18%)
  local copies, waits for them, and re-layouts  11.7 us (8%)
  other arithmetic  5.8 us (4%)
    all_to_all x1, waiting for transfers between devices, local(): got = lax.all_to_all(sent, PW, 0, 0, tiled=True)  35.5 us
    ppermute x5, starting transfers between devices, gathered_bands(): lax.ppermute(states, axis, [(i, (i + k) % n) for i in range(n)])  23.1 us
    all_to_all x1, starting transfers between devices, local(): got = lax.all_to_all(sent, PW, 0, 0, tiled=True)  20.6 us
    all_to_all x1, waiting for transfers between devices, local(): ret = lax.all_to_all(ret_sent, PW, 0, 0, tiled=True)  19.2 us
    all_to_all x1, starting transfers between devices, local(): ret = lax.all_to_all(ret_sent, PW, 0, 0, tiled=True)  6.73 us
    dot_general x1, matrix products, local(): jnp.dot(spectral.reshape(bands * length, stick_count), on_stick.T.astype(...  6.69 us
    dot_general x1, matrix products, local(): lax.dot_general(projectors, every, (((1,), (1,)), ((), ())), preferred_el...  4.99 us
    dot_general x1, matrix products, local(): jnp.dot(on_plane.astype(jnp.bfloat16), spread.reshape(count, total * stic...  4.94 us
  transfers between devices with their start and end apart: 7, of which 3 were waited for; matrix products, arithmetic and copies ran while one was open for 3% of the time, Pallas kernels for 0%

profile of v4, /device:TPU:65, one launch (start us, length us, event | category | flops | bytes accessed | tf_op | source)
XLA Modules:
  0.0 152.7 jit_solution(14502293636507479372)
XLA Ops:
  0.6 4.0 %collective-permute-start = (bf16[3,6912]{1,0:T(4,128)(2,1)}, bf16[3,6912]{1,0:T(4,128)(2,1)S(1)}, u32[]{:S(2)}, u32[]{:S(2)}) collective-permute-start(bf16[3,6912]{1,0:T(4,128)(2,1)} %param.6), channel_id=1, source_target_pairs={{0,128},{128,256},{256,384},{384,512},{512,640},{640,0},{1,129},{1... | collective-permute-start | bytes 124424 | tf_op jit(solution)/shard_map/ppermute | solution.py:56
  4.6 7.0 %collective-permute-start.1 = (bf16[3,6912]{1,0:T(4,128)(2,1)}, bf16[3,6912]{1,0:T(4,128)(2,1)S(1)}, u32[]{:S(2)}, u32[]{:S(2)}) collective-permute-start(bf16[3,6912]{1,0:T(4,128)(2,1)} %param.6), channel_id=1, source_target_pairs={{0,256},{128,384},{256,512},{384,640},{512,0},{640,128},{1,257},{1... | collective-permute-start | bytes 124424 | tf_op jit(solution)/shard_map/ppermute | solution.py:56
  11.7 3.7 %collective-permute-start.2 = (bf16[3,6912]{1,0:T(4,128)(2,1)}, bf16[3,6912]{1,0:T(4,128)(2,1)S(1)}, u32[]{:S(2)}, u32[]{:S(2)}) collective-permute-start(bf16[3,6912]{1,0:T(4,128)(2,1)} %param.6), channel_id=1, source_target_pairs={{0,384},{128,512},{256,640},{384,0},{512,128},{640,256},{1,385},{1... | collective-permute-start | bytes 124424 | tf_op jit(solution)/shard_map/ppermute | solution.py:56
  15.4 6.4 %collective-permute-start.3 = (bf16[3,6912]{1,0:T(4,128)(2,1)}, bf16[3,6912]{1,0:T(4,128)(2,1)S(1)}, u32[]{:S(2)}, u32[]{:S(2)}) collective-permute-start(bf16[3,6912]{1,0:T(4,128)(2,1)} %param.6), channel_id=1, source_target_pairs={{0,512},{128,640},{256,0},{384,128},{512,256},{640,384},{1,513},{1... | collective-permute-start | bytes 124424 | tf_op jit(solution)/shard_map/ppermute | solution.py:56
  21.8 1.9 %collective-permute-start.4 = (bf16[3,6912]{1,0:T(4,128)(2,1)}, bf16[3,6912]{1,0:T(4,128)(2,1)S(1)}, u32[]{:S(2)}, u32[]{:S(2)}) collective-permute-start(bf16[3,6912]{1,0:T(4,128)(2,1)} %param.6), channel_id=1, source_target_pairs={{0,640},{128,0},{256,128},{384,256},{512,384},{640,512},{1,641},{1... | collective-permute-start | bytes 124424 | tf_op jit(solution)/shard_map/ppermute | solution.py:56
  23.7 0.8 add_select_fusion.2
  24.5 0.6 copy-done.1
  25.1 0.3 iota_compare_fusion.1
  25.4 0.9 fusion.35
  26.3 0.9 collective-permute-done.4
  27.3 1.7 %concatenate.12 = bf16[18,6912]{1,0:T(8,128)(2,1)S(1)} concatenate(bf16[3,6912]{1,0:T(4,128)(2,1)} %param.6, bf16[3,6912]{1,0:T(4,128)(2,1)S(1)} %collective-permute-done, bf16[3,6912]{1,0:T(4,128)(2,1)S(1)} %collective-permute-done.1, bf16[3,6912]{1,0:T(4,128)(2,1)S(1)} %collective-permute-done.2, bf16[3,6912]{1,0:T(4,128)(2,1)S(1)} %collective-permute-done.3, ...), dimensions={0} | concatenate | bytes 497664 | tf_op jit(solution)/shard_map/concatenate | solution.py:57
  29.0 1.2 fusion.8
  30.2 0.1 reshape.197
  30.3 5.0 %convolution_bitcast_fusion.1 = f32[512,18]{0,1:T(8,128)S(1)} fusion(bf16[18,6912]{1,0:T(8,128)(2,1)S(1)} %concatenate.12, bf16[512,6912]{1,0:T(8,128)(2,1)} %param.9), kind=kOutput, calls=%fused_computation.12 | convolution fusion | flops 127401984 | bytes 7363584 | tf_op jit(solution)/shard_map/dot_general | solution.py:89
  35.3 0.2 copy.36
  35.4 0.2 reshape.196
  35.6 0.2 reshape.198
  35.8 0.1 copy.37
  35.9 1.4 broadcast_select_fusion
  37.4 4.9 %fusion.26 = f32[128,1296]{0,1:T(8,128)S(1)} fusion(bf16[6912,1296]{0,1:T(8,128)(2,1)S(1)} %bitcast.86, s32[6912]{0:T(1024)S(1)} %get-tuple-element.2), kind=kOutput, calls=%fused_computation.74 | convolution fusion | flops 2294120448 | bytes 18607104 | tf_op jit(solution)/shard_map/dot_general | solution.py:80
  42.3 1.0 fusion.27
  43.3 1.8 %copy.38 = f32[128,1,1369]{2,1,0:T(1,128)} copy(f32[128,1,1369]{0,2,1:T(8,128)S(1)} %maximum_bitcast_fusion) | data formatting | bytes 1401856 | tf_op jit(solution)/shard_map/all_to_all | solution.py:104
  45.1 20.6 %all-to-all-start = ((f32[128,1,1369]{2,1,0:T(1,128)}), f32[128,1,1369]{2,1,0:T(1,128)S(1)}, u32[]{:S(2)}, u32[]{:S(2)}) async-start(f32[128,1,1369]{2,1,0:T(1,128)} %copy.38), calls=%async_computation | async-start | bytes 1441792 | tf_op jit(solution)/shard_map/all_to_all | solution.py:104
  65.8 1.4 iota_compare_fusion
  67.2 35.5 %all-to-all-done = f32[128,1,1369]{2,1,0:T(1,128)S(1)} async-done(((f32[128,1,1369]{2,1,0:T(1,128)}), f32[128,1,1369]{2,1,0:T(1,128)S(1)}, u32[]{:S(2)}, u32[]{:S(2)}) %all-to-all-start) | async-done | bytes 700960 | tf_op jit(solution)/shard_map/all_to_all | solution.py:104
  102.7 1.0 copy.39
  103.7 0.1 copy.40
  103.9 0.1 reshape.200
  104.0 0.1 copy.41
  104.1 0.6 fusion.47
  104.7 0.6 convolution_multiply_fusion.1
  105.4 0.7 fusion.20
  106.0 0.6 convolution_bitcast_fusion
  106.7 0.2 reshape.203
  106.8 0.1 reshape_reshape.3
  106.9 0.1 slice_reduce_fusion
  107.1 0.4 copy.43
  107.4 0.8 reshape.204
  108.2 0.9 fusion.87
  109.1 0.1 reshape.223
  109.2 0.1 copy.42
  109.5 0.2 maximum_bitcast_fusion.1
  109.7 0.8 copy.44
  110.5 6.7 %all-to-all-start.1 = ((f32[128,1,343]{2,1,0:T(1,128)}), f32[128,1,343]{2,1,0:T(1,128)S(1)}, u32[]{:S(2)}, u32[]{:S(2)}) async-start(f32[128,1,343]{2,1,0:T(1,128)} %copy.44), calls=%async_computation.1 | async-start | bytes 393216 | tf_op jit(solution)/shard_map/all_to_all | solution.py:130
  117.2 0.2 fusion.49
  117.5 0.1 copy.49
  117.7 0.1 broadcast_in_dim.84
  117.8 19.2 %all-to-all-done.1 = f32[128,1,343]{2,1,0:T(1,128)S(1)} async-done(((f32[128,1,343]{2,1,0:T(1,128)}), f32[128,1,343]{2,1,0:T(1,128)S(1)}, u32[]{:S(2)}, u32[]{:S(2)}) %all-to-all-start.1) | async-done | bytes 175648 | tf_op jit(solution)/shard_map/all_to_all | solution.py:130
  137.0 0.1 copy.45
  137.2 0.1 slice_reduce_fusion.1
  137.3 0.1 copy.48
  137.4 0.2 reshape.206
  137.6 0.9 div.123
  138.5 0.2 div.129
  138.8 1.3 fusion.6
  140.0 0.1 div.128
  140.1 1.7 %fusion.2 = bf16[512,18]{1,0:T(8,128)(2,1)S(1)} fusion(f32[64,8,8]{2,1,0:T(8,128)S(1)} %copy.49, f32[64,8,18]{2,1,0:T(8,128)} %div.123), kind=kOutput, calls=%fused_computation.11 | convolution fusion | flops 893952 | bytes 71680 | tf_op jit(solution)/shard_map/amn,anb->amb/dot_general | solution.py:152
  141.8 0.3 fusion.3
  142.1 0.1 reshape.207
  142.2 0.6 gather_fusion
  142.8 0.1 gather.7
  142.9 6.7 %select_reduce_fusion = f32[3,6912]{1,0:T(4,128)S(1)} fusion(f32[3,128,72]{1,2,0:T(8,128)} %bitcast.101, pred[128,6912]{1,0:T(8,128)(4,1)} %iota_compare_fusion, s32[6912]{0:T(1024)} %copy-done.1), kind=kOutput, calls=%fused_computation.2 | convolution fusion | flops 2299021056 | bytes 1105920 | tf_op jit(solution)/shard_map/dot_general | solution.py:139
  149.6 2.5 %fusion = f32[3,6912]{1,0:T(4,128)} fusion(bf16[512,6912]{1,0:T(8,128)(2,1)S(1)} %bitcast.85, bf16[512,18]{1,0:T(8,128)(2,1)S(1)} %fusion.2, f32[3,6912]{1,0:T(4,128)S(1)} %select_reduce_fusion, bf16[3,6912]{1,0:T(4,128)(2,1)} %param.6, f32[6912]{0:T(1024)} %copy-done), kind=kOutput, calls=%fused_computation.4 | convolution fusion | flops 21337344 | bytes 7331328 | tf_op jit(solution)/shard_map/dot_general | solution.py:156
  152.1 0.6 broadcast_select_fusion.1
  (36 shorter events, 0.5 us)
Async XLA Ops:
  0.6 25.7 %collective-permute-start = (bf16[3,6912]{1,0:T(4,128)(2,1)}, bf16[3,6912]{1,0:T(4,128)(2,1)S(1)}, u32[]{:S(2)}, u32[]{:S(2)}) collective-permute-start(bf16[3,6912]{1,0:T(4,128)(2,1)} %param.6), channel_id=1, source_target_pairs={{0,128},{128,256},{256,384},{384,512},{512,640},{640,0},{1,129},{1... | collective-permute-start | bytes 124424 | tf_op jit(solution)/shard_map/ppermute | solution.py:56
  4.6 21.7 %collective-permute-start.1 = (bf16[3,6912]{1,0:T(4,128)(2,1)}, bf16[3,6912]{1,0:T(4,128)(2,1)S(1)}, u32[]{:S(2)}, u32[]{:S(2)}) collective-permute-start(bf16[3,6912]{1,0:T(4,128)(2,1)} %param.6), channel_id=1, source_target_pairs={{0,256},{128,384},{256,512},{384,640},{512,0},{640,128},{1,257},{1... | collective-permute-start | bytes 124424 | tf_op jit(solution)/shard_map/ppermute | solution.py:56
  11.7 14.7 %collective-permute-start.2 = (bf16[3,6912]{1,0:T(4,128)(2,1)}, bf16[3,6912]{1,0:T(4,128)(2,1)S(1)}, u32[]{:S(2)}, u32[]{:S(2)}) collective-permute-start(bf16[3,6912]{1,0:T(4,128)(2,1)} %param.6), channel_id=1, source_target_pairs={{0,384},{128,512},{256,640},{384,0},{512,128},{640,256},{1,385},{1... | collective-permute-start | bytes 124424 | tf_op jit(solution)/shard_map/ppermute | solution.py:56
  15.4 10.9 %collective-permute-start.3 = (bf16[3,6912]{1,0:T(4,128)(2,1)}, bf16[3,6912]{1,0:T(4,128)(2,1)S(1)}, u32[]{:S(2)}, u32[]{:S(2)}) collective-permute-start(bf16[3,6912]{1,0:T(4,128)(2,1)} %param.6), channel_id=1, source_target_pairs={{0,512},{128,640},{256,0},{384,128},{512,256},{640,384},{1,513},{1... | collective-permute-start | bytes 124424 | tf_op jit(solution)/shard_map/ppermute | solution.py:56
  21.8 5.5 %collective-permute-start.4 = (bf16[3,6912]{1,0:T(4,128)(2,1)}, bf16[3,6912]{1,0:T(4,128)(2,1)S(1)}, u32[]{:S(2)}, u32[]{:S(2)}) collective-permute-start(bf16[3,6912]{1,0:T(4,128)(2,1)} %param.6), channel_id=1, source_target_pairs={{0,640},{128,0},{256,128},{384,256},{512,384},{640,512},{1,641},{1... | collective-permute-start | bytes 124424 | tf_op jit(solution)/shard_map/ppermute | solution.py:56
  24.5 0.6 copy-start.1
  26.3 4.0 %copy-start = (f32[6912]{0:T(1024)}, f32[6912]{0:T(1024)S(1)}, u32[]{:S(2)}) copy-start(f32[6912]{0:T(1024)S(1)} %fusion.35) | copy-start | bytes 82948
  37.3 28.4 %copy-start.3 = (f32[4,8,8]{2,1,0:T(8,128)S(1)}, f32[4,8,8]{2,1,0:T(8,128)}, u32[]{:S(2)}) copy-start(f32[4,8,8]{2,1,0:T(8,128)} %param.11) | copy-start | bytes 3076
  42.3 62.4 %copy-start.2 = (f32[1,128,128]{2,1,0:T(8,128)S(1)}, f32[1,128,128]{2,1,0:T(8,128)}, u32[]{:S(2)}) copy-start(f32[1,128,128]{2,1,0:T(8,128)} %param.8) | copy-start | bytes 196612
  45.1 72.1 %copy-start.4 = (s32[64]{0:T(128)S(1)}, s32[64]{0:T(128)}, u32[]{:S(2)}) copy-start(s32[64]{0:T(128)} %param.10) | copy-start | bytes 772
  45.1 57.6 %all-to-all-start = ((f32[128,1,1369]{2,1,0:T(1,128)}), f32[128,1,1369]{2,1,0:T(1,128)S(1)}, u32[]{:S(2)}, u32[]{:S(2)}) async-start(f32[128,1,1369]{2,1,0:T(1,128)} %copy.38), calls=%async_computation | async-start | bytes 1441792 | tf_op jit(solution)/shard_map/all_to_all | solution.py:104
  110.5 26.5 %all-to-all-start.1 = ((f32[128,1,343]{2,1,0:T(1,128)}), f32[128,1,343]{2,1,0:T(1,128)S(1)}, u32[]{:S(2)}, u32[]{:S(2)}) async-start(f32[128,1,343]{2,1,0:T(1,128)} %copy.44), calls=%async_computation.1 | async-start | bytes 393216 | tf_op jit(solution)/shard_map/all_to_all | solution.py:130
  140.1 9.5 %slice-start = ((s8[7077888]{0:T(1024)(128)(4,1)}), s8[2883584]{0:T(1024)(128)(4,1)S(1)}, s32[]{:S(2)}) async-start(s8[7077888]{0:T(1024)(128)(4,1)} %bitcast.84), calls=%async_computation.2 | async-start | bytes 5767168
  142.9 6.7 %slice-start.1 = ((s8[7077888]{0:T(1024)(128)(4,1)}), s8[4194304]{0:T(1024)(128)(4,1)S(1)}, s32[]{:S(2)}) async-start(s8[7077888]{0:T(1024)(128)(4,1)} %bitcast.84), calls=%async_computation.3 | async-start | bytes 8388608

commit v5 on v4

--- a/solution.py
+++ b/solution.py
@@ -51,10 +51,23 @@
 
 def gathered_bands(states, axis):
     n = lax.axis_size(axis)
-    blocks = [states]
-    for k in range(1, n):
-        blocks.append(lax.ppermute(states, axis, [(i, (i + k) % n) for i in range(n)]))
-    return jnp.concatenate(blocks, axis=0)
+    copies = jnp.broadcast_to(states[None], (n,) + states.shape)
+    every = lax.all_to_all(copies, axis, 0, 0, tiled=True)
+    return every.reshape(n * states.shape[0], states.shape[1])
+
+
+def split3(x):
+    hi = x.astype(jnp.bfloat16)
+    rest = x - hi.astype(jnp.float32)
+    mid = rest.astype(jnp.bfloat16)
+    lo = (rest - mid.astype(jnp.float32)).astype(jnp.bfloat16)
+    return hi, mid, lo
+
+
+def exact_select(x, onehot):
+    hi, mid, lo = split3(x)
+    dot = lambda a: jnp.dot(a, onehot, preferred_element_type=jnp.float32)
+    return (dot(hi) + dot(mid)) + dot(lo)
 
 
 def local(states, slot_map, potential, projectors, species, coupling):
@@ -87,8 +100,8 @@
     columns = jnp.dot(z_table.T, dense, precision=highest, preferred_element_type=jnp.float32)
     energies = kinetic(slot_map, owner * stick_count, stick_count, length, side)
     partial_corr = lax.dot_general(
-        projectors, every, (((1,), (1,)), ((), ())), preferred_element_type=jnp.float32
-    )
+        every, projectors, (((1,), (1,)), ((), ())), preferred_element_type=jnp.float32
+    ).T
     partial_kin = lax.dot_general(
         energies[None, :] * wide,
         every.astype(jnp.float32),
@@ -104,7 +117,8 @@
     got = lax.all_to_all(sent, PW, 0, 0, tiled=True)
     piece = got[:, : planes * total * stick_count].reshape(npw, total, stick_count)
     owned = jnp.sum(got[:, planes * total * stick_count :], axis=0)
-    grid = jnp.transpose(piece[:, :bands, :], (1, 0, 2)).reshape(bands, planes, side, side)
+    mine = lax.dynamic_slice_in_dim(piece, group * bands, bands, axis=1)
+    grid = jnp.transpose(mine, (1, 0, 2)).reshape(bands, planes, side, side)
     half = jnp.einsum("bzjk,jx->bzxk", grid, side_table, precision=highest)
     real_space = jnp.einsum("bzxk,ky->bzxy", half, side_table, precision=highest)
     weighted = real_space * potential[None]
@@ -135,14 +149,11 @@
     reduced = ret[:, bands * stick_count + bands * total :].reshape(-1)
     correlations = reduced[: nproj * total].reshape(nproj, total) / math.sqrt(NG)
     gram_kin = reduced[nproj * total : nproj * total + bands * total].reshape(bands, total)
-    spectral = jnp.einsum("zbs,kz->bks", returned, z_table, precision=highest)
-    picked = jnp.dot(
-        spectral.reshape(bands * length, stick_count),
-        on_stick.T.astype(jnp.float32),
-        precision=highest,
-        preferred_element_type=jnp.float32,
-    ).reshape(bands, length, -1)
-    local_term = jnp.sum(jnp.where(on_plane[None], picked, 0.0), axis=1)
+    spectral = jnp.einsum("zbs,kz->bsk", returned, z_table, precision=highest)
+    picked = exact_select(
+        spectral.reshape(bands * stick_count, length), on_plane.astype(jnp.bfloat16)
+    ).reshape(bands, stick_count, -1)
+    local_term = jnp.sum(jnp.where(on_stick.T[None], picked, 0.0), axis=1)
     atoms = species.shape[0]
     per_atom = coupling.shape[1]
     kinds = coupling.shape[0]
@@ -154,19 +165,17 @@
     )
     weights = weights.reshape(atoms * per_atom, total).astype(jnp.bfloat16)
     nonlocal_term = lax.dot_general(
-        weights[:, :bands], projectors, (((0,), (0,)), ((), ())), preferred_element_type=jnp.float32
+        lax.dynamic_slice_in_dim(weights, group * bands, bands, axis=1), projectors, (((0,), (0,)), ((), ())), preferred_element_type=jnp.float32
     ) / math.sqrt(atoms * per_atom)
     applied = energies[None, :] * wide + local_term + nonlocal_term
     cross = lax.dot_general(
-        correlations[:, :bands],
+        lax.dynamic_slice_in_dim(correlations, group * bands, bands, axis=1),
         weights.astype(jnp.float32),
         (((0,), (0,)), ((), ())),
         precision=highest,
         preferred_element_type=jnp.float32,
     ) / (math.sqrt(atoms * per_atom) * math.sqrt(NG))
-    rotated = ((gram_kin + gram_local) / float(NG) + cross).reshape(bands, ngroup, bands)
-    order = (group - jnp.arange(ngroup)) % ngroup
-    subspace = jnp.take(rotated, order, axis=1).reshape(bands, total)
+    subspace = (gram_kin + gram_local) / float(NG) + cross
     return (applied, subspace)
 
 

time: 153 us -> 142 us (0.928)
  the two profiles are of different devices: /device:TPU:65 before, /device:TPU:1 now
where the time goes in v5:
time: 142 us; the launch traced here: 141 us
  waiting for transfers between devices  61.2 us (43%)
  starting transfers between devices  42.2 us (30%)
  matrix products  22.6 us (16%)
  local copies, waits for them, and re-layouts  9.42 us (7%)
  other arithmetic  4.75 us (3%)
    all_to_all x1, waiting for transfers between devices, local(): got = lax.all_to_all(sent, PW, 0, 0, tiled=True)  30.5 us
    all_to_all x1, starting transfers between devices, local(): got = lax.all_to_all(sent, PW, 0, 0, tiled=True)  20.3 us
    all_to_all x1, waiting for transfers between devices, local(): ret = lax.all_to_all(ret_sent, PW, 0, 0, tiled=True)  17.7 us
    all_to_all x1, waiting for transfers between devices, gathered_bands(): every = lax.all_to_all(copies, axis, 0, 0, tiled=True)  13 us
    all_to_all x1, starting transfers between devices, gathered_bands(): every = lax.all_to_all(copies, axis, 0, 0, tiled=True)  12.6 us
    all_to_all x1, starting transfers between devices, local(): ret = lax.all_to_all(ret_sent, PW, 0, 0, tiled=True)  9.2 us
    dot_general x1, matrix products, local(): lax.dot_general(every, projectors, (((1,), (1,)), ((), ())), preferred_el...  4.98 us
    dot_general x1, matrix products, local(): jnp.dot(on_plane.astype(jnp.bfloat16), spread.reshape(count, total * stic...  4.93 us
  transfers between devices with their start and end apart: 3, of which 3 were waited for; matrix products, arithmetic and copies ran while one was open for 2% of the time, Pallas kernels for 0%

profile of v5, /device:TPU:1, one launch (start us, length us, event | category | flops | bytes accessed | tf_op | source)
XLA Modules:
  0.0 141.2 jit_solution(14433917634575848012)
XLA Ops:
  0.6 1.6 %broadcast_in_dim.38 = bf16[6,3,6912]{2,1,0:T(4,128)(2,1)} broadcast(bf16[3,6912]{1,0:T(4,128)(2,1)} %param.6), dimensions={1,2} | broadcast | bytes 290304 | tf_op jit(solution)/shard_map/broadcast_in_dim | solution.py:54
  2.3 12.6 %all-to-all-start = ((bf16[6,3,6912]{2,1,0:T(4,128)(2,1)}), bf16[6,3,6912]{2,1,0:T(4,128)(2,1)S(1)}, u32[]{:S(2)}, u32[]{:S(2)}) async-start(bf16[6,3,6912]{2,1,0:T(4,128)(2,1)} %broadcast_in_dim.38), calls=%async_computation | async-start | bytes 663552 | tf_op jit(solution)/shard_map/all_to_all | solution.py:55
  14.9 0.8 add_select_fusion.2
  15.7 0.3 iota_compare_fusion.5
  16.0 0.9 fusion.41
  16.9 13.0 %all-to-all-done = bf16[6,3,6912]{2,1,0:T(4,128)(2,1)S(1)} async-done(((bf16[6,3,6912]{2,1,0:T(4,128)(2,1)}), bf16[6,3,6912]{2,1,0:T(4,128)(2,1)S(1)}, u32[]{:S(2)}, u32[]{:S(2)}) %all-to-all-start) | async-done | bytes 248864 | tf_op jit(solution)/shard_map/all_to_all | solution.py:55
  29.9 0.2 reshape.155
  30.1 1.2 fusion.12
  31.3 0.1 reshape.157
  31.4 5.0 %fusion.94 = f32[512,18]{1,0:T(8,128)S(1)} fusion(bf16[512,6912]{1,0:T(8,128)(2,1)} %param.9, bf16[18,6912]{1,0:T(8,128)(2,1)S(1)} %reshape.155), kind=kOutput, calls=%fused_computation.161 | convolution fusion | flops 127401984 | bytes 7363584 | tf_op jit(solution)/shard_map/dot_general | solution.py:102
  36.4 0.2 reshape.156
  36.6 0.2 reshape.158
  36.8 0.1 copy.32
  36.9 1.4 broadcast_select_fusion
  38.3 4.9 %fusion.2 = f32[128,1296]{0,1:T(8,128)S(1)} fusion(bf16[6912,1296]{0,1:T(8,128)(2,1)S(1)} %bitcast.78, s32[6912]{0:T(1024)S(1)} %get-tuple-element.2), kind=kOutput, calls=%fused_computation.8 | convolution fusion | flops 2294120448 | bytes 18607104 | tf_op jit(solution)/shard_map/dot_general | solution.py:93
  43.2 0.0 copy-start.1
  43.2 1.0 fusion.33
  44.2 1.8 %copy.33 = f32[128,1,1369]{2,1,0:T(1,128)} copy(f32[128,1,1369]{0,2,1:T(8,128)S(1)} %maximum_bitcast_fusion) | data formatting | bytes 1401856 | tf_op jit(solution)/shard_map/all_to_all | solution.py:117
  46.0 20.3 %all-to-all-start.1 = ((f32[128,1,1369]{2,1,0:T(1,128)}), f32[128,1,1369]{2,1,0:T(1,128)S(1)}, u32[]{:S(2)}, u32[]{:S(2)}) async-start(f32[128,1,1369]{2,1,0:T(1,128)} %copy.33), calls=%async_computation.1 | async-start | bytes 1441792 | tf_op jit(solution)/shard_map/all_to_all | solution.py:117
  66.4 30.5 %all-to-all-done.1 = f32[128,1,1369]{2,1,0:T(1,128)S(1)} async-done(((f32[128,1,1369]{2,1,0:T(1,128)}), f32[128,1,1369]{2,1,0:T(1,128)S(1)}, u32[]{:S(2)}, u32[]{:S(2)}) %all-to-all-start.1) | async-done | bytes 700960 | tf_op jit(solution)/shard_map/all_to_all | solution.py:117
  96.8 1.0 copy.34
  97.8 0.0 copy-start.2
  97.9 0.1 copy.35
  98.0 0.1 reshape.160
  98.2 0.1 copy.36
  98.3 0.6 fusion.53
  98.9 0.6 convolution_multiply_fusion.1
  99.5 0.7 fusion.27
  100.2 0.6 convolution_bitcast_fusion
  100.8 0.2 reshape.163
  101.0 0.1 reshape_reshape.3
  101.1 0.1 slice_reduce_fusion
  101.2 0.4 copy.38
  101.6 0.8 reshape.164
  102.4 0.9 fusion.95
  103.3 0.1 reshape.172
  103.4 0.1 copy.37
  103.5 0.1 pad.6.clone
  103.6 0.1 pad.7.clone
  103.7 0.2 maximum_bitcast_fusion.1
  103.8 0.8 copy.39
  104.6 9.2 %all-to-all-start.2 = ((f32[128,1,343]{2,1,0:T(1,128)}), f32[128,1,343]{2,1,0:T(1,128)S(1)}, u32[]{:S(2)}, u32[]{:S(2)}) async-start(f32[128,1,343]{2,1,0:T(1,128)} %copy.39), calls=%async_computation.2 | async-start | bytes 393216 | tf_op jit(solution)/shard_map/all_to_all | solution.py:144
  113.8 0.3 iota_compare_fusion.6
  114.1 0.1 copy.41
  114.2 0.2 fusion.55
  114.4 0.1 copy.44
  114.6 17.7 %all-to-all-done.2 = f32[128,1,343]{2,1,0:T(1,128)S(1)} async-done(((f32[128,1,343]{2,1,0:T(1,128)}), f32[128,1,343]{2,1,0:T(1,128)S(1)}, u32[]{:S(2)}, u32[]{:S(2)}) %all-to-all-start.2) | async-done | bytes 175648 | tf_op jit(solution)/shard_map/all_to_all | solution.py:144
  132.3 0.1 copy.40
  132.5 0.1 slice_reduce_fusion.1
  132.6 0.1 copy.43
  132.7 0.2 reshape.167
  132.9 0.2 div.123
  133.1 0.2 div.129
  133.4 0.6 fusion.11
  134.0 0.1 div.128
  134.1 1.0 fusion.1
  135.0 0.0 slice-start
  135.1 1.0 convolution_add_fusion.1
  136.0 0.0 slice-start.1
  136.1 1.0 convolution_add_fusion
  137.1 0.6 fusion.7
  137.7 0.7 select_reduce_fusion
  138.4 1.8 %fusion = f32[3,6912]{1,0:T(4,128)} fusion(bf16[512,6912]{1,0:T(8,128)(2,1)S(1)} %bitcast.80, bf16[512,18]{1,0:T(8,128)(2,1)S(1)} %fusion.7, s32[]{:T(128)S(6)} %select_n.144, f32[3,6912]{1,0:T(4,128)S(1)} %select_reduce_fusion, bf16[3,6912]{1,0:T(4,128)(2,1)S(1)} %copy-done, f32[6912]{0:T(1024)S(1)} %fusion.41), kind=kOutput, calls=%fused_computation.4 | convolution fusion | flops 21337344 | bytes 7331332 | tf_op jit(solution)/shard_map/dot_general | solution.py:167
  140.2 1.0 fusion.8
  (18 shorter events, 0.2 us)
Async XLA Ops:
  2.3 27.6 %all-to-all-start = ((bf16[6,3,6912]{2,1,0:T(4,128)(2,1)}), bf16[6,3,6912]{2,1,0:T(4,128)(2,1)S(1)}, u32[]{:S(2)}, u32[]{:S(2)}) async-start(bf16[6,3,6912]{2,1,0:T(4,128)(2,1)} %broadcast_in_dim.38), calls=%async_computation | async-start | bytes 663552 | tf_op jit(solution)/shard_map/all_to_all | solution.py:55
  43.2 55.6 %copy-start.1 = (f32[1,128,128]{2,1,0:T(8,128)S(1)}, f32[1,128,128]{2,1,0:T(8,128)}, u32[]{:S(2)}) copy-start(f32[1,128,128]{2,1,0:T(8,128)} %param.8) | copy-start | bytes 196612
  46.0 50.8 %all-to-all-start.1 = ((f32[128,1,1369]{2,1,0:T(1,128)}), f32[128,1,1369]{2,1,0:T(1,128)S(1)}, u32[]{:S(2)}, u32[]{:S(2)}) async-start(f32[128,1,1369]{2,1,0:T(1,128)} %copy.33), calls=%async_computation.1 | async-start | bytes 1441792 | tf_op jit(solution)/shard_map/all_to_all | solution.py:117
  97.8 16.3 %copy-start.2 = (f32[4,8,8]{2,1,0:T(8,128)S(1)}, f32[4,8,8]{2,1,0:T(8,128)}, u32[]{:S(2)}) copy-start(f32[4,8,8]{2,1,0:T(8,128)} %param.11) | copy-start | bytes 3076
  97.8 16.4 %copy-start.3 = (s32[64]{0:T(128)S(1)}, s32[64]{0:T(128)}, u32[]{:S(2)}) copy-start(s32[64]{0:T(128)} %param.10) | copy-start | bytes 772
  104.6 27.7 %all-to-all-start.2 = ((f32[128,1,343]{2,1,0:T(1,128)}), f32[128,1,343]{2,1,0:T(1,128)S(1)}, u32[]{:S(2)}, u32[]{:S(2)}) async-start(f32[128,1,343]{2,1,0:T(1,128)} %copy.39), calls=%async_computation.2 | async-start | bytes 393216 | tf_op jit(solution)/shard_map/all_to_all | solution.py:144
  135.0 3.3 %slice-start = ((s8[7077888]{0:T(1024)(128)(4,1)}), s8[4194304]{0:T(1024)(128)(4,1)S(1)}, s32[]{:S(2)}) async-start(s8[7077888]{0:T(1024)(128)(4,1)} %bitcast.79), calls=%async_computation.3 | async-start | bytes 8388608
  136.0 2.3 %slice-start.1 = ((s8[7077888]{0:T(1024)(128)(4,1)}), s8[2883584]{0:T(1024)(128)(4,1)S(1)}, s32[]{:S(2)}) async-start(s8[7077888]{0:T(1024)(128)(4,1)} %bitcast.79), calls=%async_computation.4 | async-start | bytes 5767168
  137.1 1.3 copy-start

commit v6 on v5

--- a/solution.py
+++ b/solution.py
@@ -57,11 +57,11 @@
 
 
 def split3(x):
-    hi = x.astype(jnp.bfloat16)
-    rest = x - hi.astype(jnp.float32)
-    mid = rest.astype(jnp.bfloat16)
-    lo = (rest - mid.astype(jnp.float32)).astype(jnp.bfloat16)
-    return hi, mid, lo
+    hi = lax.reduce_precision(x, exponent_bits=8, mantissa_bits=7)
+    rest = x - hi
+    mid = lax.reduce_precision(rest, exponent_bits=8, mantissa_bits=7)
+    lo = rest - mid
+    return hi.astype(jnp.bfloat16), mid.astype(jnp.bfloat16), lo.astype(jnp.bfloat16)
 
 
 def exact_select(x, onehot):

time: 142 us -> 142 us (level)
  no operation moved by 1% of the time
where the time goes in v6:
time: 142 us; the launch traced here: 141 us
  waiting for transfers between devices  61.2 us (43%)
  starting transfers between devices  42.2 us (30%)
  matrix products  22.6 us (16%)
  local copies, waits for them, and re-layouts  9.42 us (7%)
  other arithmetic  4.75 us (3%)
    all_to_all x1, waiting for transfers between devices, local(): got = lax.all_to_all(sent, PW, 0, 0, tiled=True)  30.5 us
    all_to_all x1, starting transfers between devices, local(): got = lax.all_to_all(sent, PW, 0, 0, tiled=True)  20.3 us
    all_to_all x1, waiting for transfers between devices, local(): ret = lax.all_to_all(ret_sent, PW, 0, 0, tiled=True)  17.7 us
    all_to_all x1, waiting for transfers between devices, gathered_bands(): every = lax.all_to_all(copies, axis, 0, 0, tiled=True)  13 us
    all_to_all x1, starting transfers between devices, gathered_bands(): every = lax.all_to_all(copies, axis, 0, 0, tiled=True)  12.6 us
    all_to_all x1, starting transfers between devices, local(): ret = lax.all_to_all(ret_sent, PW, 0, 0, tiled=True)  9.2 us
    dot_general x1, matrix products, local(): lax.dot_general(every, projectors, (((1,), (1,)), ((), ())), preferred_el...  4.98 us
    dot_general x1, matrix products, local(): jnp.dot(on_plane.astype(jnp.bfloat16), spread.reshape(count, total * stic...  4.93 us
  transfers between devices with their start and end apart: 3, of which 3 were waited for; matrix products, arithmetic and copies ran while one was open for 2% of the time, Pallas kernels for 0%

profile of v6, /device:TPU:1, one launch (start us, length us, event | category | flops | bytes accessed | tf_op | source)
XLA Modules:
  0.0 141.2 jit_solution(12422417528538531069)
XLA Ops:
  0.6 1.6 %broadcast_in_dim.38 = bf16[6,3,6912]{2,1,0:T(4,128)(2,1)} broadcast(bf16[3,6912]{1,0:T(4,128)(2,1)} %param.6), dimensions={1,2} | broadcast | bytes 290304 | tf_op jit(solution)/shard_map/broadcast_in_dim | solution.py:54
  2.3 12.6 %all-to-all-start = ((bf16[6,3,6912]{2,1,0:T(4,128)(2,1)}), bf16[6,3,6912]{2,1,0:T(4,128)(2,1)S(1)}, u32[]{:S(2)}, u32[]{:S(2)}) async-start(bf16[6,3,6912]{2,1,0:T(4,128)(2,1)} %broadcast_in_dim.38), calls=%async_computation | async-start | bytes 663552 | tf_op jit(solution)/shard_map/all_to_all | solution.py:55
  14.9 0.8 add_select_fusion.2
  15.7 0.3 iota_compare_fusion.5
  16.0 0.9 fusion.40
  16.9 13.0 %all-to-all-done = bf16[6,3,6912]{2,1,0:T(4,128)(2,1)S(1)} async-done(((bf16[6,3,6912]{2,1,0:T(4,128)(2,1)}), bf16[6,3,6912]{2,1,0:T(4,128)(2,1)S(1)}, u32[]{:S(2)}, u32[]{:S(2)}) %all-to-all-start) | async-done | bytes 248864 | tf_op jit(solution)/shard_map/all_to_all | solution.py:55
  29.9 0.2 reshape.155
  30.1 1.2 fusion.13
  31.3 0.1 reshape.157
  31.4 5.0 %fusion.93 = f32[512,18]{1,0:T(8,128)S(1)} fusion(bf16[512,6912]{1,0:T(8,128)(2,1)} %param.9, bf16[18,6912]{1,0:T(8,128)(2,1)S(1)} %reshape.155), kind=kOutput, calls=%fused_computation.162 | convolution fusion | flops 127401984 | bytes 7363584 | tf_op jit(solution)/shard_map/dot_general | solution.py:102
  36.4 0.2 reshape.156
  36.6 0.2 reshape.158
  36.8 0.1 copy.32
  36.9 1.4 broadcast_select_fusion
  38.3 4.9 %fusion.2 = f32[128,1296]{0,1:T(8,128)S(1)} fusion(bf16[6912,1296]{0,1:T(8,128)(2,1)S(1)} %bitcast.78, s32[6912]{0:T(1024)S(1)} %get-tuple-element.2), kind=kOutput, calls=%fused_computation.8 | convolution fusion | flops 2294120448 | bytes 18607104 | tf_op jit(solution)/shard_map/dot_general | solution.py:93
  43.2 0.0 copy-start.1
  43.2 1.0 fusion.32
  44.2 1.8 %copy.33 = f32[128,1,1369]{2,1,0:T(1,128)} copy(f32[128,1,1369]{0,2,1:T(8,128)S(1)} %maximum_bitcast_fusion) | data formatting | bytes 1401856 | tf_op jit(solution)/shard_map/all_to_all | solution.py:117
  46.0 20.3 %all-to-all-start.1 = ((f32[128,1,1369]{2,1,0:T(1,128)}), f32[128,1,1369]{2,1,0:T(1,128)S(1)}, u32[]{:S(2)}, u32[]{:S(2)}) async-start(f32[128,1,1369]{2,1,0:T(1,128)} %copy.33), calls=%async_computation.1 | async-start | bytes 1441792 | tf_op jit(solution)/shard_map/all_to_all | solution.py:117
  66.4 30.5 %all-to-all-done.1 = f32[128,1,1369]{2,1,0:T(1,128)S(1)} async-done(((f32[128,1,1369]{2,1,0:T(1,128)}), f32[128,1,1369]{2,1,0:T(1,128)S(1)}, u32[]{:S(2)}, u32[]{:S(2)}) %all-to-all-start.1) | async-done | bytes 700960 | tf_op jit(solution)/shard_map/all_to_all | solution.py:117
  96.8 1.0 copy.34
  97.9 0.1 copy.35
  98.0 0.1 reshape.160
  98.2 0.1 copy.36
  98.3 0.6 fusion.52
  98.9 0.6 convolution_multiply_fusion.1
  99.5 0.7 fusion.26
  100.2 0.6 convolution_bitcast_fusion
  100.8 0.2 reshape.163
  101.0 0.1 reshape_reshape.3
  101.1 0.1 slice_reduce_fusion
  101.2 0.4 copy.38
  101.6 0.8 reshape.164
  102.4 0.9 fusion.94
  103.3 0.1 reshape.172
  103.4 0.1 copy.37
  103.5 0.1 pad.6.clone
  103.6 0.1 pad.7.clone
  103.7 0.2 maximum_bitcast_fusion.1
  103.8 0.8 copy.39
  104.6 9.2 %all-to-all-start.2 = ((f32[128,1,343]{2,1,0:T(1,128)}), f32[128,1,343]{2,1,0:T(1,128)S(1)}, u32[]{:S(2)}, u32[]{:S(2)}) async-start(f32[128,1,343]{2,1,0:T(1,128)} %copy.39), calls=%async_computation.2 | async-start | bytes 393216 | tf_op jit(solution)/shard_map/all_to_all | solution.py:144
  113.8 0.3 iota_compare_fusion.6
  114.1 0.1 copy.41
  114.2 0.2 fusion.54
  114.4 0.1 copy.44
  114.6 17.7 %all-to-all-done.2 = f32[128,1,343]{2,1,0:T(1,128)S(1)} async-done(((f32[128,1,343]{2,1,0:T(1,128)}), f32[128,1,343]{2,1,0:T(1,128)S(1)}, u32[]{:S(2)}, u32[]{:S(2)}) %all-to-all-start.2) | async-done | bytes 175648 | tf_op jit(solution)/shard_map/all_to_all | solution.py:144
  132.3 0.1 copy.40
  132.5 0.1 slice_reduce_fusion.1
  132.6 0.1 copy.43
  132.7 0.2 reshape.167
  132.9 0.2 div.123
  133.1 0.2 div.129
  133.4 0.6 fusion.12
  134.0 0.1 div.128
  134.1 1.0 fusion.1
  135.0 0.0 slice-start
  135.1 1.0 convolution_add_fusion.1
  136.1 0.0 slice-start.1
  136.1 1.0 convolution_add_fusion
  137.1 0.6 fusion.7
  137.7 0.7 select_reduce_fusion
  138.4 0.0 slice-done.1
  138.4 1.8 %fusion = f32[3,6912]{1,0:T(4,128)} fusion(bf16[512,6912]{1,0:T(8,128)(2,1)S(1)} %bitcast.80, bf16[512,18]{1,0:T(8,128)(2,1)S(1)} %fusion.7, s32[]{:T(128)S(6)} %select_n.144, f32[3,6912]{1,0:T(4,128)S(1)} %select_reduce_fusion, bf16[3,6912]{1,0:T(4,128)(2,1)S(1)} %copy-done, f32[6912]{0:T(1024)S(1)} %fusion.40), kind=kOutput, calls=%fused_computation.4 | convolution fusion | flops 21337344 | bytes 7331332 | tf_op jit(solution)/shard_map/dot_general | solution.py:167
  140.2 1.0 fusion.8
  (18 shorter events, 0.2 us)
Async XLA Ops:
  2.3 27.6 %all-to-all-start = ((bf16[6,3,6912]{2,1,0:T(4,128)(2,1)}), bf16[6,3,6912]{2,1,0:T(4,128)(2,1)S(1)}, u32[]{:S(2)}, u32[]{:S(2)}) async-start(bf16[6,3,6912]{2,1,0:T(4,128)(2,1)} %broadcast_in_dim.38), calls=%async_computation | async-start | bytes 663552 | tf_op jit(solution)/shard_map/all_to_all | solution.py:55
  43.2 55.6 %copy-start.1 = (f32[1,128,128]{2,1,0:T(8,128)S(1)}, f32[1,128,128]{2,1,0:T(8,128)}, u32[]{:S(2)}) copy-start(f32[1,128,128]{2,1,0:T(8,128)} %param.8) | copy-start | bytes 196612
  46.0 50.8 %all-to-all-start.1 = ((f32[128,1,1369]{2,1,0:T(1,128)}), f32[128,1,1369]{2,1,0:T(1,128)S(1)}, u32[]{:S(2)}, u32[]{:S(2)}) async-start(f32[128,1,1369]{2,1,0:T(1,128)} %copy.33), calls=%async_computation.1 | async-start | bytes 1441792 | tf_op jit(solution)/shard_map/all_to_all | solution.py:117
  97.8 16.3 %copy-start.2 = (f32[4,8,8]{2,1,0:T(8,128)S(1)}, f32[4,8,8]{2,1,0:T(8,128)}, u32[]{:S(2)}) copy-start(f32[4,8,8]{2,1,0:T(8,128)} %param.11) | copy-start | bytes 3076
  97.8 16.4 %copy-start.3 = (s32[64]{0:T(128)S(1)}, s32[64]{0:T(128)}, u32[]{:S(2)}) copy-start(s32[64]{0:T(128)} %param.10) | copy-start | bytes 772
  104.6 27.7 %all-to-all-start.2 = ((f32[128,1,343]{2,1,0:T(1,128)}), f32[128,1,343]{2,1,0:T(1,128)S(1)}, u32[]{:S(2)}, u32[]{:S(2)}) async-start(f32[128,1,343]{2,1,0:T(1,128)} %copy.39), calls=%async_computation.2 | async-start | bytes 393216 | tf_op jit(solution)/shard_map/all_to_all | solution.py:144
  135.0 3.3 %slice-start = ((s8[7077888]{0:T(1024)(128)(4,1)}), s8[4194304]{0:T(1024)(128)(4,1)S(1)}, s32[]{:S(2)}) async-start(s8[7077888]{0:T(1024)(128)(4,1)} %bitcast.79), calls=%async_computation.3 | async-start | bytes 8388608
  136.1 2.3 %slice-start.1 = ((s8[7077888]{0:T(1024)(128)(4,1)}), s8[2883584]{0:T(1024)(128)(4,1)S(1)}, s32[]{:S(2)}) async-start(s8[7077888]{0:T(1024)(128)(4,1)} %bitcast.79), calls=%async_computation.4 | async-start | bytes 5767168
  137.1 1.3 copy-start

commit v7 on v6

--- a/solution.py
+++ b/solution.py
@@ -62,6 +62,11 @@
     mid = lax.reduce_precision(rest, exponent_bits=8, mantissa_bits=7)
     lo = rest - mid
     return hi.astype(jnp.bfloat16), mid.astype(jnp.bfloat16), lo.astype(jnp.bfloat16)
+
+
+def split2(x):
+    hi = lax.reduce_precision(x, exponent_bits=8, mantissa_bits=7)
+    return hi.astype(jnp.bfloat16), (x - hi).astype(jnp.bfloat16)
 
 
 def exact_select(x, onehot):
@@ -113,11 +118,20 @@
     packed = jnp.concatenate([partial_corr.reshape(-1), partial_kin.reshape(-1)])
     width = -(-packed.shape[0] // npw)
     packed = jnp.pad(packed, (0, width * npw - packed.shape[0])).reshape(npw, width)
-    sent = jnp.concatenate([columns.reshape(npw, planes * total * stick_count), packed], axis=1)
+    columns = columns.reshape(npw, total, stick_count)
+    exact = jnp.concatenate(
+        [lax.dynamic_slice_in_dim(columns, group * bands, bands, axis=1).reshape(npw, -1), packed], axis=1
+    )
+    exact_hi, exact_lo = split2(exact)
+    sent = jnp.concatenate(
+        [exact_hi, exact_lo, columns.reshape(npw, -1).astype(jnp.bfloat16)], axis=1
+    )
     got = lax.all_to_all(sent, PW, 0, 0, tiled=True)
-    piece = got[:, : planes * total * stick_count].reshape(npw, total, stick_count)
-    owned = jnp.sum(got[:, planes * total * stick_count :], axis=0)
-    mine = lax.dynamic_slice_in_dim(piece, group * bands, bands, axis=1)
+    nexact = exact.shape[1]
+    joined = got[:, :nexact].astype(jnp.float32) + got[:, nexact : 2 * nexact].astype(jnp.float32)
+    mine = joined[:, : bands * stick_count].reshape(npw, bands, stick_count)
+    owned = jnp.sum(joined[:, bands * stick_count :], axis=0)
+    piece = got[:, 2 * nexact :].astype(jnp.float32).reshape(npw, total, stick_count)
     grid = jnp.transpose(mine, (1, 0, 2)).reshape(bands, planes, side, side)
     half = jnp.einsum("bzjk,jx->bzxk", grid, side_table, precision=highest)
     real_space = jnp.einsum("bzxk,ky->bzxy", half, side_table, precision=highest)
@@ -125,6 +139,7 @@
     back_half = jnp.einsum("bzxy,ky->bzxk", weighted, side_table, precision=highest)
     back_grid = jnp.einsum("bzxk,jx->bzjk", back_half, side_table, precision=highest)
     back_own = back_grid.reshape(bands, side * side)
+    piece = lax.dynamic_update_slice_in_dim(piece, mine, group * bands, axis=1)
     plane_gram = lax.dot_general(
         back_own,
         jnp.transpose(piece, (1, 0, 2)).reshape(total, side * side),

time: 142 us -> 139 us (0.979)
  waiting for transfers between devices: 61.2 us -> 54.9 us
  local copies, waits for them, and re-layouts: 9.42 us -> 12.3 us
    all_to_all x1, waiting for transfers between devices: 30.5 us -> 24.2 us  [local(): got = lax.all_to_all(sent, PW, 0, 0, tiled=True)]
    unnamed x13 -> x16, local copies, waits for them, and re-layouts: 0.11 us -> 2.48 us
    concatenate x0 -> x1, local copies, waits for them, and re-layouts: none -> 1.65 us  [local(): jnp.concatenate([exact_hi, exact_lo, columns.reshape(npw, -1).astype(jnp....]
where the time goes in v7:
time: 139 us; the launch traced here: 138 us
  waiting for transfers between devices  54.9 us (39%)
  starting transfers between devices  42.1 us (30%)
  matrix products  21.8 us (16%)
  local copies, waits for them, and re-layouts  12.3 us (9%)
  other arithmetic  5.82 us (4%)
    all_to_all x1, waiting for transfers between devices, local(): got = lax.all_to_all(sent, PW, 0, 0, tiled=True)  24.2 us
    all_to_all x1, starting transfers between devices, local(): got = lax.all_to_all(sent, PW, 0, 0, tiled=True)  20.3 us
    all_to_all x1, waiting for transfers between devices, local(): ret = lax.all_to_all(ret_sent, PW, 0, 0, tiled=True)  17.7 us
    all_to_all x1, waiting for transfers between devices, gathered_bands(): every = lax.all_to_all(copies, axis, 0, 0, tiled=True)  13 us
    all_to_all x1, starting transfers between devices, gathered_bands(): every = lax.all_to_all(copies, axis, 0, 0, tiled=True)  12.6 us
    all_to_all x1, starting transfers between devices, local(): ret = lax.all_to_all(ret_sent, PW, 0, 0, tiled=True)  9.12 us
    dot_general x1, matrix products, local(): lax.dot_general(every, projectors, (((1,), (1,)), ((), ())), preferred_el...  4.98 us
    dot_general x1, matrix products, local(): jnp.dot(on_plane.astype(jnp.bfloat16), spread.reshape(count, total * stic...  4.94 us
  transfers between devices with their start and end apart: 3, of which 3 were waited for; matrix products, arithmetic and copies ran while one was open for 2% of the time, Pallas kernels for 0%

profile of v7, /device:TPU:1, one launch (start us, length us, event | category | flops | bytes accessed | tf_op | source)
XLA Modules:
  0.0 138.0 jit_solution(5672642310502986734)
XLA Ops:
  0.6 1.6 %broadcast_in_dim.38 = bf16[6,3,6912]{2,1,0:T(4,128)(2,1)} broadcast(bf16[3,6912]{1,0:T(4,128)(2,1)} %param.6), dimensions={1,2} | broadcast | bytes 290304 | tf_op jit(solution)/shard_map/broadcast_in_dim | solution.py:54
  2.3 12.6 %all-to-all-start = ((bf16[6,3,6912]{2,1,0:T(4,128)(2,1)}), bf16[6,3,6912]{2,1,0:T(4,128)(2,1)S(1)}, u32[]{:S(2)}, u32[]{:S(2)}) async-start(bf16[6,3,6912]{2,1,0:T(4,128)(2,1)} %broadcast_in_dim.38), calls=%async_computation | async-start | bytes 663552 | tf_op jit(solution)/shard_map/all_to_all | solution.py:55
  14.9 0.8 add_select_fusion.2
  15.7 0.3 iota_compare_fusion.5
  16.0 0.9 fusion.41
  16.8 13.0 %all-to-all-done = bf16[6,3,6912]{2,1,0:T(4,128)(2,1)S(1)} async-done(((bf16[6,3,6912]{2,1,0:T(4,128)(2,1)}), bf16[6,3,6912]{2,1,0:T(4,128)(2,1)S(1)}, u32[]{:S(2)}, u32[]{:S(2)}) %all-to-all-start) | async-done | bytes 248864 | tf_op jit(solution)/shard_map/all_to_all | solution.py:55
  29.8 0.2 reshape.167
  30.1 1.4 %broadcast_select_fusion = bf16[6912,18,72]{0,2,1:T(8,128)(2,1)S(1)} fusion(pred[6912,72]{0,1:T(8,128)(4,1)S(1)} %iota_compare_fusion.5, bf16[6912,18]{0,1:T(8,128)(2,1)S(1)} %bitcast.87), kind=kLoop, calls=%fused_computation | loop fusion | flops 8957952 | bytes 18662400 | tf_op jit(solution)/shard_map/jit(_where)/select_n | solution.py:97
  31.5 4.9 %fusion.2 = f32[128,1296]{0,1:T(8,128)S(1)} fusion(bf16[6912,1296]{0,1:T(8,128)(2,1)S(1)} %bitcast.80, s32[6912]{0:T(1024)S(1)} %get-tuple-element.4), kind=kOutput, calls=%fused_computation.8 | convolution fusion | flops 2294120448 | bytes 18607104 | tf_op jit(solution)/shard_map/dot_general | solution.py:98
  36.4 1.0 fusion.94
  37.4 0.4 fusion.14
  37.8 0.1 reshape.171
  37.9 5.0 %fusion.95 = f32[512,18]{1,0:T(8,128)S(1)} fusion(bf16[512,6912]{1,0:T(8,128)(2,1)} %param.9, bf16[18,6912]{1,0:T(8,128)(2,1)S(1)} %reshape.167), kind=kOutput, calls=%fused_computation.168 | convolution fusion | flops 127401984 | bytes 7363584 | tf_op jit(solution)/shard_map/dot_general | solution.py:107
  42.9 0.2 reshape.170
  43.1 0.2 reshape.172
  43.3 0.1 copy.34
  43.4 1.6 %concatenate.14 = bf16[128,1874]{0,1:T(8,128)(2,1)S(1)} concatenate(bf16[128,289]{0,1:T(8,128)(2,1)S(1)} %get-tuple-element.3, bf16[128,289]{0,1:T(8,128)(2,1)S(1)} %get-tuple-element.2, bf16[128,1296]{0,1:T(8,128)(2,1)S(1)} %get-tuple-element.6), dimensions={1} | concatenate | bytes 959488 | tf_op jit(solution)/shard_map/concatenate | solution.py:126
  45.1 0.5 broadcast.192
  45.6 1.0 reduce
  46.6 0.3 copy.50
  46.9 1.4 %reshape.192 = bf16[128,2,937]{2,1,0:T(2,128)(2,1)} reshape(bf16[128,1874]{1,0:T(8,128)(2,1)S(1)} %copy.50) | data formatting | bytes 959488
  48.3 20.3 %all-to-all-start.1 = ((bf16[128,2,937]{2,1,0:T(2,128)(2,1)}), bf16[128,2,937]{2,1,0:T(2,128)(2,1)S(1)}, u32[]{:S(2)}, u32[]{:S(2)}) async-start(bf16[128,2,937]{2,1,0:T(2,128)(2,1)} %reshape.192), calls=%async_computation.1 | async-start | bytes 1048576 | tf_op jit(solution)/shard_map/all_to_all | solution.py:129
  68.6 24.2 %all-to-all-done.1 = bf16[128,2,937]{2,1,0:T(2,128)(2,1)S(1)} async-done(((bf16[128,2,937]{2,1,0:T(2,128)(2,1)}), bf16[128,2,937]{2,1,0:T(2,128)(2,1)S(1)}, u32[]{:S(2)}, u32[]{:S(2)}) %all-to-all-start.1) | async-done | bytes 479776 | tf_op jit(solution)/shard_map/all_to_all | solution.py:129
  92.9 0.7 reshape.193
  93.6 1.0 copy.36
  94.6 0.1 slice.43
  94.8 0.1 copy.37
  94.9 0.1 reshape.174
  95.0 0.1 copy.38
  95.2 0.6 fusion.53
  95.7 0.6 convolution_multiply_fusion.1
  96.4 0.7 fusion.27
  97.0 0.6 convolution_bitcast_fusion
  97.7 0.2 reshape.177
  97.8 0.1 reshape_reshape.3
  98.0 0.1 slice_reduce_fusion
  98.2 0.4 copy.40
  98.5 0.8 reshape.180
  99.3 0.9 fusion.96
  100.2 0.1 reshape.190
  100.3 0.1 copy.39
  100.4 0.1 pad.6.clone
  100.6 0.2 maximum_bitcast_fusion
  100.8 0.8 copy.41
  101.6 9.1 %all-to-all-start.2 = ((f32[128,1,343]{2,1,0:T(1,128)}), f32[128,1,343]{2,1,0:T(1,128)S(1)}, u32[]{:S(2)}, u32[]{:S(2)}) async-start(f32[128,1,343]{2,1,0:T(1,128)} %copy.41), calls=%async_computation.2 | async-start | bytes 393216 | tf_op jit(solution)/shard_map/all_to_all | solution.py:159
  110.7 0.3 iota_compare_fusion.6
  111.0 0.2 fusion.55
  111.3 0.1 copy.46
  111.4 17.7 %all-to-all-done.2 = f32[128,1,343]{2,1,0:T(1,128)S(1)} async-done(((f32[128,1,343]{2,1,0:T(1,128)}), f32[128,1,343]{2,1,0:T(1,128)S(1)}, u32[]{:S(2)}, u32[]{:S(2)}) %all-to-all-start.2) | async-done | bytes 175648 | tf_op jit(solution)/shard_map/all_to_all | solution.py:159
  129.1 0.1 copy.42
  129.2 0.1 slice_reduce_fusion.1
  129.4 0.1 copy.45
  129.5 0.2 reshape.183
  129.7 0.2 div.123
  129.9 0.2 div.129
  130.2 0.6 fusion.13
  130.8 0.1 div.128
  130.9 1.0 fusion.1
  131.8 1.0 convolution_add_fusion.1
  132.8 1.0 convolution_add_fusion
  133.9 0.6 fusion.7
  134.4 0.7 select_reduce_fusion
  135.2 1.8 %fusion = f32[3,6912]{1,0:T(4,128)} fusion(bf16[512,6912]{1,0:T(8,128)(2,1)S(1)} %bitcast.82, bf16[512,18]{1,0:T(8,128)(2,1)S(1)} %fusion.7, s32[]{:T(128)S(6)} %select_n.145, f32[3,6912]{1,0:T(4,128)S(1)} %select_reduce_fusion, bf16[3,6912]{1,0:T(4,128)(2,1)S(1)} %copy-done, f32[6912]{0:T(1024)S(1)} %fusion.41), kind=kOutput, calls=%fused_computation.4 | convolution fusion | flops 21337344 | bytes 7331332 | tf_op jit(solution)/shard_map/dot_general | solution.py:182
  136.9 1.0 fusion.8
  (27 shorter events, 0.4 us)
Async XLA Ops:
  2.3 27.6 %all-to-all-start = ((bf16[6,3,6912]{2,1,0:T(4,128)(2,1)}), bf16[6,3,6912]{2,1,0:T(4,128)(2,1)S(1)}, u32[]{:S(2)}, u32[]{:S(2)}) async-start(bf16[6,3,6912]{2,1,0:T(4,128)(2,1)} %broadcast_in_dim.38), calls=%async_computation | async-start | bytes 663552 | tf_op jit(solution)/shard_map/all_to_all | solution.py:55
  31.5 5.9 %copy-start = (bf16[3,6912]{1,0:T(4,128)(2,1)S(1)}, bf16[3,6912]{1,0:T(4,128)(2,1)}, u32[]{:S(2)}) copy-start(bf16[3,6912]{1,0:T(4,128)(2,1)} %param.6) | copy-start | bytes 124420
  42.9 52.8 %copy-start.1 = (f32[1,128,128]{2,1,0:T(8,128)S(1)}, f32[1,128,128]{2,1,0:T(8,128)}, u32[]{:S(2)}) copy-start(f32[1,128,128]{2,1,0:T(8,128)} %param.8) | copy-start | bytes 196612
  48.3 44.6 %all-to-all-start.1 = ((bf16[128,2,937]{2,1,0:T(2,128)(2,1)}), bf16[128,2,937]{2,1,0:T(2,128)(2,1)S(1)}, u32[]{:S(2)}, u32[]{:S(2)}) async-start(bf16[128,2,937]{2,1,0:T(2,128)(2,1)} %reshape.192), calls=%async_computation.1 | async-start | bytes 1048576 | tf_op jit(solution)/shard_map/all_to_all | solution.py:129
  94.6 16.3 %copy-start.2 = (f32[4,8,8]{2,1,0:T(8,128)S(1)}, f32[4,8,8]{2,1,0:T(8,128)}, u32[]{:S(2)}) copy-start(f32[4,8,8]{2,1,0:T(8,128)} %param.11) | copy-start | bytes 3076
  94.6 16.4 %copy-start.3 = (s32[64]{0:T(128)S(1)}, s32[64]{0:T(128)}, u32[]{:S(2)}) copy-start(s32[64]{0:T(128)} %param.10) | copy-start | bytes 772
  101.6 27.5 %all-to-all-start.2 = ((f32[128,1,343]{2,1,0:T(1,128)}), f32[128,1,343]{2,1,0:T(1,128)S(1)}, u32[]{:S(2)}, u32[]{:S(2)}) async-start(f32[128,1,343]{2,1,0:T(1,128)} %copy.41), calls=%async_computation.2 | async-start | bytes 393216 | tf_op jit(solution)/shard_map/all_to_all | solution.py:159
  131.8 3.3 %slice-start = ((s8[7077888]{0:T(1024)(128)(4,1)}), s8[4194304]{0:T(1024)(128)(4,1)S(1)}, s32[]{:S(2)}) async-start(s8[7077888]{0:T(1024)(128)(4,1)} %bitcast.81), calls=%async_computation.3 | async-start | bytes 8388608
  132.8 2.3 %slice-start.1 = ((s8[7077888]{0:T(1024)(128)(4,1)}), s8[2883584]{0:T(1024)(128)(4,1)S(1)}, s32[]{:S(2)}) async-start(s8[7077888]{0:T(1024)(128)(4,1)} %bitcast.81), calls=%async_computation.4 | async-start | bytes 5767168

commit v8 on v7

--- a/solution.py
+++ b/solution.py
@@ -119,19 +119,30 @@
     width = -(-packed.shape[0] // npw)
     packed = jnp.pad(packed, (0, width * npw - packed.shape[0])).reshape(npw, width)
     columns = columns.reshape(npw, total, stick_count)
-    exact = jnp.concatenate(
-        [lax.dynamic_slice_in_dim(columns, group * bands, bands, axis=1).reshape(npw, -1), packed], axis=1
-    )
-    exact_hi, exact_lo = split2(exact)
+    columns_hi = lax.reduce_precision(columns, exponent_bits=8, mantissa_bits=7)
+    columns_lo = lax.dynamic_slice_in_dim(columns - columns_hi, group * bands, bands, axis=1)
+    packed_hi, packed_lo = split2(packed)
     sent = jnp.concatenate(
-        [exact_hi, exact_lo, columns.reshape(npw, -1).astype(jnp.bfloat16)], axis=1
+        [
+            columns_hi.reshape(npw, -1).astype(jnp.bfloat16),
+            columns_lo.reshape(npw, -1).astype(jnp.bfloat16),
+            packed_hi,
+            packed_lo,
+        ],
+        axis=1,
     )
     got = lax.all_to_all(sent, PW, 0, 0, tiled=True)
-    nexact = exact.shape[1]
-    joined = got[:, :nexact].astype(jnp.float32) + got[:, nexact : 2 * nexact].astype(jnp.float32)
-    mine = joined[:, : bands * stick_count].reshape(npw, bands, stick_count)
-    owned = jnp.sum(joined[:, bands * stick_count :], axis=0)
-    piece = got[:, 2 * nexact :].astype(jnp.float32).reshape(npw, total, stick_count)
+    nall = total * stick_count
+    nown = bands * stick_count
+    piece = got[:, :nall].astype(jnp.float32).reshape(npw, total, stick_count)
+    mine = lax.dynamic_slice_in_dim(piece, group * bands, bands, axis=1) + got[
+        :, nall : nall + nown
+    ].astype(jnp.float32).reshape(npw, bands, stick_count)
+    owned = jnp.sum(
+        got[:, nall + nown : nall + nown + width].astype(jnp.float32)
+        + got[:, nall + nown + width :].astype(jnp.float32),
+        axis=0,
+    )
     grid = jnp.transpose(mine, (1, 0, 2)).reshape(bands, planes, side, side)
     half = jnp.einsum("bzjk,jx->bzxk", grid, side_table, precision=highest)
     real_space = jnp.einsum("bzxk,ky->bzxy", half, side_table, precision=highest)

time: 139 us -> 134 us (0.964)
  local copies, waits for them, and re-layouts: 12.3 us -> 10.2 us
  starting transfers between devices: 42.1 us -> 40.2 us
    all_to_all x1, starting transfers between devices: 9.12 us -> 7.2 us  [local(): ret = lax.all_to_all(ret_sent, PW, 0, 0, tiled=True)]
where the time goes in v8:
time: 134 us
  waiting for transfers between devices  54.7 us (41%)
  starting transfers between devices  40.2 us (30%)
  matrix products  21.8 us (16%)
  local copies, waits for them, and re-layouts  10.2 us (8%)
  other arithmetic  5.79 us (4%)
    all_to_all x1, waiting for transfers between devices, local(): got = lax.all_to_all(sent, PW, 0, 0, tiled=True)  24.1 us
    all_to_all x1, starting transfers between devices, local(): got = lax.all_to_all(sent, PW, 0, 0, tiled=True)  20.3 us
    all_to_all x1, waiting for transfers between devices, local(): ret = lax.all_to_all(ret_sent, PW, 0, 0, tiled=True)  17.6 us
    all_to_all x1, waiting for transfers between devices, gathered_bands(): every = lax.all_to_all(copies, axis, 0, 0, tiled=True)  13 us
    all_to_all x1, starting transfers between devices, gathered_bands(): every = lax.all_to_all(copies, axis, 0, 0, tiled=True)  12.6 us
    all_to_all x1, starting transfers between devices, local(): ret = lax.all_to_all(ret_sent, PW, 0, 0, tiled=True)  7.2 us
    dot_general x1, matrix products, local(): lax.dot_general(every, projectors, (((1,), (1,)), ((), ())), preferred_el...  4.98 us
    dot_general x1, matrix products, local(): jnp.dot(on_plane.astype(jnp.bfloat16), spread.reshape(count, total * stic...  4.93 us
  transfers between devices with their start and end apart: 3, of which 3 were waited for; matrix products, arithmetic and copies ran while one was open for 2% of the time, Pallas kernels for 0%

profile of v8, /device:TPU:1, one launch (start us, length us, event | category | flops | bytes accessed | tf_op | source)
XLA Modules:
  0.0 133.7 jit_solution(6231656973435487630)
XLA Ops:
  0.6 1.6 %broadcast_in_dim.38 = bf16[6,3,6912]{2,1,0:T(4,128)(2,1)} broadcast(bf16[3,6912]{1,0:T(4,128)(2,1)} %param.6), dimensions={1,2} | broadcast | bytes 290304 | tf_op jit(solution)/shard_map/broadcast_in_dim | solution.py:54
  2.3 12.6 %all-to-all-start = ((bf16[6,3,6912]{2,1,0:T(4,128)(2,1)}), bf16[6,3,6912]{2,1,0:T(4,128)(2,1)S(1)}, u32[]{:S(2)}, u32[]{:S(2)}) async-start(bf16[6,3,6912]{2,1,0:T(4,128)(2,1)} %broadcast_in_dim.38), calls=%async_computation | async-start | bytes 663552 | tf_op jit(solution)/shard_map/all_to_all | solution.py:55
  14.9 0.8 add_select_fusion.2
  15.7 0.3 iota_compare_fusion.5
  16.0 0.9 fusion.44
  16.9 13.0 %all-to-all-done = bf16[6,3,6912]{2,1,0:T(4,128)(2,1)S(1)} async-done(((bf16[6,3,6912]{2,1,0:T(4,128)(2,1)}), bf16[6,3,6912]{2,1,0:T(4,128)(2,1)S(1)}, u32[]{:S(2)}, u32[]{:S(2)}) %all-to-all-start) | async-done | bytes 248864 | tf_op jit(solution)/shard_map/all_to_all | solution.py:55
  29.9 0.2 reshape.170
  30.1 1.4 %broadcast_select_fusion = bf16[6912,18,72]{0,2,1:T(8,128)(2,1)S(1)} fusion(pred[6912,72]{0,1:T(8,128)(4,1)S(1)} %iota_compare_fusion.5, bf16[6912,18]{0,1:T(8,128)(2,1)S(1)} %bitcast.92), kind=kLoop, calls=%fused_computation | loop fusion | flops 8957952 | bytes 18662400 | tf_op jit(solution)/shard_map/jit(_where)/select_n | solution.py:97
  31.5 4.9 %fusion.2 = f32[128,1296]{0,1:T(8,128)S(1)} fusion(bf16[6912,1296]{0,1:T(8,128)(2,1)S(1)} %bitcast.84, s32[6912]{0:T(1024)S(1)} %get-tuple-element.6), kind=kOutput, calls=%fused_computation.8 | convolution fusion | flops 2294120448 | bytes 18607104 | tf_op jit(solution)/shard_map/dot_general | solution.py:98
  36.4 1.0 reduce-precision_convert_fusion
  37.4 0.4 fusion.14
  37.8 0.1 reshape.173
  37.9 5.0 %fusion.97 = f32[512,18]{1,0:T(8,128)S(1)} fusion(bf16[512,6912]{1,0:T(8,128)(2,1)} %param.9, bf16[18,6912]{1,0:T(8,128)(2,1)S(1)} %reshape.170), kind=kOutput, calls=%fused_computation.170 | convolution fusion | flops 127401984 | bytes 7363584 | tf_op jit(solution)/shard_map/dot_general | solution.py:107
  42.9 0.2 reshape.172
  43.1 0.2 reshape.174
  43.3 0.1 copy.52
  43.5 0.4 concatenate.10
  43.9 0.5 broadcast.192
  44.4 1.0 reduce
  45.4 0.3 copy.76
  45.6 1.2 reshape.197
  46.8 20.3 %all-to-all-start.1 = ((bf16[128,2,829]{2,1,0:T(2,128)(2,1)}), bf16[128,2,829]{2,1,0:T(2,128)(2,1)S(1)}, u32[]{:S(2)}, u32[]{:S(2)}) async-start(bf16[128,2,829]{2,1,0:T(2,128)(2,1)} %reshape.197), calls=%async_computation.1 | async-start | bytes 917504 | tf_op jit(solution)/shard_map/all_to_all | solution.py:134
  67.2 24.1 %all-to-all-done.1 = bf16[128,2,829]{2,1,0:T(2,128)(2,1)S(1)} async-done(((bf16[128,2,829]{2,1,0:T(2,128)(2,1)}), bf16[128,2,829]{2,1,0:T(2,128)(2,1)S(1)}, u32[]{:S(2)}, u32[]{:S(2)}) %all-to-all-start.1) | async-done | bytes 424480 | tf_op jit(solution)/shard_map/all_to_all | solution.py:134
  91.2 0.6 reshape.198
  92.0 0.1 slice.37
  92.1 0.2 copy.69
  92.4 0.1 copy.70
  92.5 0.1 copy.57
  92.7 0.1 reshape.179
  92.8 0.1 copy.58
  92.9 0.6 fusion.56
  93.5 0.6 convolution_multiply_fusion.1
  94.1 0.7 fusion.29
  94.8 0.6 convolution_bitcast_fusion
  95.4 0.2 reshape.182
  95.6 0.1 reshape_reshape.3
  95.7 0.1 add_reduce_fusion
  95.8 0.4 copy.60
  96.2 0.8 reshape.183
  97.0 0.9 fusion.98
  97.9 0.1 reshape.195
  98.0 0.1 copy.59
  98.3 0.2 maximum_bitcast_fusion
  98.4 0.8 copy.61
  99.2 7.2 %all-to-all-start.2 = ((f32[128,1,343]{2,1,0:T(1,128)}), f32[128,1,343]{2,1,0:T(1,128)S(1)}, u32[]{:S(2)}, u32[]{:S(2)}) async-start(f32[128,1,343]{2,1,0:T(1,128)} %copy.61), calls=%async_computation.2 | async-start | bytes 393216 | tf_op jit(solution)/shard_map/all_to_all | solution.py:170
  106.5 0.3 iota_compare_fusion.6
  106.8 0.2 fusion.58
  107.0 0.1 copy.66
  107.2 17.6 %all-to-all-done.2 = f32[128,1,343]{2,1,0:T(1,128)S(1)} async-done(((f32[128,1,343]{2,1,0:T(1,128)}), f32[128,1,343]{2,1,0:T(1,128)S(1)}, u32[]{:S(2)}, u32[]{:S(2)}) %all-to-all-start.2) | async-done | bytes 175648 | tf_op jit(solution)/shard_map/all_to_all | solution.py:170
  124.8 0.1 copy.62
  125.0 0.1 slice_reduce_fusion
  125.1 0.1 copy.65
  125.2 0.2 reshape.186
  125.4 0.2 div.123
  125.6 0.2 div.129
  125.9 0.6 fusion.13
  126.5 0.1 div.128
  126.6 1.0 fusion.1
  127.6 1.0 convolution_add_fusion.1
  128.6 1.0 convolution_add_fusion
  129.6 0.6 fusion.7
  130.2 0.7 select_reduce_fusion
  130.9 1.8 %fusion = f32[3,6912]{1,0:T(4,128)} fusion(bf16[512,6912]{1,0:T(8,128)(2,1)S(1)} %bitcast.86, bf16[512,18]{1,0:T(8,128)(2,1)S(1)} %fusion.7, s32[]{:T(128)S(6)} %select_n.146, f32[3,6912]{1,0:T(4,128)S(1)} %select_reduce_fusion, bf16[3,6912]{1,0:T(4,128)(2,1)S(1)} %copy-done, f32[6912]{0:T(1024)S(1)} %fusion.44), kind=kOutput, calls=%fused_computation.4 | convolution fusion | flops 21337344 | bytes 7331332 | tf_op jit(solution)/shard_map/dot_general | solution.py:193
  132.7 1.0 fusion.8
  (28 shorter events, 0.5 us)
Async XLA Ops:
  2.3 27.6 %all-to-all-start = ((bf16[6,3,6912]{2,1,0:T(4,128)(2,1)}), bf16[6,3,6912]{2,1,0:T(4,128)(2,1)S(1)}, u32[]{:S(2)}, u32[]{:S(2)}) async-start(bf16[6,3,6912]{2,1,0:T(4,128)(2,1)} %broadcast_in_dim.38), calls=%async_computation | async-start | bytes 663552 | tf_op jit(solution)/shard_map/all_to_all | solution.py:55
  31.5 5.9 %copy-start = (bf16[3,6912]{1,0:T(4,128)(2,1)S(1)}, bf16[3,6912]{1,0:T(4,128)(2,1)}, u32[]{:S(2)}) copy-start(bf16[3,6912]{1,0:T(4,128)(2,1)} %param.6) | copy-start | bytes 124420
  43.1 50.4 %copy-start.1 = (f32[1,128,128]{2,1,0:T(8,128)S(1)}, f32[1,128,128]{2,1,0:T(8,128)}, u32[]{:S(2)}) copy-start(f32[1,128,128]{2,1,0:T(8,128)} %param.8) | copy-start | bytes 196612
  46.8 44.4 %all-to-all-start.1 = ((bf16[128,2,829]{2,1,0:T(2,128)(2,1)}), bf16[128,2,829]{2,1,0:T(2,128)(2,1)S(1)}, u32[]{:S(2)}, u32[]{:S(2)}) async-start(bf16[128,2,829]{2,1,0:T(2,128)(2,1)} %reshape.197), calls=%async_computation.1 | async-start | bytes 917504 | tf_op jit(solution)/shard_map/all_to_all | solution.py:134
  92.1 14.6 %copy-start.2 = (f32[4,8,8]{2,1,0:T(8,128)S(1)}, f32[4,8,8]{2,1,0:T(8,128)}, u32[]{:S(2)}) copy-start(f32[4,8,8]{2,1,0:T(8,128)} %param.11) | copy-start | bytes 3076
  92.1 14.7 %copy-start.3 = (s32[64]{0:T(128)S(1)}, s32[64]{0:T(128)}, u32[]{:S(2)}) copy-start(s32[64]{0:T(128)} %param.10) | copy-start | bytes 772
  99.2 25.6 %all-to-all-start.2 = ((f32[128,1,343]{2,1,0:T(1,128)}), f32[128,1,343]{2,1,0:T(1,128)S(1)}, u32[]{:S(2)}, u32[]{:S(2)}) async-start(f32[128,1,343]{2,1,0:T(1,128)} %copy.61), calls=%async_computation.2 | async-start | bytes 393216 | tf_op jit(solution)/shard_map/all_to_all | solution.py:170
  127.5 3.3 %slice-start = ((s8[7077888]{0:T(1024)(128)(4,1)}), s8[4194304]{0:T(1024)(128)(4,1)S(1)}, s32[]{:S(2)}) async-start(s8[7077888]{0:T(1024)(128)(4,1)} %bitcast.85), calls=%async_computation.3 | async-start | bytes 8388608
  128.6 2.3 %slice-start.1 = ((s8[7077888]{0:T(1024)(128)(4,1)}), s8[2883584]{0:T(1024)(128)(4,1)S(1)}, s32[]{:S(2)}) async-start(s8[7077888]{0:T(1024)(128)(4,1)} %bitcast.85), calls=%async_computation.4 | async-start | bytes 5767168

commit v9 on v8

--- a/solution.py
+++ b/solution.py
@@ -104,9 +104,13 @@
     side_table = cas_table(side_frequency(jnp.arange(side)), length)
     columns = jnp.dot(z_table.T, dense, precision=highest, preferred_element_type=jnp.float32)
     energies = kinetic(slot_map, owner * stick_count, stick_count, length, side)
+    lanes = -(-total // 128) * 128
     partial_corr = lax.dot_general(
-        every, projectors, (((1,), (1,)), ((), ())), preferred_element_type=jnp.float32
-    ).T
+        projectors,
+        jnp.pad(every, ((0, lanes - total), (0, 0))),
+        (((1,), (1,)), ((), ())),
+        preferred_element_type=jnp.float32,
+    )[:, :total]
     partial_kin = lax.dot_general(
         energies[None, :] * wide,
         every.astype(jnp.float32),

time: 134 us -> 135 us (level)
  no operation moved by 1% of the time
where the time goes in v9:
time: 135 us; the launch traced here: 134 us
  waiting for transfers between devices  54.7 us (41%)
  starting transfers between devices  40.2 us (30%)
  matrix products  22.3 us (17%)
  local copies, waits for them, and re-layouts  10.3 us (8%)
  other arithmetic  5.79 us (4%)
    all_to_all x1, waiting for transfers between devices, local(): got = lax.all_to_all(sent, PW, 0, 0, tiled=True)  24.1 us
    all_to_all x1, starting transfers between devices, local(): got = lax.all_to_all(sent, PW, 0, 0, tiled=True)  20.3 us
    all_to_all x1, waiting for transfers between devices, local(): ret = lax.all_to_all(ret_sent, PW, 0, 0, tiled=True)  17.6 us
    all_to_all x1, waiting for transfers between devices, gathered_bands(): every = lax.all_to_all(copies, axis, 0, 0, tiled=True)  13 us
    all_to_all x1, starting transfers between devices, gathered_bands(): every = lax.all_to_all(copies, axis, 0, 0, tiled=True)  12.6 us
    all_to_all x1, starting transfers between devices, local(): ret = lax.all_to_all(ret_sent, PW, 0, 0, tiled=True)  7.19 us
    dot_general x1, matrix products, local(): lax.dot_general(projectors, jnp.pad(every, ((0, lanes - total), (0, 0))),...  5.44 us
    dot_general x1, matrix products, local(): jnp.dot(on_plane.astype(jnp.bfloat16), spread.reshape(count, total * stic...  4.93 us
  transfers between devices with their start and end apart: 3, of which 3 were waited for; matrix products, arithmetic and copies ran while one was open for 2% of the time, Pallas kernels for 0%

profile of v9, /device:TPU:1, one launch (start us, length us, event | category | flops | bytes accessed | tf_op | source)
XLA Modules:
  0.0 134.3 jit_solution(5291943580439484605)
XLA Ops:
  0.6 1.6 %broadcast_in_dim.38 = bf16[6,3,6912]{2,1,0:T(4,128)(2,1)} broadcast(bf16[3,6912]{1,0:T(4,128)(2,1)} %param.6), dimensions={1,2} | broadcast | bytes 290304 | tf_op jit(solution)/shard_map/broadcast_in_dim | solution.py:54
  2.3 12.6 %all-to-all-start = ((bf16[6,3,6912]{2,1,0:T(4,128)(2,1)}), bf16[6,3,6912]{2,1,0:T(4,128)(2,1)S(1)}, u32[]{:S(2)}, u32[]{:S(2)}) async-start(bf16[6,3,6912]{2,1,0:T(4,128)(2,1)} %broadcast_in_dim.38), calls=%async_computation | async-start | bytes 663552 | tf_op jit(solution)/shard_map/all_to_all | solution.py:55
  14.9 0.8 add_select_fusion.2
  15.7 0.3 iota_compare_fusion.5
  16.0 0.9 fusion.49
  16.9 13.0 %all-to-all-done = bf16[6,3,6912]{2,1,0:T(4,128)(2,1)S(1)} async-done(((bf16[6,3,6912]{2,1,0:T(4,128)(2,1)}), bf16[6,3,6912]{2,1,0:T(4,128)(2,1)S(1)}, u32[]{:S(2)}, u32[]{:S(2)}) %all-to-all-start) | async-done | bytes 248864 | tf_op jit(solution)/shard_map/all_to_all | solution.py:55
  29.9 0.2 reshape.170
  30.1 1.4 %broadcast_select_fusion = bf16[6912,18,72]{0,2,1:T(8,128)(2,1)S(1)} fusion(pred[6912,72]{0,1:T(8,128)(4,1)S(1)} %iota_compare_fusion.5, bf16[6912,18]{0,1:T(8,128)(2,1)S(1)} %bitcast.93), kind=kLoop, calls=%fused_computation | loop fusion | flops 8957952 | bytes 18662400 | tf_op jit(solution)/shard_map/jit(_where)/select_n | solution.py:97
  31.5 4.9 %fusion.2 = f32[128,1296]{0,1:T(8,128)S(1)} fusion(bf16[6912,1296]{0,1:T(8,128)(2,1)S(1)} %bitcast.85, s32[6912]{0:T(1024)S(1)} %get-tuple-element.6), kind=kOutput, calls=%fused_computation.8 | convolution fusion | flops 2294120448 | bytes 18607104 | tf_op jit(solution)/shard_map/dot_general | solution.py:98
  36.4 1.0 reduce-precision_convert_fusion
  37.4 0.4 fusion.19
  37.8 0.1 reshape.173
  37.9 5.4 %fusion.9 = f32[512,128]{0,1:T(8,128)S(1)} fusion(bf16[512,6912]{1,0:T(8,128)(2,1)} %param.9, bf16[18,6912]{1,0:T(8,128)(2,1)S(1)} %reshape.170), kind=kOutput, calls=%fused_computation.17 | convolution fusion | flops 905969664 | bytes 7588864 | tf_op jit(solution)/shard_map/dot_general | solution.py:108
  43.4 0.1 copy.51
  43.5 0.2 reshape.172
  43.7 0.2 reshape.174
  43.9 0.1 copy.52
  44.1 0.4 concatenate.10
  44.5 0.5 broadcast.194
  45.0 1.0 reduce
  46.0 0.3 copy.75
  46.2 1.2 reshape.197
  47.5 20.3 %all-to-all-start.1 = ((bf16[128,2,829]{2,1,0:T(2,128)(2,1)}), bf16[128,2,829]{2,1,0:T(2,128)(2,1)S(1)}, u32[]{:S(2)}, u32[]{:S(2)}) async-start(bf16[128,2,829]{2,1,0:T(2,128)(2,1)} %reshape.197), calls=%async_computation.1 | async-start | bytes 917504 | tf_op jit(solution)/shard_map/all_to_all | solution.py:138
  67.8 24.1 %all-to-all-done.1 = bf16[128,2,829]{2,1,0:T(2,128)(2,1)S(1)} async-done(((bf16[128,2,829]{2,1,0:T(2,128)(2,1)}), bf16[128,2,829]{2,1,0:T(2,128)(2,1)S(1)}, u32[]{:S(2)}, u32[]{:S(2)}) %all-to-all-start.1) | async-done | bytes 424480 | tf_op jit(solution)/shard_map/all_to_all | solution.py:138
  91.9 0.6 reshape.198
  92.6 0.1 slice.42
  92.7 0.2 copy.68
  93.0 0.1 copy.69
  93.2 0.1 copy.57
  93.3 0.1 reshape.179
  93.4 0.1 copy.58
  93.5 0.6 fusion.61
  94.1 0.6 convolution_multiply_fusion.1
  94.8 0.7 fusion.34
  95.4 0.6 convolution_bitcast_fusion
  96.1 0.2 reshape.182
  96.2 0.1 reshape_reshape.3
  96.4 0.1 add_reduce_fusion
  96.5 0.4 copy.60
  96.8 0.8 reshape.183
  97.6 0.9 fusion.103
  98.5 0.1 reshape.195
  98.6 0.1 copy.59
  98.9 0.2 maximum_bitcast_fusion
  99.1 0.8 copy.61
  99.9 7.2 %all-to-all-start.2 = ((f32[128,1,343]{2,1,0:T(1,128)}), f32[128,1,343]{2,1,0:T(1,128)S(1)}, u32[]{:S(2)}, u32[]{:S(2)}) async-start(f32[128,1,343]{2,1,0:T(1,128)} %copy.61), calls=%async_computation.2 | async-start | bytes 393216 | tf_op jit(solution)/shard_map/all_to_all | solution.py:174
  107.1 0.3 iota_compare_fusion.6
  107.4 0.2 fusion.63
  107.7 0.1 copy.66
  107.8 17.6 %all-to-all-done.2 = f32[128,1,343]{2,1,0:T(1,128)S(1)} async-done(((f32[128,1,343]{2,1,0:T(1,128)}), f32[128,1,343]{2,1,0:T(1,128)S(1)}, u32[]{:S(2)}, u32[]{:S(2)}) %all-to-all-start.2) | async-done | bytes 175648 | tf_op jit(solution)/shard_map/all_to_all | solution.py:174
  125.4 0.1 copy.62
  125.6 0.1 slice_reduce_fusion
  125.7 0.1 copy.65
  125.8 0.2 reshape.186
  126.0 0.2 div.123
  126.3 0.2 div.129
  126.5 0.6 fusion.18
  127.2 1.0 fusion.1
  128.2 1.0 convolution_add_fusion.1
  129.2 1.0 convolution_add_fusion
  130.2 0.6 fusion.12
  130.8 0.7 select_reduce_fusion
  131.5 1.8 %fusion = f32[3,6912]{1,0:T(4,128)} fusion(bf16[512,6912]{1,0:T(8,128)(2,1)S(1)} %bitcast.87, bf16[512,18]{1,0:T(8,128)(2,1)S(1)} %fusion.12, s32[]{:T(128)S(6)} %select_n.146, f32[3,6912]{1,0:T(4,128)S(1)} %select_reduce_fusion, bf16[3,6912]{1,0:T(4,128)(2,1)S(1)} %copy-done, f32[6912]{0:T(1024)S(1)} %fusion.49), kind=kOutput, calls=%fused_computation.4 | convolution fusion | flops 21337344 | bytes 7331332 | tf_op jit(solution)/shard_map/dot_general | solution.py:197
  133.3 1.0 fusion.13
  (30 shorter events, 0.6 us)
Async XLA Ops:
  2.3 27.6 %all-to-all-start = ((bf16[6,3,6912]{2,1,0:T(4,128)(2,1)}), bf16[6,3,6912]{2,1,0:T(4,128)(2,1)S(1)}, u32[]{:S(2)}, u32[]{:S(2)}) async-start(bf16[6,3,6912]{2,1,0:T(4,128)(2,1)} %broadcast_in_dim.38), calls=%async_computation | async-start | bytes 663552 | tf_op jit(solution)/shard_map/all_to_all | solution.py:55
  31.5 5.9 %copy-start = (bf16[3,6912]{1,0:T(4,128)(2,1)S(1)}, bf16[3,6912]{1,0:T(4,128)(2,1)}, u32[]{:S(2)}) copy-start(bf16[3,6912]{1,0:T(4,128)(2,1)} %param.6) | copy-start | bytes 124420
  43.7 50.4 %copy-start.1 = (f32[1,128,128]{2,1,0:T(8,128)S(1)}, f32[1,128,128]{2,1,0:T(8,128)}, u32[]{:S(2)}) copy-start(f32[1,128,128]{2,1,0:T(8,128)} %param.8) | copy-start | bytes 196612
  47.5 44.4 %all-to-all-start.1 = ((bf16[128,2,829]{2,1,0:T(2,128)(2,1)}), bf16[128,2,829]{2,1,0:T(2,128)(2,1)S(1)}, u32[]{:S(2)}, u32[]{:S(2)}) async-start(bf16[128,2,829]{2,1,0:T(2,128)(2,1)} %reshape.197), calls=%async_computation.1 | async-start | bytes 917504 | tf_op jit(solution)/shard_map/all_to_all | solution.py:138
  92.7 14.6 %copy-start.2 = (f32[4,8,8]{2,1,0:T(8,128)S(1)}, f32[4,8,8]{2,1,0:T(8,128)}, u32[]{:S(2)}) copy-start(f32[4,8,8]{2,1,0:T(8,128)} %param.11) | copy-start | bytes 3076
  92.7 14.7 %copy-start.3 = (s32[64]{0:T(128)S(1)}, s32[64]{0:T(128)}, u32[]{:S(2)}) copy-start(s32[64]{0:T(128)} %param.10) | copy-start | bytes 772
  99.9 25.6 %all-to-all-start.2 = ((f32[128,1,343]{2,1,0:T(1,128)}), f32[128,1,343]{2,1,0:T(1,128)S(1)}, u32[]{:S(2)}, u32[]{:S(2)}) async-start(f32[128,1,343]{2,1,0:T(1,128)} %copy.61), calls=%async_computation.2 | async-start | bytes 393216 | tf_op jit(solution)/shard_map/all_to_all | solution.py:174
  128.2 3.3 %slice-start = ((s8[7077888]{0:T(1024)(128)(4,1)}), s8[4194304]{0:T(1024)(128)(4,1)S(1)}, s32[]{:S(2)}) async-start(s8[7077888]{0:T(1024)(128)(4,1)} %bitcast.86), calls=%async_computation.3 | async-start | bytes 8388608
  129.2 2.3 %slice-start.1 = ((s8[7077888]{0:T(1024)(128)(4,1)}), s8[2883584]{0:T(1024)(128)(4,1)S(1)}, s32[]{:S(2)}) async-start(s8[7077888]{0:T(1024)(128)(4,1)} %bitcast.86), calls=%async_computation.4 | async-start | bytes 5767168

commit v10 on v8

--- a/solution.py
+++ b/solution.py
@@ -70,9 +70,9 @@
 
 
 def exact_select(x, onehot):
-    hi, mid, lo = split3(x)
+    hi, lo = split2(x)
     dot = lambda a: jnp.dot(a, onehot, preferred_element_type=jnp.float32)
-    return (dot(hi) + dot(mid)) + dot(lo)
+    return dot(hi) + dot(lo)
 
 
 def local(states, slot_map, potential, projectors, species, coupling):

time: 134 us -> 133 us (level)
    dot_general x3 -> x2, matrix products: 2.95 us -> 1.97 us  [exact_select(): dot = lambda a: jnp.dot(a, onehot, preferred_element_type=jnp.float32)]
where the time goes in v10:
time: 133 us
  waiting for transfers between devices  54.7 us (41%)
  starting transfers between devices  40.2 us (30%)
  matrix products  20.8 us (16%)
  local copies, waits for them, and re-layouts  10.2 us (8%)
  other arithmetic  5.79 us (4%)
    all_to_all x1, waiting for transfers between devices, local(): got = lax.all_to_all(sent, PW, 0, 0, tiled=True)  24.1 us
    all_to_all x1, starting transfers between devices, local(): got = lax.all_to_all(sent, PW, 0, 0, tiled=True)  20.3 us
    all_to_all x1, waiting for transfers between devices, local(): ret = lax.all_to_all(ret_sent, PW, 0, 0, tiled=True)  17.6 us
    all_to_all x1, waiting for transfers between devices, gathered_bands(): every = lax.all_to_all(copies, axis, 0, 0, tiled=True)  13 us
    all_to_all x1, starting transfers between devices, gathered_bands(): every = lax.all_to_all(copies, axis, 0, 0, tiled=True)  12.6 us
    all_to_all x1, starting transfers between devices, local(): ret = lax.all_to_all(ret_sent, PW, 0, 0, tiled=True)  7.19 us
    dot_general x1, matrix products, local(): lax.dot_general(every, projectors, (((1,), (1,)), ((), ())), preferred_el...  4.98 us
    dot_general x1, matrix products, local(): jnp.dot(on_plane.astype(jnp.bfloat16), spread.reshape(count, total * stic...  4.93 us
  transfers between devices with their start and end apart: 3, of which 3 were waited for; matrix products, arithmetic and copies ran while one was open for 2% of the time, Pallas kernels for 0%

profile of v10, /device:TPU:1, one launch (start us, length us, event | category | flops | bytes accessed | tf_op | source)
XLA Modules:
  0.0 132.7 jit_solution(1588290547753356346)
XLA Ops:
  0.6 1.6 %broadcast_in_dim.38 = bf16[6,3,6912]{2,1,0:T(4,128)(2,1)} broadcast(bf16[3,6912]{1,0:T(4,128)(2,1)} %param.6), dimensions={1,2} | broadcast | bytes 290304 | tf_op jit(solution)/shard_map/broadcast_in_dim | solution.py:54
  2.3 12.6 %all-to-all-start = ((bf16[6,3,6912]{2,1,0:T(4,128)(2,1)}), bf16[6,3,6912]{2,1,0:T(4,128)(2,1)S(1)}, u32[]{:S(2)}, u32[]{:S(2)}) async-start(bf16[6,3,6912]{2,1,0:T(4,128)(2,1)} %broadcast_in_dim.38), calls=%async_computation | async-start | bytes 663552 | tf_op jit(solution)/shard_map/all_to_all | solution.py:55
  14.9 0.8 add_select_fusion.2
  15.7 0.3 iota_compare_fusion.4
  16.0 0.9 fusion.43
  16.9 13.0 %all-to-all-done = bf16[6,3,6912]{2,1,0:T(4,128)(2,1)S(1)} async-done(((bf16[6,3,6912]{2,1,0:T(4,128)(2,1)}), bf16[6,3,6912]{2,1,0:T(4,128)(2,1)S(1)}, u32[]{:S(2)}, u32[]{:S(2)}) %all-to-all-start) | async-done | bytes 248864 | tf_op jit(solution)/shard_map/all_to_all | solution.py:55
  29.9 0.2 reshape.170
  30.1 1.4 %broadcast_select_fusion = bf16[6912,18,72]{0,2,1:T(8,128)(2,1)S(1)} fusion(pred[6912,72]{0,1:T(8,128)(4,1)S(1)} %iota_compare_fusion.4, bf16[6912,18]{0,1:T(8,128)(2,1)S(1)} %bitcast.92), kind=kLoop, calls=%fused_computation | loop fusion | flops 8957952 | bytes 18662400 | tf_op jit(solution)/shard_map/jit(_where)/select_n | solution.py:97
  31.5 4.9 %fusion.2 = f32[128,1296]{0,1:T(8,128)S(1)} fusion(bf16[6912,1296]{0,1:T(8,128)(2,1)S(1)} %bitcast.84, s32[6912]{0:T(1024)S(1)} %get-tuple-element.6), kind=kOutput, calls=%fused_computation.7 | convolution fusion | flops 2294120448 | bytes 18607104 | tf_op jit(solution)/shard_map/dot_general | solution.py:98
  36.4 1.0 reduce-precision_convert_fusion
  37.4 0.4 fusion.13
  37.8 0.1 reshape.173
  37.9 5.0 %fusion.96 = f32[512,18]{1,0:T(8,128)S(1)} fusion(bf16[512,6912]{1,0:T(8,128)(2,1)} %param.9, bf16[18,6912]{1,0:T(8,128)(2,1)S(1)} %reshape.170), kind=kOutput, calls=%fused_computation.166 | convolution fusion | flops 127401984 | bytes 7363584 | tf_op jit(solution)/shard_map/dot_general | solution.py:107
  42.9 0.2 reshape.172
  43.1 0.2 reshape.174
  43.3 0.1 copy.52
  43.5 0.4 concatenate.10
  43.9 0.5 broadcast.192
  44.4 1.0 reduce
  45.4 0.3 copy.76
  45.6 1.2 reshape.197
  46.8 20.3 %all-to-all-start.1 = ((bf16[128,2,829]{2,1,0:T(2,128)(2,1)}), bf16[128,2,829]{2,1,0:T(2,128)(2,1)S(1)}, u32[]{:S(2)}, u32[]{:S(2)}) async-start(bf16[128,2,829]{2,1,0:T(2,128)(2,1)} %reshape.197), calls=%async_computation.1 | async-start | bytes 917504 | tf_op jit(solution)/shard_map/all_to_all | solution.py:134
  67.2 24.1 %all-to-all-done.1 = bf16[128,2,829]{2,1,0:T(2,128)(2,1)S(1)} async-done(((bf16[128,2,829]{2,1,0:T(2,128)(2,1)}), bf16[128,2,829]{2,1,0:T(2,128)(2,1)S(1)}, u32[]{:S(2)}, u32[]{:S(2)}) %all-to-all-start.1) | async-done | bytes 424480 | tf_op jit(solution)/shard_map/all_to_all | solution.py:134
  91.2 0.6 reshape.198
  92.0 0.1 slice.37
  92.1 0.2 copy.69
  92.4 0.1 copy.70
  92.5 0.1 copy.57
  92.7 0.1 reshape.179
  92.8 0.1 copy.58
  92.9 0.6 fusion.55
  93.5 0.6 convolution_multiply_fusion.1
  94.1 0.7 fusion.28
  94.8 0.6 convolution_bitcast_fusion
  95.4 0.2 reshape.182
  95.6 0.1 reshape_reshape.3
  95.7 0.1 add_reduce_fusion
  95.8 0.4 copy.60
  96.2 0.8 reshape.183
  97.0 0.9 fusion.97
  97.9 0.1 reshape.195
  98.0 0.1 copy.59
  98.1 0.1 pad.6.clone
  98.3 0.2 maximum_bitcast_fusion
  98.4 0.8 copy.61
  99.2 7.2 %all-to-all-start.2 = ((f32[128,1,343]{2,1,0:T(1,128)}), f32[128,1,343]{2,1,0:T(1,128)S(1)}, u32[]{:S(2)}, u32[]{:S(2)}) async-start(f32[128,1,343]{2,1,0:T(1,128)} %copy.61), calls=%async_computation.2 | async-start | bytes 393216 | tf_op jit(solution)/shard_map/all_to_all | solution.py:170
  106.4 0.3 iota_compare_fusion.5
  106.8 0.2 fusion.57
  107.0 0.1 copy.66
  107.2 17.6 %all-to-all-done.2 = f32[128,1,343]{2,1,0:T(1,128)S(1)} async-done(((f32[128,1,343]{2,1,0:T(1,128)}), f32[128,1,343]{2,1,0:T(1,128)S(1)}, u32[]{:S(2)}, u32[]{:S(2)}) %all-to-all-start.2) | async-done | bytes 175648 | tf_op jit(solution)/shard_map/all_to_all | solution.py:170
  124.8 0.1 copy.62
  125.0 0.1 slice_reduce_fusion
  125.1 0.1 copy.65
  125.2 0.2 reshape.186
  125.4 0.2 div.123
  125.6 0.2 div.129
  125.9 0.6 fusion.12
  126.5 0.1 div.128
  126.6 1.0 fusion.1
  127.6 1.0 convolution_add_fusion
  128.6 0.6 fusion.6
  129.1 0.7 select_reduce_fusion
  129.9 1.8 %fusion = f32[3,6912]{1,0:T(4,128)} fusion(bf16[512,6912]{1,0:T(8,128)(2,1)S(1)} %bitcast.86, bf16[512,18]{1,0:T(8,128)(2,1)S(1)} %fusion.6, s32[]{:T(128)S(6)} %select_n.146, f32[3,6912]{1,0:T(4,128)S(1)} %select_reduce_fusion, bf16[3,6912]{1,0:T(4,128)(2,1)S(1)} %copy-done, f32[6912]{0:T(1024)S(1)} %fusion.43), kind=kOutput, calls=%fused_computation.3 | convolution fusion | flops 21337344 | bytes 7331332 | tf_op jit(solution)/shard_map/dot_general | solution.py:193
  131.7 1.0 fusion.7
  (27 shorter events, 0.5 us)
Async XLA Ops:
  2.3 27.6 %all-to-all-start = ((bf16[6,3,6912]{2,1,0:T(4,128)(2,1)}), bf16[6,3,6912]{2,1,0:T(4,128)(2,1)S(1)}, u32[]{:S(2)}, u32[]{:S(2)}) async-start(bf16[6,3,6912]{2,1,0:T(4,128)(2,1)} %broadcast_in_dim.38), calls=%async_computation | async-start | bytes 663552 | tf_op jit(solution)/shard_map/all_to_all | solution.py:55
  31.5 5.9 %copy-start = (bf16[3,6912]{1,0:T(4,128)(2,1)S(1)}, bf16[3,6912]{1,0:T(4,128)(2,1)}, u32[]{:S(2)}) copy-start(bf16[3,6912]{1,0:T(4,128)(2,1)} %param.6) | copy-start | bytes 124420
  43.1 50.4 %copy-start.1 = (f32[1,128,128]{2,1,0:T(8,128)S(1)}, f32[1,128,128]{2,1,0:T(8,128)}, u32[]{:S(2)}) copy-start(f32[1,128,128]{2,1,0:T(8,128)} %param.8) | copy-start | bytes 196612
  46.8 44.4 %all-to-all-start.1 = ((bf16[128,2,829]{2,1,0:T(2,128)(2,1)}), bf16[128,2,829]{2,1,0:T(2,128)(2,1)S(1)}, u32[]{:S(2)}, u32[]{:S(2)}) async-start(bf16[128,2,829]{2,1,0:T(2,128)(2,1)} %reshape.197), calls=%async_computation.1 | async-start | bytes 917504 | tf_op jit(solution)/shard_map/all_to_all | solution.py:134
  92.1 14.6 %copy-start.2 = (f32[4,8,8]{2,1,0:T(8,128)S(1)}, f32[4,8,8]{2,1,0:T(8,128)}, u32[]{:S(2)}) copy-start(f32[4,8,8]{2,1,0:T(8,128)} %param.11) | copy-start | bytes 3076
  92.1 14.7 %copy-start.3 = (s32[64]{0:T(128)S(1)}, s32[64]{0:T(128)}, u32[]{:S(2)}) copy-start(s32[64]{0:T(128)} %param.10) | copy-start | bytes 772
  99.2 25.6 %all-to-all-start.2 = ((f32[128,1,343]{2,1,0:T(1,128)}), f32[128,1,343]{2,1,0:T(1,128)S(1)}, u32[]{:S(2)}, u32[]{:S(2)}) async-start(f32[128,1,343]{2,1,0:T(1,128)} %copy.61), calls=%async_computation.2 | async-start | bytes 393216 | tf_op jit(solution)/shard_map/all_to_all | solution.py:170
  126.6 3.3 %slice-start = ((s8[7077888]{0:T(1024)(128)(4,1)}), s8[4194304]{0:T(1024)(128)(4,1)S(1)}, s32[]{:S(2)}) async-start(s8[7077888]{0:T(1024)(128)(4,1)} %bitcast.85), calls=%async_computation.3 | async-start | bytes 8388608
  127.5 2.4 %slice-start.1 = ((s8[7077888]{0:T(1024)(128)(4,1)}), s8[2883584]{0:T(1024)(128)(4,1)S(1)}, s32[]{:S(2)}) async-start(s8[7077888]{0:T(1024)(128)(4,1)} %bitcast.85), calls=%async_computation.4 | async-start | bytes 5767168

commit v11 on v10

--- a/solution.py
+++ b/solution.py
@@ -102,7 +102,7 @@
     )
     z_table = cas_table(jnp.arange(length), length)
     side_table = cas_table(side_frequency(jnp.arange(side)), length)
-    columns = jnp.dot(z_table.T, dense, precision=highest, preferred_element_type=jnp.float32)
+    columns = jnp.dot(z_table.T, dense, precision=lax.Precision.HIGH, preferred_element_type=jnp.float32)
     energies = kinetic(slot_map, owner * stick_count, stick_count, length, side)
     partial_corr = lax.dot_general(
         every, projectors, (((1,), (1,)), ((), ())), preferred_element_type=jnp.float32
@@ -144,11 +144,11 @@
         axis=0,
     )
     grid = jnp.transpose(mine, (1, 0, 2)).reshape(bands, planes, side, side)
-    half = jnp.einsum("bzjk,jx->bzxk", grid, side_table, precision=highest)
-    real_space = jnp.einsum("bzxk,ky->bzxy", half, side_table, precision=highest)
+    half = jnp.einsum("bzjk,jx->bzxk", grid, side_table, precision=lax.Precision.HIGH)
+    real_space = jnp.einsum("bzxk,ky->bzxy", half, side_table, precision=lax.Precision.HIGH)
     weighted = real_space * potential[None]
-    back_half = jnp.einsum("bzxy,ky->bzxk", weighted, side_table, precision=highest)
-    back_grid = jnp.einsum("bzxk,jx->bzjk", back_half, side_table, precision=highest)
+    back_half = jnp.einsum("bzxy,ky->bzxk", weighted, side_table, precision=lax.Precision.HIGH)
+    back_grid = jnp.einsum("bzxk,jx->bzjk", back_half, side_table, precision=lax.Precision.HIGH)
     back_own = back_grid.reshape(bands, side * side)
     piece = lax.dynamic_update_slice_in_dim(piece, mine, group * bands, axis=1)
     plane_gram = lax.dot_general(
@@ -175,7 +175,7 @@
     reduced = ret[:, bands * stick_count + bands * total :].reshape(-1)
     correlations = reduced[: nproj * total].reshape(nproj, total) / math.sqrt(NG)
     gram_kin = reduced[nproj * total : nproj * total + bands * total].reshape(bands, total)
-    spectral = jnp.einsum("zbs,kz->bsk", returned, z_table, precision=highest)
+    spectral = jnp.einsum("zbs,kz->bsk", returned, z_table, precision=lax.Precision.HIGH)
     picked = exact_select(
         spectral.reshape(bands * stick_count, length), on_plane.astype(jnp.bfloat16)
     ).reshape(bands, stick_count, -1)

time: 133 us -> 133 us (level)
  no operation moved by 1% of the time
where the time goes in v11:
time: 133 us; the launch traced here: 132 us
  waiting for transfers between devices  54.7 us (41%)
  starting transfers between devices  40.2 us (30%)
  matrix products  20 us (15%)
  local copies, waits for them, and re-layouts  10.2 us (8%)
  other arithmetic  5.79 us (4%)
    all_to_all x1, waiting for transfers between devices, local(): got = lax.all_to_all(sent, PW, 0, 0, tiled=True)  24.1 us
    all_to_all x1, starting transfers between devices, local(): got = lax.all_to_all(sent, PW, 0, 0, tiled=True)  20.3 us
    all_to_all x1, waiting for transfers between devices, local(): ret = lax.all_to_all(ret_sent, PW, 0, 0, tiled=True)  17.6 us
    all_to_all x1, waiting for transfers between devices, gathered_bands(): every = lax.all_to_all(copies, axis, 0, 0, tiled=True)  13 us
    all_to_all x1, starting transfers between devices, gathered_bands(): every = lax.all_to_all(copies, axis, 0, 0, tiled=True)  12.6 us
    all_to_all x1, starting transfers between devices, local(): ret = lax.all_to_all(ret_sent, PW, 0, 0, tiled=True)  7.2 us
    dot_general x1, matrix products, local(): lax.dot_general(every, projectors, (((1,), (1,)), ((), ())), preferred_el...  4.98 us
    dot_general x1, matrix products, local(): jnp.dot(on_plane.astype(jnp.bfloat16), spread.reshape(count, total * stic...  4.93 us
  transfers between devices with their start and end apart: 3, of which 3 were waited for; matrix products, arithmetic and copies ran while one was open for 2% of the time, Pallas kernels for 0%

profile of v11, /device:TPU:1, one launch (start us, length us, event | category | flops | bytes accessed | tf_op | source)
XLA Modules:
  0.0 131.9 jit_solution(12006253404694393052)
XLA Ops:
  0.6 1.6 %broadcast_in_dim.38 = bf16[6,3,6912]{2,1,0:T(4,128)(2,1)} broadcast(bf16[3,6912]{1,0:T(4,128)(2,1)} %param.6), dimensions={1,2} | broadcast | bytes 290304 | tf_op jit(solution)/shard_map/broadcast_in_dim | solution.py:54
  2.3 12.6 %all-to-all-start = ((bf16[6,3,6912]{2,1,0:T(4,128)(2,1)}), bf16[6,3,6912]{2,1,0:T(4,128)(2,1)S(1)}, u32[]{:S(2)}, u32[]{:S(2)}) async-start(bf16[6,3,6912]{2,1,0:T(4,128)(2,1)} %broadcast_in_dim.38), calls=%async_computation | async-start | bytes 663552 | tf_op jit(solution)/shard_map/all_to_all | solution.py:55
  14.9 0.8 add_select_fusion.2
  15.7 0.3 iota_compare_fusion.4
  16.0 0.9 fusion.43
  16.9 13.0 %all-to-all-done = bf16[6,3,6912]{2,1,0:T(4,128)(2,1)S(1)} async-done(((bf16[6,3,6912]{2,1,0:T(4,128)(2,1)}), bf16[6,3,6912]{2,1,0:T(4,128)(2,1)S(1)}, u32[]{:S(2)}, u32[]{:S(2)}) %all-to-all-start) | async-done | bytes 248864 | tf_op jit(solution)/shard_map/all_to_all | solution.py:55
  29.9 0.2 reshape.170
  30.1 1.4 %broadcast_select_fusion = bf16[6912,18,72]{0,2,1:T(8,128)(2,1)S(1)} fusion(pred[6912,72]{0,1:T(8,128)(4,1)S(1)} %iota_compare_fusion.4, bf16[6912,18]{0,1:T(8,128)(2,1)S(1)} %bitcast.92), kind=kLoop, calls=%fused_computation | loop fusion | flops 8957952 | bytes 18662400 | tf_op jit(solution)/shard_map/jit(_where)/select_n | solution.py:97
  31.5 4.9 %fusion.2 = f32[128,1296]{0,1:T(8,128)S(1)} fusion(bf16[6912,1296]{0,1:T(8,128)(2,1)S(1)} %bitcast.84, s32[6912]{0:T(1024)S(1)} %get-tuple-element.6), kind=kOutput, calls=%fused_computation.7 | convolution fusion | flops 2294120448 | bytes 18607104 | tf_op jit(solution)/shard_map/dot_general | solution.py:98
  36.4 0.7 reduce-precision_convert_fusion
  37.2 0.4 fusion.13
  37.6 0.1 reshape.173
  37.6 5.0 %fusion.96 = f32[512,18]{1,0:T(8,128)S(1)} fusion(bf16[512,6912]{1,0:T(8,128)(2,1)} %param.9, bf16[18,6912]{1,0:T(8,128)(2,1)S(1)} %reshape.170), kind=kOutput, calls=%fused_computation.166 | convolution fusion | flops 127401984 | bytes 7363584 | tf_op jit(solution)/shard_map/dot_general | solution.py:107
  42.6 0.2 reshape.172
  42.8 0.2 reshape.174
  43.1 0.1 copy.52
  43.2 0.4 concatenate.10
  43.6 0.5 broadcast.192
  44.1 1.0 reduce
  45.1 0.3 copy.76
  45.4 1.2 reshape.197
  46.6 20.3 %all-to-all-start.1 = ((bf16[128,2,829]{2,1,0:T(2,128)(2,1)}), bf16[128,2,829]{2,1,0:T(2,128)(2,1)S(1)}, u32[]{:S(2)}, u32[]{:S(2)}) async-start(bf16[128,2,829]{2,1,0:T(2,128)(2,1)} %reshape.197), calls=%async_computation.1 | async-start | bytes 917504 | tf_op jit(solution)/shard_map/all_to_all | solution.py:134
  66.9 24.1 %all-to-all-done.1 = bf16[128,2,829]{2,1,0:T(2,128)(2,1)S(1)} async-done(((bf16[128,2,829]{2,1,0:T(2,128)(2,1)}), bf16[128,2,829]{2,1,0:T(2,128)(2,1)S(1)}, u32[]{:S(2)}, u32[]{:S(2)}) %all-to-all-start.1) | async-done | bytes 424480 | tf_op jit(solution)/shard_map/all_to_all | solution.py:134
  91.0 0.6 reshape.198
  91.7 0.1 slice.37
  91.8 0.2 copy.69
  92.1 0.1 copy.70
  92.3 0.1 copy.57
  92.4 0.1 reshape.179
  92.5 0.1 copy.58
  92.7 0.5 fusion.55
  93.2 0.5 convolution_multiply_fusion.1
  93.7 0.5 fusion.28
  94.2 0.5 convolution_bitcast_fusion
  94.7 0.2 reshape.182
  94.8 0.1 reshape_reshape.3
  95.0 0.1 add_reduce_fusion
  95.1 0.4 copy.60
  95.5 0.8 reshape.183
  96.2 0.9 fusion.97
  97.2 0.1 reshape.195
  97.2 0.1 copy.59
  97.4 0.1 pad.6.clone
  97.5 0.2 maximum_bitcast_fusion
  97.7 0.8 copy.61
  98.5 7.2 %all-to-all-start.2 = ((f32[128,1,343]{2,1,0:T(1,128)}), f32[128,1,343]{2,1,0:T(1,128)S(1)}, u32[]{:S(2)}, u32[]{:S(2)}) async-start(f32[128,1,343]{2,1,0:T(1,128)} %copy.61), calls=%async_computation.2 | async-start | bytes 393216 | tf_op jit(solution)/shard_map/all_to_all | solution.py:170
  105.7 0.3 iota_compare_fusion.5
  106.1 0.2 fusion.57
  106.3 0.1 copy.66
  106.4 17.6 %all-to-all-done.2 = f32[128,1,343]{2,1,0:T(1,128)S(1)} async-done(((f32[128,1,343]{2,1,0:T(1,128)}), f32[128,1,343]{2,1,0:T(1,128)S(1)}, u32[]{:S(2)}, u32[]{:S(2)}) %all-to-all-start.2) | async-done | bytes 175648 | tf_op jit(solution)/shard_map/all_to_all | solution.py:170
  124.1 0.1 copy.62
  124.2 0.1 slice_reduce_fusion
  124.3 0.1 copy.65
  124.4 0.2 reshape.186
  124.7 0.2 div.123
  124.9 0.2 div.129
  125.1 0.5 fusion.12
  125.6 0.1 div.128
  125.7 1.0 fusion.1
  126.7 1.0 convolution_add_fusion
  127.7 0.6 fusion.6
  128.3 0.7 select_reduce_fusion
  129.1 1.8 %fusion = f32[3,6912]{1,0:T(4,128)} fusion(bf16[512,6912]{1,0:T(8,128)(2,1)S(1)} %bitcast.86, bf16[512,18]{1,0:T(8,128)(2,1)S(1)} %fusion.6, s32[]{:T(128)S(6)} %select_n.146, f32[3,6912]{1,0:T(4,128)S(1)} %select_reduce_fusion, bf16[3,6912]{1,0:T(4,128)(2,1)S(1)} %copy-done, f32[6912]{0:T(1024)S(1)} %fusion.43), kind=kOutput, calls=%fused_computation.3 | convolution fusion | flops 21337344 | bytes 7331332 | tf_op jit(solution)/shard_map/dot_general | solution.py:193
  130.9 1.0 fusion.7
  (27 shorter events, 0.5 us)
Async XLA Ops:
  2.3 27.6 %all-to-all-start = ((bf16[6,3,6912]{2,1,0:T(4,128)(2,1)}), bf16[6,3,6912]{2,1,0:T(4,128)(2,1)S(1)}, u32[]{:S(2)}, u32[]{:S(2)}) async-start(bf16[6,3,6912]{2,1,0:T(4,128)(2,1)} %broadcast_in_dim.38), calls=%async_computation | async-start | bytes 663552 | tf_op jit(solution)/shard_map/all_to_all | solution.py:55
  31.5 5.7 %copy-start = (bf16[3,6912]{1,0:T(4,128)(2,1)S(1)}, bf16[3,6912]{1,0:T(4,128)(2,1)}, u32[]{:S(2)}) copy-start(bf16[3,6912]{1,0:T(4,128)(2,1)} %param.6) | copy-start | bytes 124420
  42.8 50.3 %copy-start.1 = (f32[1,128,128]{2,1,0:T(8,128)S(1)}, f32[1,128,128]{2,1,0:T(8,128)}, u32[]{:S(2)}) copy-start(f32[1,128,128]{2,1,0:T(8,128)} %param.8) | copy-start | bytes 196612
  46.6 44.4 %all-to-all-start.1 = ((bf16[128,2,829]{2,1,0:T(2,128)(2,1)}), bf16[128,2,829]{2,1,0:T(2,128)(2,1)S(1)}, u32[]{:S(2)}, u32[]{:S(2)}) async-start(bf16[128,2,829]{2,1,0:T(2,128)(2,1)} %reshape.197), calls=%async_computation.1 | async-start | bytes 917504 | tf_op jit(solution)/shard_map/all_to_all | solution.py:134
  91.8 14.1 %copy-start.2 = (f32[4,8,8]{2,1,0:T(8,128)S(1)}, f32[4,8,8]{2,1,0:T(8,128)}, u32[]{:S(2)}) copy-start(f32[4,8,8]{2,1,0:T(8,128)} %param.11) | copy-start | bytes 3076
  91.8 14.2 %copy-start.3 = (s32[64]{0:T(128)S(1)}, s32[64]{0:T(128)}, u32[]{:S(2)}) copy-start(s32[64]{0:T(128)} %param.10) | copy-start | bytes 772
  98.5 25.6 %all-to-all-start.2 = ((f32[128,1,343]{2,1,0:T(1,128)}), f32[128,1,343]{2,1,0:T(1,128)S(1)}, u32[]{:S(2)}, u32[]{:S(2)}) async-start(f32[128,1,343]{2,1,0:T(1,128)} %copy.61), calls=%async_computation.2 | async-start | bytes 393216 | tf_op jit(solution)/shard_map/all_to_all | solution.py:170
  125.7 3.3 %slice-start = ((s8[7077888]{0:T(1024)(128)(4,1)}), s8[4194304]{0:T(1024)(128)(4,1)S(1)}, s32[]{:S(2)}) async-start(s8[7077888]{0:T(1024)(128)(4,1)} %bitcast.85), calls=%async_computation.3 | async-start | bytes 8388608
  126.7 2.4 %slice-start.1 = ((s8[7077888]{0:T(1024)(128)(4,1)}), s8[2883584]{0:T(1024)(128)(4,1)S(1)}, s32[]{:S(2)}) async-start(s8[7077888]{0:T(1024)(128)(4,1)} %bitcast.85), calls=%async_computation.4 | async-start | bytes 5767168

commit v12 on v11

--- a/solution.py
+++ b/solution.py
@@ -111,7 +111,7 @@
         energies[None, :] * wide,
         every.astype(jnp.float32),
         (((1,), (1,)), ((), ())),
-        precision=highest,
+        precision=lax.Precision.HIGH,
         preferred_element_type=jnp.float32,
     )
     nproj = partial_corr.shape[0]
@@ -155,7 +155,7 @@
         back_own,
         jnp.transpose(piece, (1, 0, 2)).reshape(total, side * side),
         (((1,), (1,)), ((), ())),
-        precision=highest,
+        precision=lax.Precision.HIGH,
         preferred_element_type=jnp.float32,
     )
     back = jnp.transpose(back_own.reshape(bands, npw, stick_count), (1, 0, 2))

time: 133 us -> 132 us (level)
  no operation moved by 1% of the time
where the time goes in v12:
time: 132 us; the launch traced here: 131 us
  waiting for transfers between devices  54.7 us (41%)
  starting transfers between devices  40.2 us (30%)
  matrix products  19.5 us (15%)
  local copies, waits for them, and re-layouts  10.2 us (8%)
  other arithmetic  5.79 us (4%)
    all_to_all x1, waiting for transfers between devices, local(): got = lax.all_to_all(sent, PW, 0, 0, tiled=True)  24.1 us
    all_to_all x1, starting transfers between devices, local(): got = lax.all_to_all(sent, PW, 0, 0, tiled=True)  20.3 us
    all_to_all x1, waiting for transfers between devices, local(): ret = lax.all_to_all(ret_sent, PW, 0, 0, tiled=True)  17.6 us
    all_to_all x1, waiting for transfers between devices, gathered_bands(): every = lax.all_to_all(copies, axis, 0, 0, tiled=True)  13 us
    all_to_all x1, starting transfers between devices, gathered_bands(): every = lax.all_to_all(copies, axis, 0, 0, tiled=True)  12.6 us
    all_to_all x1, starting transfers between devices, local(): ret = lax.all_to_all(ret_sent, PW, 0, 0, tiled=True)  7.2 us
    dot_general x1, matrix products, local(): lax.dot_general(every, projectors, (((1,), (1,)), ((), ())), preferred_el...  4.98 us
    dot_general x1, matrix products, local(): jnp.dot(on_plane.astype(jnp.bfloat16), spread.reshape(count, total * stic...  4.93 us
  transfers between devices with their start and end apart: 3, of which 3 were waited for; matrix products, arithmetic and copies ran while one was open for 2% of the time, Pallas kernels for 0%

profile of v12, /device:TPU:1, one launch (start us, length us, event | category | flops | bytes accessed | tf_op | source)
XLA Modules:
  0.0 131.4 jit_solution(14568222296143553249)
XLA Ops:
  0.6 1.6 %broadcast_in_dim.38 = bf16[6,3,6912]{2,1,0:T(4,128)(2,1)} broadcast(bf16[3,6912]{1,0:T(4,128)(2,1)} %param.6), dimensions={1,2} | broadcast | bytes 290304 | tf_op jit(solution)/shard_map/broadcast_in_dim | solution.py:54
  2.3 12.6 %all-to-all-start = ((bf16[6,3,6912]{2,1,0:T(4,128)(2,1)}), bf16[6,3,6912]{2,1,0:T(4,128)(2,1)S(1)}, u32[]{:S(2)}, u32[]{:S(2)}) async-start(bf16[6,3,6912]{2,1,0:T(4,128)(2,1)} %broadcast_in_dim.38), calls=%async_computation | async-start | bytes 663552 | tf_op jit(solution)/shard_map/all_to_all | solution.py:55
  14.9 0.8 add_select_fusion.2
  15.7 0.3 iota_compare_fusion.4
  16.0 0.9 fusion.43
  16.9 13.0 %all-to-all-done = bf16[6,3,6912]{2,1,0:T(4,128)(2,1)S(1)} async-done(((bf16[6,3,6912]{2,1,0:T(4,128)(2,1)}), bf16[6,3,6912]{2,1,0:T(4,128)(2,1)S(1)}, u32[]{:S(2)}, u32[]{:S(2)}) %all-to-all-start) | async-done | bytes 248864 | tf_op jit(solution)/shard_map/all_to_all | solution.py:55
  29.9 0.2 reshape.170
  30.1 1.4 %broadcast_select_fusion = bf16[6912,18,72]{0,2,1:T(8,128)(2,1)S(1)} fusion(pred[6912,72]{0,1:T(8,128)(4,1)S(1)} %iota_compare_fusion.4, bf16[6912,18]{0,1:T(8,128)(2,1)S(1)} %bitcast.92), kind=kLoop, calls=%fused_computation | loop fusion | flops 8957952 | bytes 18662400 | tf_op jit(solution)/shard_map/jit(_where)/select_n | solution.py:97
  31.5 4.9 %fusion.2 = f32[128,1296]{0,1:T(8,128)S(1)} fusion(bf16[6912,1296]{0,1:T(8,128)(2,1)S(1)} %bitcast.84, s32[6912]{0:T(1024)S(1)} %get-tuple-element.6), kind=kOutput, calls=%fused_computation.7 | convolution fusion | flops 2294120448 | bytes 18607104 | tf_op jit(solution)/shard_map/dot_general | solution.py:98
  36.4 0.7 reduce-precision_convert_fusion
  37.2 0.3 fusion.13
  37.4 0.1 reshape.173
  37.5 5.0 %fusion.96 = f32[512,18]{1,0:T(8,128)S(1)} fusion(bf16[512,6912]{1,0:T(8,128)(2,1)} %param.9, bf16[18,6912]{1,0:T(8,128)(2,1)S(1)} %reshape.170), kind=kOutput, calls=%fused_computation.166 | convolution fusion | flops 127401984 | bytes 7363584 | tf_op jit(solution)/shard_map/dot_general | solution.py:107
  42.5 0.2 reshape.172
  42.7 0.2 reshape.174
  42.9 0.1 copy.52
  43.1 0.4 concatenate.10
  43.5 0.5 broadcast.192
  44.0 1.0 reduce
  45.0 0.3 copy.76
  45.2 1.2 reshape.197
  46.5 20.3 %all-to-all-start.1 = ((bf16[128,2,829]{2,1,0:T(2,128)(2,1)}), bf16[128,2,829]{2,1,0:T(2,128)(2,1)S(1)}, u32[]{:S(2)}, u32[]{:S(2)}) async-start(bf16[128,2,829]{2,1,0:T(2,128)(2,1)} %reshape.197), calls=%async_computation.1 | async-start | bytes 917504 | tf_op jit(solution)/shard_map/all_to_all | solution.py:134
  66.8 24.1 %all-to-all-done.1 = bf16[128,2,829]{2,1,0:T(2,128)(2,1)S(1)} async-done(((bf16[128,2,829]{2,1,0:T(2,128)(2,1)}), bf16[128,2,829]{2,1,0:T(2,128)(2,1)S(1)}, u32[]{:S(2)}, u32[]{:S(2)}) %all-to-all-start.1) | async-done | bytes 424480 | tf_op jit(solution)/shard_map/all_to_all | solution.py:134
  90.9 0.6 reshape.198
  91.6 0.1 slice.37
  91.7 0.2 copy.69
  92.0 0.1 copy.70
  92.2 0.1 copy.57
  92.3 0.1 reshape.179
  92.4 0.1 copy.58
  92.5 0.5 fusion.55
  93.0 0.5 convolution_multiply_fusion.1
  93.5 0.5 fusion.28
  94.0 0.5 convolution_bitcast_fusion
  94.6 0.2 reshape.182
  94.7 0.1 reshape_reshape.3
  94.9 0.1 add_reduce_fusion
  95.0 0.4 copy.60
  95.3 0.8 reshape.183
  96.1 0.5 fusion.97
  96.6 0.1 reshape.195
  96.7 0.1 copy.59
  96.8 0.1 pad.6.clone
  97.0 0.2 maximum_bitcast_fusion
  97.2 0.8 copy.61
  98.0 7.2 %all-to-all-start.2 = ((f32[128,1,343]{2,1,0:T(1,128)}), f32[128,1,343]{2,1,0:T(1,128)S(1)}, u32[]{:S(2)}, u32[]{:S(2)}) async-start(f32[128,1,343]{2,1,0:T(1,128)} %copy.61), calls=%async_computation.2 | async-start | bytes 393216 | tf_op jit(solution)/shard_map/all_to_all | solution.py:170
  105.2 0.3 iota_compare_fusion.5
  105.5 0.2 fusion.57
  105.8 0.1 copy.66
  105.9 17.6 %all-to-all-done.2 = f32[128,1,343]{2,1,0:T(1,128)S(1)} async-done(((f32[128,1,343]{2,1,0:T(1,128)}), f32[128,1,343]{2,1,0:T(1,128)S(1)}, u32[]{:S(2)}, u32[]{:S(2)}) %all-to-all-start.2) | async-done | bytes 175648 | tf_op jit(solution)/shard_map/all_to_all | solution.py:170
  123.5 0.1 copy.62
  123.7 0.1 slice_reduce_fusion
  123.8 0.1 copy.65
  123.9 0.2 reshape.186
  124.1 0.2 div.123
  124.4 0.2 div.129
  124.6 0.5 fusion.12
  125.1 0.1 div.128
  125.2 1.0 fusion.1
  126.2 1.0 convolution_add_fusion
  127.2 0.6 fusion.6
  127.8 0.7 select_reduce_fusion
  128.5 1.8 %fusion = f32[3,6912]{1,0:T(4,128)} fusion(bf16[512,6912]{1,0:T(8,128)(2,1)S(1)} %bitcast.86, bf16[512,18]{1,0:T(8,128)(2,1)S(1)} %fusion.6, s32[]{:T(128)S(6)} %select_n.146, f32[3,6912]{1,0:T(4,128)S(1)} %select_reduce_fusion, bf16[3,6912]{1,0:T(4,128)(2,1)S(1)} %copy-done, f32[6912]{0:T(1024)S(1)} %fusion.43), kind=kOutput, calls=%fused_computation.3 | convolution fusion | flops 21337344 | bytes 7331332 | tf_op jit(solution)/shard_map/dot_general | solution.py:193
  130.3 1.0 fusion.7
  (27 shorter events, 0.5 us)
Async XLA Ops:
  2.3 27.6 %all-to-all-start = ((bf16[6,3,6912]{2,1,0:T(4,128)(2,1)}), bf16[6,3,6912]{2,1,0:T(4,128)(2,1)S(1)}, u32[]{:S(2)}, u32[]{:S(2)}) async-start(bf16[6,3,6912]{2,1,0:T(4,128)(2,1)} %broadcast_in_dim.38), calls=%async_computation | async-start | bytes 663552 | tf_op jit(solution)/shard_map/all_to_all | solution.py:55
  31.5 5.7 %copy-start = (bf16[3,6912]{1,0:T(4,128)(2,1)S(1)}, bf16[3,6912]{1,0:T(4,128)(2,1)}, u32[]{:S(2)}) copy-start(bf16[3,6912]{1,0:T(4,128)(2,1)} %param.6) | copy-start | bytes 124420
  42.7 50.3 %copy-start.1 = (f32[1,128,128]{2,1,0:T(8,128)S(1)}, f32[1,128,128]{2,1,0:T(8,128)}, u32[]{:S(2)}) copy-start(f32[1,128,128]{2,1,0:T(8,128)} %param.8) | copy-start | bytes 196612
  46.5 44.4 %all-to-all-start.1 = ((bf16[128,2,829]{2,1,0:T(2,128)(2,1)}), bf16[128,2,829]{2,1,0:T(2,128)(2,1)S(1)}, u32[]{:S(2)}, u32[]{:S(2)}) async-start(bf16[128,2,829]{2,1,0:T(2,128)(2,1)} %reshape.197), calls=%async_computation.1 | async-start | bytes 917504 | tf_op jit(solution)/shard_map/all_to_all | solution.py:134
  91.7 13.7 %copy-start.2 = (f32[4,8,8]{2,1,0:T(8,128)S(1)}, f32[4,8,8]{2,1,0:T(8,128)}, u32[]{:S(2)}) copy-start(f32[4,8,8]{2,1,0:T(8,128)} %param.11) | copy-start | bytes 3076
  91.7 13.8 %copy-start.3 = (s32[64]{0:T(128)S(1)}, s32[64]{0:T(128)}, u32[]{:S(2)}) copy-start(s32[64]{0:T(128)} %param.10) | copy-start | bytes 772
  98.0 25.6 %all-to-all-start.2 = ((f32[128,1,343]{2,1,0:T(1,128)}), f32[128,1,343]{2,1,0:T(1,128)S(1)}, u32[]{:S(2)}, u32[]{:S(2)}) async-start(f32[128,1,343]{2,1,0:T(1,128)} %copy.61), calls=%async_computation.2 | async-start | bytes 393216 | tf_op jit(solution)/shard_map/all_to_all | solution.py:170
  125.2 3.3 %slice-start = ((s8[7077888]{0:T(1024)(128)(4,1)}), s8[4194304]{0:T(1024)(128)(4,1)S(1)}, s32[]{:S(2)}) async-start(s8[7077888]{0:T(1024)(128)(4,1)} %bitcast.85), calls=%async_computation.3 | async-start | bytes 8388608
  126.2 2.4 %slice-start.1 = ((s8[7077888]{0:T(1024)(128)(4,1)}), s8[2883584]{0:T(1024)(128)(4,1)S(1)}, s32[]{:S(2)}) async-start(s8[7077888]{0:T(1024)(128)(4,1)} %bitcast.85), calls=%async_computation.4 | async-start | bytes 5767168

commit v13 on v12

--- a/solution.py
+++ b/solution.py
@@ -94,15 +94,22 @@
     stick_of = slot_map % stick_count
     on_stick = stick_of[:, None] == jnp.arange(stick_count)[None, :]
     on_plane = jnp.arange(length)[:, None] == plane_of[None, :]
-    spread = jnp.where(on_stick[:, None, :], every.T[:, :, None], jnp.zeros((), every.dtype))
-    dense = jnp.dot(
-        on_plane.astype(jnp.bfloat16),
-        spread.reshape(count, total * stick_count),
-        preferred_element_type=jnp.float32,
-    )
     z_table = cas_table(jnp.arange(length), length)
     side_table = cas_table(side_frequency(jnp.arange(side)), length)
-    columns = jnp.dot(z_table.T, dense, precision=lax.Precision.HIGH, preferred_element_type=jnp.float32)
+    plane_bf16 = on_plane.astype(jnp.bfloat16)
+
+    def z_columns(rows):
+        spread = jnp.where(on_stick[:, None, :], rows.T[:, :, None], jnp.zeros((), rows.dtype))
+        dense = jnp.dot(
+            plane_bf16, spread.reshape(count, -1), preferred_element_type=jnp.float32
+        )
+        cols = jnp.dot(z_table.T, dense, precision=lax.Precision.HIGH, preferred_element_type=jnp.float32)
+        return cols.reshape(npw, rows.shape[0] * stick_count)
+
+    own_columns = z_columns(states)
+    doubled = jnp.concatenate([every, every], axis=0)
+    others = lax.dynamic_slice_in_dim(doubled, (group + 1) * bands, total - bands, axis=0)
+    other_columns = z_columns(others)
     energies = kinetic(slot_map, owner * stick_count, stick_count, length, side)
     partial_corr = lax.dot_general(
         every, projectors, (((1,), (1,)), ((), ())), preferred_element_type=jnp.float32
@@ -118,31 +125,25 @@
     packed = jnp.concatenate([partial_corr.reshape(-1), partial_kin.reshape(-1)])
     width = -(-packed.shape[0] // npw)
     packed = jnp.pad(packed, (0, width * npw - packed.shape[0])).reshape(npw, width)
-    columns = columns.reshape(npw, total, stick_count)
-    columns_hi = lax.reduce_precision(columns, exponent_bits=8, mantissa_bits=7)
-    columns_lo = lax.dynamic_slice_in_dim(columns - columns_hi, group * bands, bands, axis=1)
+    own_hi, own_lo = split2(own_columns)
     packed_hi, packed_lo = split2(packed)
     sent = jnp.concatenate(
-        [
-            columns_hi.reshape(npw, -1).astype(jnp.bfloat16),
-            columns_lo.reshape(npw, -1).astype(jnp.bfloat16),
-            packed_hi,
-            packed_lo,
-        ],
-        axis=1,
+        [own_hi, own_lo, other_columns.astype(jnp.bfloat16), packed_hi, packed_lo], axis=1
     )
     got = lax.all_to_all(sent, PW, 0, 0, tiled=True)
-    nall = total * stick_count
     nown = bands * stick_count
-    piece = got[:, :nall].astype(jnp.float32).reshape(npw, total, stick_count)
-    mine = lax.dynamic_slice_in_dim(piece, group * bands, bands, axis=1) + got[
-        :, nall : nall + nown
-    ].astype(jnp.float32).reshape(npw, bands, stick_count)
+    noth = (total - bands) * stick_count
+    mine = (
+        got[:, :nown].astype(jnp.float32) + got[:, nown : 2 * nown].astype(jnp.float32)
+    ).reshape(npw, bands, stick_count)
+    rest = got[:, 2 * nown : 2 * nown + noth].astype(jnp.float32).reshape(npw, total - bands, stick_count)
+    tail = 2 * nown + noth
     owned = jnp.sum(
-        got[:, nall + nown : nall + nown + width].astype(jnp.float32)
-        + got[:, nall + nown + width :].astype(jnp.float32),
+        got[:, tail : tail + width].astype(jnp.float32)
+        + got[:, tail + width : tail + 2 * width].astype(jnp.float32),
         axis=0,
     )
+    piece = jnp.concatenate([mine, rest], axis=1)
     grid = jnp.transpose(mine, (1, 0, 2)).reshape(bands, planes, side, side)
     half = jnp.einsum("bzjk,jx->bzxk", grid, side_table, precision=lax.Precision.HIGH)
     real_space = jnp.einsum("bzxk,ky->bzxy", half, side_table, precision=lax.Precision.HIGH)
@@ -150,7 +151,6 @@
     back_half = jnp.einsum("bzxy,ky->bzxk", weighted, side_table, precision=lax.Precision.HIGH)
     back_grid = jnp.einsum("bzxk,jx->bzjk", back_half, side_table, precision=lax.Precision.HIGH)
     back_own = back_grid.reshape(bands, side * side)
-    piece = lax.dynamic_update_slice_in_dim(piece, mine, group * bands, axis=1)
     plane_gram = lax.dot_general(
         back_own,
         jnp.transpose(piece, (1, 0, 2)).reshape(total, side * side),
@@ -171,7 +171,8 @@
     returned = ret[:, : bands * stick_count].reshape(npw * planes, bands, stick_count)
     gram_local = jnp.sum(
         ret[:, bands * stick_count : bands * stick_count + bands * total], axis=0
-    ).reshape(bands, total)
+    ).reshape(bands, ngroup, bands)
+    gram_local = jnp.take(gram_local, (jnp.arange(ngroup) - group) % ngroup, axis=1).reshape(bands, total)
     reduced = ret[:, bands * stick_count + bands * total :].reshape(-1)
     correlations = reduced[: nproj * total].reshape(nproj, total) / math.sqrt(NG)
     gram_kin = reduced[nproj * total : nproj * total + bands * total].reshape(bands, total)

time: 132 us -> 133 us (level)
  waiting for transfers between devices: 54.7 us -> 50.2 us
  other arithmetic: 5.79 us -> 8.2 us
  local copies, waits for them, and re-layouts: 10.2 us -> 11.8 us
    all_to_all x1, waiting for transfers between devices: 13 us -> 8.62 us  [gathered_bands(): every = lax.all_to_all(copies, axis, 0, 0, tiled=True)]
    select_n x1 -> x3, other arithmetic: 1.41 us -> 2.77 us  [the longest x2 2.76 us: z_columns(): jnp.where(on_stick[:, None, :], rows.T[:, :, None], jnp.zeros((), rows.dt...]
    dot_general x2 -> x4, matrix products: 5.63 us -> 6.57 us  [the longest x2 5.2 us: z_columns(): jnp.dot(plane_bf16, spread.reshape(count, -1), preferred_element_type=jnp...]
    unnamed x19 -> x16, local copies, waits for them, and re-layouts: 2.66 us -> 3.23 us
  transfers between devices with their start and end apart: 3 -> 3, of which waited for: 3 -> 3; matrix products, arithmetic and copies ran while one was open for 2% -> 5% of each run, Pallas kernels for 0% -> 0%
where the time goes in v13:
time: 133 us; the launch traced here: 132 us
  waiting for transfers between devices  50.2 us (38%)
  starting transfers between devices  40.1 us (30%)
  matrix products  20.4 us (15%)
  local copies, waits for them, and re-layouts  11.8 us (9%)
  other arithmetic  8.2 us (6%)
    all_to_all x1, waiting for transfers between devices, local(): got = lax.all_to_all(sent, PW, 0, 0, tiled=True)  23.8 us
    all_to_all x1, starting transfers between devices, local(): got = lax.all_to_all(sent, PW, 0, 0, tiled=True)  20.3 us
    all_to_all x1, waiting for transfers between devices, local(): ret = lax.all_to_all(ret_sent, PW, 0, 0, tiled=True)  17.8 us
    all_to_all x1, starting transfers between devices, gathered_bands(): every = lax.all_to_all(copies, axis, 0, 0, tiled=True)  12.6 us
    all_to_all x1, waiting for transfers between devices, gathered_bands(): every = lax.all_to_all(copies, axis, 0, 0, tiled=True)  8.62 us
    all_to_all x1, starting transfers between devices, local(): ret = lax.all_to_all(ret_sent, PW, 0, 0, tiled=True)  7.18 us
    dot_general x2, matrix products, z_columns(): jnp.dot(plane_bf16, spread.reshape(count, -1), preferred_element_type=jnp...  5.2 us
    dot_general x1, matrix products, local(): lax.dot_general(every, projectors, (((1,), (1,)), ((), ())), preferred_el...  4.98 us
  transfers between devices with their start and end apart: 3, of which 3 were waited for; matrix products, arithmetic and copies ran while one was open for 5% of the time, Pallas kernels for 0%

profile of v13, /device:TPU:1, one launch (start us, length us, event | category | flops | bytes accessed | tf_op | source)
XLA Modules:
  0.0 131.8 jit_solution(2494458868882071187)
XLA Ops:
  0.6 1.6 %broadcast_in_dim.108 = bf16[6,3,6912]{2,1,0:T(4,128)(2,1)} broadcast(bf16[3,6912]{1,0:T(4,128)(2,1)} %param.6), dimensions={1,2} | broadcast | bytes 290304 | tf_op jit(solution)/shard_map/broadcast_in_dim | solution.py:54
  2.2 12.6 %all-to-all-start = ((bf16[6,3,6912]{2,1,0:T(4,128)(2,1)}), bf16[6,3,6912]{2,1,0:T(4,128)(2,1)S(1)}, u32[]{:S(2)}, u32[]{:S(2)}) async-start(bf16[6,3,6912]{2,1,0:T(4,128)(2,1)} %broadcast_in_dim.108), calls=%async_computation | async-start | bytes 663552 | tf_op jit(solution)/shard_map/all_to_all | solution.py:55
  14.9 0.8 add_select_fusion.2
  15.7 0.3 iota_compare_fusion.5
  15.9 0.9 fusion.45
  16.8 0.8 copy.70
  17.6 0.7 fusion.58
  18.3 1.3 broadcast_select_fusion.1
  19.7 1.0 fusion.3
  20.7 0.5 fusion.14
  21.2 8.6 %all-to-all-done = bf16[6,3,6912]{2,1,0:T(4,128)(2,1)S(1)} async-done(((bf16[6,3,6912]{2,1,0:T(4,128)(2,1)}), bf16[6,3,6912]{2,1,0:T(4,128)(2,1)S(1)}, u32[]{:S(2)}, u32[]{:S(2)}) %all-to-all-start) | async-done | bytes 248864 | tf_op jit(solution)/shard_map/all_to_all | solution.py:55
  29.8 0.2 reshape.210
  30.1 0.2 fusion.12
  30.3 1.4 %broadcast_select_fusion = bf16[6912,15,72]{0,2,1:T(8,128)(2,1)S(1)} fusion(pred[6912,72]{0,1:T(8,128)(4,1)S(1)} %iota_compare_fusion.5, bf16[6912,15]{0,1:T(8,128)(2,1)S(1)} %fusion.12), kind=kLoop, calls=%fused_computation.1 | loop fusion | flops 7464960 | bytes 15634944 | tf_op jit(solution)/shard_map/jit(_where)/select_n | solution.py:102
  31.8 4.2 %fusion.2 = f32[128,1080]{0,1:T(8,128)S(1)} fusion(bf16[6912,1080]{0,1:T(8,128)(2,1)S(1)} %bitcast.90, s32[6912]{0:T(1024)S(1)} %get-tuple-element.6), kind=kOutput, calls=%fused_computation.8 | convolution fusion | flops 1911914496 | bytes 15510528 | tf_op jit(solution)/shard_map/dot_general | solution.py:103
  35.9 0.9 convolution_convert_fusion
  36.8 0.3 fusion.17
  37.2 5.0 %fusion.103 = f32[512,18]{1,0:T(8,128)S(1)} fusion(bf16[512,6912]{1,0:T(8,128)(2,1)} %param.9, bf16[18,6912]{1,0:T(8,128)(2,1)S(1)} %reshape.210), kind=kOutput, calls=%fused_computation.184 | convolution fusion | flops 127401984 | bytes 7363584 | tf_op jit(solution)/shard_map/dot_general | solution.py:114
  42.2 0.2 reshape.211
  42.4 0.2 reshape.213
  42.7 0.4 concatenate.17
  43.1 0.5 broadcast.283
  43.6 1.0 reduce
  44.6 0.3 copy.84
  44.9 1.2 reshape.243
  46.1 20.3 %all-to-all-start.1 = ((bf16[128,2,829]{2,1,0:T(2,128)(2,1)}), bf16[128,2,829]{2,1,0:T(2,128)(2,1)S(1)}, u32[]{:S(2)}, u32[]{:S(2)}) async-start(bf16[128,2,829]{2,1,0:T(2,128)(2,1)} %reshape.243), calls=%async_computation.1 | async-start | bytes 917504 | tf_op jit(solution)/shard_map/all_to_all | solution.py:133
  66.4 0.3 iota_compare_fusion.6
  66.7 23.8 %all-to-all-done.1 = bf16[128,2,829]{2,1,0:T(2,128)(2,1)S(1)} async-done(((bf16[128,2,829]{2,1,0:T(2,128)(2,1)}), bf16[128,2,829]{2,1,0:T(2,128)(2,1)S(1)}, u32[]{:S(2)}, u32[]{:S(2)}) %all-to-all-start.1) | async-done | bytes 424480 | tf_op jit(solution)/shard_map/all_to_all | solution.py:133
  90.5 0.6 reshape.244
  91.3 0.1 slice.44
  91.6 0.1 copy.63
  91.7 0.1 reshape.215
  91.8 0.1 copy.64
  92.0 0.5 fusion.57
  92.5 0.5 convolution_multiply_fusion.1
  93.0 0.5 fusion.30
  93.5 0.5 convolution_bitcast_fusion
  94.0 0.2 reshape.218
  94.1 0.1 reshape_reshape.3
  94.3 0.1 add_reduce_fusion
  94.4 0.2 copy.78
  94.7 0.4 copy.67
  95.0 0.8 reshape.221
  95.8 0.5 fusion.104
  96.4 0.1 copy.65
  96.7 0.2 maximum_bitcast_fusion.1
  96.9 0.8 copy.68
  97.7 7.2 %all-to-all-start.2 = ((f32[128,1,343]{2,1,0:T(1,128)}), f32[128,1,343]{2,1,0:T(1,128)S(1)}, u32[]{:S(2)}, u32[]{:S(2)}) async-start(f32[128,1,343]{2,1,0:T(1,128)} %copy.68), calls=%async_computation.2 | async-start | bytes 393216 | tf_op jit(solution)/shard_map/all_to_all | solution.py:170
  104.9 0.2 fusion.59
  105.1 0.1 copy.73
  105.5 17.8 %all-to-all-done.2 = f32[128,1,343]{2,1,0:T(1,128)S(1)} async-done(((f32[128,1,343]{2,1,0:T(1,128)}), f32[128,1,343]{2,1,0:T(1,128)S(1)}, u32[]{:S(2)}, u32[]{:S(2)}) %all-to-all-start.2) | async-done | bytes 175648 | tf_op jit(solution)/shard_map/all_to_all | solution.py:170
  123.2 0.1 copy.69
  123.5 0.2 reshape.224
  123.7 0.2 div.123
  123.9 0.2 div.128
  124.2 0.1 slice_reduce_fusion
  124.3 0.5 fusion.16
  125.0 0.6 gather_fusion
  125.7 1.0 fusion.1
  126.6 1.0 convolution_add_fusion
  127.6 0.6 fusion.8
  128.2 0.7 select_reduce_fusion
  129.0 1.8 %fusion = f32[3,6912]{1,0:T(4,128)} fusion(bf16[512,6912]{1,0:T(8,128)(2,1)S(1)} %bitcast.92, bf16[512,18]{1,0:T(8,128)(2,1)S(1)} %fusion.8, s32[]{:T(128)S(6)} %select_n.198, f32[3,6912]{1,0:T(4,128)S(1)} %select_reduce_fusion, bf16[3,6912]{1,0:T(4,128)(2,1)S(1)} %copy-done, f32[6912]{0:T(1024)S(1)} %fusion.45), kind=kOutput, calls=%fused_computation.4 | convolution fusion | flops 21337344 | bytes 7331332 | tf_op jit(solution)/shard_map/dot_general | solution.py:194
  130.8 1.0 fusion.9
  (38 shorter events, 1.4 us)
Async XLA Ops:
  2.2 27.6 %all-to-all-start = ((bf16[6,3,6912]{2,1,0:T(4,128)(2,1)}), bf16[6,3,6912]{2,1,0:T(4,128)(2,1)S(1)}, u32[]{:S(2)}, u32[]{:S(2)}) async-start(bf16[6,3,6912]{2,1,0:T(4,128)(2,1)} %broadcast_in_dim.108), calls=%async_computation | async-start | bytes 663552 | tf_op jit(solution)/shard_map/all_to_all | solution.py:55
  31.7 5.1 %copy-start = (bf16[3,6912]{1,0:T(4,128)(2,1)S(1)}, bf16[3,6912]{1,0:T(4,128)(2,1)}, u32[]{:S(2)}) copy-start(bf16[3,6912]{1,0:T(4,128)(2,1)} %param.6) | copy-start | bytes 124420
  42.2 50.3 %copy-start.1 = (f32[1,128,128]{2,1,0:T(8,128)S(1)}, f32[1,128,128]{2,1,0:T(8,128)}, u32[]{:S(2)}) copy-start(f32[1,128,128]{2,1,0:T(8,128)} %param.8) | copy-start | bytes 196612
  46.1 44.4 %all-to-all-start.1 = ((bf16[128,2,829]{2,1,0:T(2,128)(2,1)}), bf16[128,2,829]{2,1,0:T(2,128)(2,1)S(1)}, u32[]{:S(2)}, u32[]{:S(2)}) async-start(bf16[128,2,829]{2,1,0:T(2,128)(2,1)} %reshape.243), calls=%async_computation.1 | async-start | bytes 917504 | tf_op jit(solution)/shard_map/all_to_all | solution.py:133
  91.5 13.3 %copy-start.2 = (s32[64]{0:T(128)S(1)}, s32[64]{0:T(128)}, u32[]{:S(2)}) copy-start(s32[64]{0:T(128)} %param.10) | copy-start | bytes 772
  97.7 25.5 %all-to-all-start.2 = ((f32[128,1,343]{2,1,0:T(1,128)}), f32[128,1,343]{2,1,0:T(1,128)S(1)}, u32[]{:S(2)}, u32[]{:S(2)}) async-start(f32[128,1,343]{2,1,0:T(1,128)} %copy.68), calls=%async_computation.2 | async-start | bytes 393216 | tf_op jit(solution)/shard_map/all_to_all | solution.py:170
  125.7 3.3 %slice-start = ((s8[7077888]{0:T(1024)(128)(4,1)}), s8[4194304]{0:T(1024)(128)(4,1)S(1)}, s32[]{:S(2)}) async-start(s8[7077888]{0:T(1024)(128)(4,1)} %bitcast.91), calls=%async_computation.3 | async-start | bytes 8388608
  126.6 2.4 %slice-start.1 = ((s8[7077888]{0:T(1024)(128)(4,1)}), s8[2883584]{0:T(1024)(128)(4,1)S(1)}, s32[]{:S(2)}) async-start(s8[7077888]{0:T(1024)(128)(4,1)} %bitcast.91), calls=%async_computation.4 | async-start | bytes 5767168

commit v14 on v12

--- a/solution.py
+++ b/solution.py
@@ -71,8 +71,8 @@
 
 def exact_select(x, onehot):
     hi, lo = split2(x)
-    dot = lambda a: jnp.dot(a, onehot, preferred_element_type=jnp.float32)
-    return dot(hi) + dot(lo)
+    both = jnp.dot(jnp.concatenate([hi, lo], axis=0), onehot, preferred_element_type=jnp.float32)
+    return both[: x.shape[0]] + both[x.shape[0] :]
 
 
 def local(states, slot_map, potential, projectors, species, coupling):

time: 132 us -> 135 us (1.023)
  matrix products: 19.5 us -> 22.2 us
    dot_general x1, matrix products: 1.8 us -> 4.8 us  [local(): lax.dot_general(lax.dynamic_slice_in_dim(weights, group * bands, bands, a...]
where the time goes in v14:
time: 135 us
  waiting for transfers between devices  54.7 us (41%)
  starting transfers between devices  40.2 us (30%)
  matrix products  22.2 us (16%)
  local copies, waits for them, and re-layouts  10.1 us (7%)
  other arithmetic  6.37 us (5%)
    all_to_all x1, waiting for transfers between devices, local(): got = lax.all_to_all(sent, PW, 0, 0, tiled=True)  24.1 us
    all_to_all x1, starting transfers between devices, local(): got = lax.all_to_all(sent, PW, 0, 0, tiled=True)  20.3 us
    all_to_all x1, waiting for transfers between devices, local(): ret = lax.all_to_all(ret_sent, PW, 0, 0, tiled=True)  17.6 us
    all_to_all x1, waiting for transfers between devices, gathered_bands(): every = lax.all_to_all(copies, axis, 0, 0, tiled=True)  13 us
    all_to_all x1, starting transfers between devices, gathered_bands(): every = lax.all_to_all(copies, axis, 0, 0, tiled=True)  12.6 us
    all_to_all x1, starting transfers between devices, local(): ret = lax.all_to_all(ret_sent, PW, 0, 0, tiled=True)  7.19 us
    dot_general x1, matrix products, local(): lax.dot_general(every, projectors, (((1,), (1,)), ((), ())), preferred_el...  4.97 us
    dot_general x1, matrix products, local(): jnp.dot(on_plane.astype(jnp.bfloat16), spread.reshape(count, total * stic...  4.93 us
  transfers between devices with their start and end apart: 3, of which 3 were waited for; matrix products, arithmetic and copies ran while one was open for 2% of the time, Pallas kernels for 0%

profile of v14, /device:TPU:1, one launch (start us, length us, event | category | flops | bytes accessed | tf_op | source)
XLA Modules:
  0.0 134.6 jit_solution(10265704878292054753)
XLA Ops:
  0.6 1.6 %broadcast_in_dim.38 = bf16[6,3,6912]{2,1,0:T(4,128)(2,1)} broadcast(bf16[3,6912]{1,0:T(4,128)(2,1)} %param.6), dimensions={1,2} | broadcast | bytes 290304 | tf_op jit(solution)/shard_map/broadcast_in_dim | solution.py:54
  2.2 12.6 %all-to-all-start = ((bf16[6,3,6912]{2,1,0:T(4,128)(2,1)}), bf16[6,3,6912]{2,1,0:T(4,128)(2,1)S(1)}, u32[]{:S(2)}, u32[]{:S(2)}) async-start(bf16[6,3,6912]{2,1,0:T(4,128)(2,1)} %broadcast_in_dim.38), calls=%async_computation | async-start | bytes 663552 | tf_op jit(solution)/shard_map/all_to_all | solution.py:55
  14.9 0.8 add_select_fusion.2
  15.7 0.3 iota_compare_fusion.3
  16.0 0.9 fusion.44
  16.8 13.0 %all-to-all-done = bf16[6,3,6912]{2,1,0:T(4,128)(2,1)S(1)} async-done(((bf16[6,3,6912]{2,1,0:T(4,128)(2,1)}), bf16[6,3,6912]{2,1,0:T(4,128)(2,1)S(1)}, u32[]{:S(2)}, u32[]{:S(2)}) %all-to-all-start) | async-done | bytes 248864 | tf_op jit(solution)/shard_map/all_to_all | solution.py:55
  29.8 0.2 reshape.170
  30.1 1.4 %broadcast_select_fusion = bf16[6912,18,72]{0,2,1:T(8,128)(2,1)S(1)} fusion(pred[6912,72]{0,1:T(8,128)(4,1)S(1)} %iota_compare_fusion.3, bf16[6912,18]{0,1:T(8,128)(2,1)S(1)} %bitcast.92), kind=kLoop, calls=%fused_computation | loop fusion | flops 8957952 | bytes 18662400 | tf_op jit(solution)/shard_map/jit(_where)/select_n | solution.py:97
  31.5 4.9 %fusion.2 = f32[128,1296]{0,1:T(8,128)S(1)} fusion(bf16[6912,1296]{0,1:T(8,128)(2,1)S(1)} %bitcast.86, s32[6912]{0:T(1024)S(1)} %get-tuple-element.8), kind=kOutput, calls=%fused_computation.7 | convolution fusion | flops 2294120448 | bytes 18607104 | tf_op jit(solution)/shard_map/dot_general | solution.py:98
  36.4 0.7 reduce-precision_convert_fusion
  37.1 0.3 fusion.15
  37.4 0.1 reshape.173
  37.5 5.0 %fusion.98 = f32[512,18]{1,0:T(8,128)S(1)} fusion(bf16[512,6912]{1,0:T(8,128)(2,1)} %param.9, bf16[18,6912]{1,0:T(8,128)(2,1)S(1)} %reshape.170), kind=kOutput, calls=%fused_computation.169 | convolution fusion | flops 127401984 | bytes 7363584 | tf_op jit(solution)/shard_map/dot_general | solution.py:107
  42.5 0.2 reshape.172
  42.7 0.2 reshape.174
  42.9 0.1 copy.52
  43.1 0.4 concatenate.13
  43.5 0.5 broadcast.194
  44.0 1.0 reduce
  45.0 0.3 copy.76
  45.2 1.2 reshape.197
  46.4 20.3 %all-to-all-start.1 = ((bf16[128,2,829]{2,1,0:T(2,128)(2,1)}), bf16[128,2,829]{2,1,0:T(2,128)(2,1)S(1)}, u32[]{:S(2)}, u32[]{:S(2)}) async-start(bf16[128,2,829]{2,1,0:T(2,128)(2,1)} %reshape.197), calls=%async_computation.1 | async-start | bytes 917504 | tf_op jit(solution)/shard_map/all_to_all | solution.py:134
  66.8 24.1 %all-to-all-done.1 = bf16[128,2,829]{2,1,0:T(2,128)(2,1)S(1)} async-done(((bf16[128,2,829]{2,1,0:T(2,128)(2,1)}), bf16[128,2,829]{2,1,0:T(2,128)(2,1)S(1)}, u32[]{:S(2)}, u32[]{:S(2)}) %all-to-all-start.1) | async-done | bytes 424480 | tf_op jit(solution)/shard_map/all_to_all | solution.py:134
  90.8 0.6 reshape.198
  91.6 0.1 slice.45
  91.7 0.2 copy.69
  92.0 0.1 copy.70
  92.1 0.1 copy.57
  92.3 0.1 reshape.179
  92.4 0.1 copy.58
  92.5 0.5 fusion.56
  93.0 0.5 convolution_multiply_fusion.1
  93.5 0.5 fusion.29
  94.0 0.5 convolution_bitcast_fusion
  94.5 0.2 reshape.182
  94.7 0.1 reshape_reshape.3
  94.8 0.1 add_reduce_fusion
  95.0 0.4 copy.60
  95.3 0.8 reshape.183
  96.1 0.5 fusion.99
  96.6 0.1 reshape.195
  96.7 0.1 copy.59
  96.9 0.1 pad.9.clone
  97.0 0.2 maximum_bitcast_fusion
  97.2 0.8 copy.61
  98.0 7.2 %all-to-all-start.2 = ((f32[128,1,343]{2,1,0:T(1,128)}), f32[128,1,343]{2,1,0:T(1,128)S(1)}, u32[]{:S(2)}, u32[]{:S(2)}) async-start(f32[128,1,343]{2,1,0:T(1,128)} %copy.61), calls=%async_computation.2 | async-start | bytes 393216 | tf_op jit(solution)/shard_map/all_to_all | solution.py:170
  105.2 0.3 iota_compare_fusion.4
  105.5 0.2 fusion.58
  105.7 0.1 copy.66
  105.9 17.6 %all-to-all-done.2 = f32[128,1,343]{2,1,0:T(1,128)S(1)} async-done(((f32[128,1,343]{2,1,0:T(1,128)}), f32[128,1,343]{2,1,0:T(1,128)S(1)}, u32[]{:S(2)}, u32[]{:S(2)}) %all-to-all-start.2) | async-done | bytes 175648 | tf_op jit(solution)/shard_map/all_to_all | solution.py:170
  123.5 0.1 copy.62
  123.7 0.1 slice_reduce_fusion
  123.8 0.1 copy.65
  123.9 0.2 reshape.186
  124.1 0.2 div.123
  124.4 0.2 div.129
  124.6 0.5 reduce-precision_convert_fusion.1
  125.1 0.1 div.128
  125.2 1.7 %fusion.1 = f32[432,6912]{1,0:T(8,128)S(1)} fusion(s32[6912]{0:T(1024)S(1)} %get-tuple-element.8, bf16[216,128]{1,0:T(8,128)(2,1)S(1)} %get-tuple-element.5, bf16[216,128]{1,0:T(8,128)(2,1)S(1)} %get-tuple-element.4), kind=kOutput, calls=%fused_computation.6 | convolution fusion | flops 765517824 | bytes 12082176 | tf_op jit(solution)/shard_map/dot_general | solution.py:74
  126.9 0.6 slice_add_fusion
  127.5 0.6 fusion.5
  128.1 0.7 select_reduce_fusion
  128.8 4.8 %fusion = f32[3,6912]{1,0:T(4,128)} fusion(bf16[512,6912]{1,0:T(8,128)(2,1)} %param.9, bf16[512,18]{1,0:T(8,128)(2,1)S(1)} %fusion.5, s32[]{:T(128)S(6)} %select_n.146, f32[3,6912]{1,0:T(4,128)S(1)} %select_reduce_fusion, bf16[3,6912]{1,0:T(4,128)(2,1)S(1)} %copy-done, f32[6912]{0:T(1024)S(1)} %fusion.44), kind=kOutput, calls=%fused_computation.2 | convolution fusion | flops 21337344 | bytes 7331332 | tf_op jit(solution)/shard_map/dot_general | solution.py:193
  133.6 1.0 fusion.6
  (22 shorter events, 0.4 us)
Async XLA Ops:
  2.2 27.6 %all-to-all-start = ((bf16[6,3,6912]{2,1,0:T(4,128)(2,1)}), bf16[6,3,6912]{2,1,0:T(4,128)(2,1)S(1)}, u32[]{:S(2)}, u32[]{:S(2)}) async-start(bf16[6,3,6912]{2,1,0:T(4,128)(2,1)} %broadcast_in_dim.38), calls=%async_computation | async-start | bytes 663552 | tf_op jit(solution)/shard_map/all_to_all | solution.py:55
  31.5 5.7 %copy-start = (bf16[3,6912]{1,0:T(4,128)(2,1)S(1)}, bf16[3,6912]{1,0:T(4,128)(2,1)}, u32[]{:S(2)}) copy-start(bf16[3,6912]{1,0:T(4,128)(2,1)} %param.6) | copy-start | bytes 124420
  42.5 50.5 %copy-start.1 = (f32[1,128,128]{2,1,0:T(8,128)S(1)}, f32[1,128,128]{2,1,0:T(8,128)}, u32[]{:S(2)}) copy-start(f32[1,128,128]{2,1,0:T(8,128)} %param.8) | copy-start | bytes 196612
  46.4 44.4 %all-to-all-start.1 = ((bf16[128,2,829]{2,1,0:T(2,128)(2,1)}), bf16[128,2,829]{2,1,0:T(2,128)(2,1)S(1)}, u32[]{:S(2)}, u32[]{:S(2)}) async-start(bf16[128,2,829]{2,1,0:T(2,128)(2,1)} %reshape.197), calls=%async_computation.1 | async-start | bytes 917504 | tf_op jit(solution)/shard_map/all_to_all | solution.py:134
  91.5 13.9 %copy-start.2 = (f32[4,8,8]{2,1,0:T(8,128)S(1)}, f32[4,8,8]{2,1,0:T(8,128)}, u32[]{:S(2)}) copy-start(f32[4,8,8]{2,1,0:T(8,128)} %param.11) | copy-start | bytes 3076
  91.5 14.0 %copy-start.3 = (s32[64]{0:T(128)S(1)}, s32[64]{0:T(128)}, u32[]{:S(2)}) copy-start(s32[64]{0:T(128)} %param.10) | copy-start | bytes 772
  98.0 25.6 %all-to-all-start.2 = ((f32[128,1,343]{2,1,0:T(1,128)}), f32[128,1,343]{2,1,0:T(1,128)S(1)}, u32[]{:S(2)}, u32[]{:S(2)}) async-start(f32[128,1,343]{2,1,0:T(1,128)} %copy.61), calls=%async_computation.2 | async-start | bytes 393216 | tf_op jit(solution)/shard_map/all_to_all | solution.py:170

commit v15 on v12

--- a/solution.py
+++ b/solution.py
@@ -185,9 +185,9 @@
     kinds = coupling.shape[0]
     symmetric = 0.5 * (coupling + jnp.swapaxes(coupling, 1, 2))
     onehot = (species[:, None] == jnp.arange(kinds)[None, :]).astype(jnp.float32)
-    chosen = jnp.einsum("as,smn->amn", onehot, symmetric, precision=highest)
+    chosen = jnp.einsum("as,smn->amn", onehot, symmetric, precision=lax.Precision.HIGH)
     weights = jnp.einsum(
-        "amn,anb->amb", chosen, correlations.reshape(atoms, per_atom, total), precision=highest
+        "amn,anb->amb", chosen, correlations.reshape(atoms, per_atom, total), precision=lax.Precision.HIGH
     )
     weights = weights.reshape(atoms * per_atom, total).astype(jnp.bfloat16)
     nonlocal_term = lax.dot_general(
@@ -198,7 +198,7 @@
         lax.dynamic_slice_in_dim(correlations, group * bands, bands, axis=1),
         weights.astype(jnp.float32),
         (((0,), (0,)), ((), ())),
-        precision=highest,
+        precision=lax.Precision.HIGH,
         preferred_element_type=jnp.float32,
     ) / (math.sqrt(atoms * per_atom) * math.sqrt(NG))
     subspace = (gram_kin + gram_local) / float(NG) + cross

time: 132 us -> 132 us (level)
  no operation moved by 1% of the time
where the time goes in v15:
time: 132 us; the launch traced here: 131 us
  waiting for transfers between devices  54.7 us (41%)
  starting transfers between devices  40.2 us (30%)
  matrix products  19.2 us (15%)
  local copies, waits for them, and re-layouts  10.4 us (8%)
  other arithmetic  5.79 us (4%)
    all_to_all x1, waiting for transfers between devices, local(): got = lax.all_to_all(sent, PW, 0, 0, tiled=True)  24.1 us
    all_to_all x1, starting transfers between devices, local(): got = lax.all_to_all(sent, PW, 0, 0, tiled=True)  20.3 us
    all_to_all x1, waiting for transfers between devices, local(): ret = lax.all_to_all(ret_sent, PW, 0, 0, tiled=True)  17.6 us
    all_to_all x1, waiting for transfers between devices, gathered_bands(): every = lax.all_to_all(copies, axis, 0, 0, tiled=True)  13 us
    all_to_all x1, starting transfers between devices, gathered_bands(): every = lax.all_to_all(copies, axis, 0, 0, tiled=True)  12.6 us
    all_to_all x1, starting transfers between devices, local(): ret = lax.all_to_all(ret_sent, PW, 0, 0, tiled=True)  7.19 us
    dot_general x1, matrix products, local(): lax.dot_general(every, projectors, (((1,), (1,)), ((), ())), preferred_el...  4.98 us
    dot_general x1, matrix products, local(): jnp.dot(on_plane.astype(jnp.bfloat16), spread.reshape(count, total * stic...  4.93 us
  transfers between devices with their start and end apart: 3, of which 3 were waited for; matrix products, arithmetic and copies ran while one was open for 2% of the time, Pallas kernels for 0%

profile of v15, /device:TPU:1, one launch (start us, length us, event | category | flops | bytes accessed | tf_op | source)
XLA Modules:
  0.0 131.3 jit_solution(7949323179357234458)
XLA Ops:
  0.6 1.6 %broadcast_in_dim.38 = bf16[6,3,6912]{2,1,0:T(4,128)(2,1)} broadcast(bf16[3,6912]{1,0:T(4,128)(2,1)} %param.6), dimensions={1,2} | broadcast | bytes 290304 | tf_op jit(solution)/shard_map/broadcast_in_dim | solution.py:54
  2.3 12.6 %all-to-all-start = ((bf16[6,3,6912]{2,1,0:T(4,128)(2,1)}), bf16[6,3,6912]{2,1,0:T(4,128)(2,1)S(1)}, u32[]{:S(2)}, u32[]{:S(2)}) async-start(bf16[6,3,6912]{2,1,0:T(4,128)(2,1)} %broadcast_in_dim.38), calls=%async_computation | async-start | bytes 663552 | tf_op jit(solution)/shard_map/all_to_all | solution.py:55
  14.9 0.8 add_select_fusion.2
  15.7 0.3 iota_compare_fusion.4
  16.0 0.9 fusion.43
  16.9 13.0 %all-to-all-done = bf16[6,3,6912]{2,1,0:T(4,128)(2,1)S(1)} async-done(((bf16[6,3,6912]{2,1,0:T(4,128)(2,1)}), bf16[6,3,6912]{2,1,0:T(4,128)(2,1)S(1)}, u32[]{:S(2)}, u32[]{:S(2)}) %all-to-all-start) | async-done | bytes 248864 | tf_op jit(solution)/shard_map/all_to_all | solution.py:55
  29.9 0.2 reshape.170
  30.1 1.4 %broadcast_select_fusion = bf16[6912,18,72]{0,2,1:T(8,128)(2,1)S(1)} fusion(pred[6912,72]{0,1:T(8,128)(4,1)S(1)} %iota_compare_fusion.4, bf16[6912,18]{0,1:T(8,128)(2,1)S(1)} %bitcast.92), kind=kLoop, calls=%fused_computation | loop fusion | flops 8957952 | bytes 18662400 | tf_op jit(solution)/shard_map/jit(_where)/select_n | solution.py:97
  31.5 4.9 %fusion.2 = f32[128,1296]{0,1:T(8,128)S(1)} fusion(bf16[6912,1296]{0,1:T(8,128)(2,1)S(1)} %bitcast.84, s32[6912]{0:T(1024)S(1)} %get-tuple-element.6), kind=kOutput, calls=%fused_computation.7 | convolution fusion | flops 2294120448 | bytes 18607104 | tf_op jit(solution)/shard_map/dot_general | solution.py:98
  36.4 0.7 reduce-precision_convert_fusion
  37.2 0.3 fusion.13
  37.4 0.1 reshape.173
  37.5 5.0 %fusion.96 = f32[512,18]{1,0:T(8,128)S(1)} fusion(bf16[512,6912]{1,0:T(8,128)(2,1)} %param.9, bf16[18,6912]{1,0:T(8,128)(2,1)S(1)} %reshape.170), kind=kOutput, calls=%fused_computation.166 | convolution fusion | flops 127401984 | bytes 7363584 | tf_op jit(solution)/shard_map/dot_general | solution.py:107
  42.5 0.2 reshape.172
  42.7 0.2 reshape.174
  42.9 0.1 copy.52
  43.1 0.4 concatenate.10
  43.5 0.5 broadcast.192
  44.0 1.0 reduce
  45.0 0.3 copy.76
  45.2 1.2 reshape.197
  46.5 20.3 %all-to-all-start.1 = ((bf16[128,2,829]{2,1,0:T(2,128)(2,1)}), bf16[128,2,829]{2,1,0:T(2,128)(2,1)S(1)}, u32[]{:S(2)}, u32[]{:S(2)}) async-start(bf16[128,2,829]{2,1,0:T(2,128)(2,1)} %reshape.197), calls=%async_computation.1 | async-start | bytes 917504 | tf_op jit(solution)/shard_map/all_to_all | solution.py:134
  66.8 24.1 %all-to-all-done.1 = bf16[128,2,829]{2,1,0:T(2,128)(2,1)S(1)} async-done(((bf16[128,2,829]{2,1,0:T(2,128)(2,1)}), bf16[128,2,829]{2,1,0:T(2,128)(2,1)S(1)}, u32[]{:S(2)}, u32[]{:S(2)}) %all-to-all-start.1) | async-done | bytes 424480 | tf_op jit(solution)/shard_map/all_to_all | solution.py:134
  90.9 0.6 reshape.198
  91.6 0.1 slice.37
  91.7 0.2 copy.69
  92.0 0.1 copy.70
  92.2 0.1 copy.57
  92.3 0.1 reshape.179
  92.4 0.1 copy.58
  92.5 0.5 fusion.55
  93.0 0.5 convolution_multiply_fusion.1
  93.5 0.5 fusion.28
  94.0 0.5 convolution_bitcast_fusion
  94.6 0.2 reshape.182
  94.7 0.1 reshape_reshape.3
  94.9 0.1 add_reduce_fusion
  95.0 0.4 copy.60
  95.3 0.8 reshape.183
  96.1 0.5 fusion.97
  96.6 0.1 reshape.195
  96.7 0.1 copy.59
  97.0 0.2 maximum_bitcast_fusion
  97.2 0.8 copy.61
  98.0 7.2 %all-to-all-start.2 = ((f32[128,1,343]{2,1,0:T(1,128)}), f32[128,1,343]{2,1,0:T(1,128)S(1)}, u32[]{:S(2)}, u32[]{:S(2)}) async-start(f32[128,1,343]{2,1,0:T(1,128)} %copy.61), calls=%async_computation.2 | async-start | bytes 393216 | tf_op jit(solution)/shard_map/all_to_all | solution.py:170
  105.2 0.3 iota_compare_fusion.5
  105.5 0.2 fusion.57
  105.7 0.1 copy.66
  105.9 17.6 %all-to-all-done.2 = f32[128,1,343]{2,1,0:T(1,128)S(1)} async-done(((f32[128,1,343]{2,1,0:T(1,128)}), f32[128,1,343]{2,1,0:T(1,128)S(1)}, u32[]{:S(2)}, u32[]{:S(2)}) %all-to-all-start.2) | async-done | bytes 175648 | tf_op jit(solution)/shard_map/all_to_all | solution.py:170
  123.5 0.1 copy.62
  123.7 0.1 slice_reduce_fusion
  123.8 0.1 copy.65
  123.9 0.2 reshape.186
  124.1 0.2 div.123
  124.4 0.2 div.129
  124.6 0.5 fusion.12
  125.1 0.1 div.128
  125.2 1.0 fusion.1
  126.2 1.0 convolution_add_fusion
  127.2 0.4 fusion.6
  127.6 0.7 select_reduce_fusion
  128.3 0.3 slice-done.1
  128.5 1.8 %fusion = f32[3,6912]{1,0:T(4,128)} fusion(bf16[512,6912]{1,0:T(8,128)(2,1)S(1)} %bitcast.86, bf16[512,18]{1,0:T(8,128)(2,1)S(1)} %fusion.6, s32[]{:T(128)S(6)} %select_n.146, f32[3,6912]{1,0:T(4,128)S(1)} %select_reduce_fusion, bf16[3,6912]{1,0:T(4,128)(2,1)S(1)} %copy-done, f32[6912]{0:T(1024)S(1)} %fusion.43), kind=kOutput, calls=%fused_computation.3 | convolution fusion | flops 21337344 | bytes 7331332 | tf_op jit(solution)/shard_map/dot_general | solution.py:193
  130.3 1.0 fusion.7
  (27 shorter events, 0.5 us)
Async XLA Ops:
  2.3 27.6 %all-to-all-start = ((bf16[6,3,6912]{2,1,0:T(4,128)(2,1)}), bf16[6,3,6912]{2,1,0:T(4,128)(2,1)S(1)}, u32[]{:S(2)}, u32[]{:S(2)}) async-start(bf16[6,3,6912]{2,1,0:T(4,128)(2,1)} %broadcast_in_dim.38), calls=%async_computation | async-start | bytes 663552 | tf_op jit(solution)/shard_map/all_to_all | solution.py:55
  31.5 5.7 %copy-start = (bf16[3,6912]{1,0:T(4,128)(2,1)S(1)}, bf16[3,6912]{1,0:T(4,128)(2,1)}, u32[]{:S(2)}) copy-start(bf16[3,6912]{1,0:T(4,128)(2,1)} %param.6) | copy-start | bytes 124420
  42.7 50.3 %copy-start.1 = (f32[1,128,128]{2,1,0:T(8,128)S(1)}, f32[1,128,128]{2,1,0:T(8,128)}, u32[]{:S(2)}) copy-start(f32[1,128,128]{2,1,0:T(8,128)} %param.8) | copy-start | bytes 196612
  46.5 44.4 %all-to-all-start.1 = ((bf16[128,2,829]{2,1,0:T(2,128)(2,1)}), bf16[128,2,829]{2,1,0:T(2,128)(2,1)S(1)}, u32[]{:S(2)}, u32[]{:S(2)}) async-start(bf16[128,2,829]{2,1,0:T(2,128)(2,1)} %reshape.197), calls=%async_computation.1 | async-start | bytes 917504 | tf_op jit(solution)/shard_map/all_to_all | solution.py:134
  91.7 13.7 %copy-start.2 = (f32[4,8,8]{2,1,0:T(8,128)S(1)}, f32[4,8,8]{2,1,0:T(8,128)}, u32[]{:S(2)}) copy-start(f32[4,8,8]{2,1,0:T(8,128)} %param.11) | copy-start | bytes 3076
  91.7 13.8 %copy-start.3 = (s32[64]{0:T(128)S(1)}, s32[64]{0:T(128)}, u32[]{:S(2)}) copy-start(s32[64]{0:T(128)} %param.10) | copy-start | bytes 772
  98.0 25.6 %all-to-all-start.2 = ((f32[128,1,343]{2,1,0:T(1,128)}), f32[128,1,343]{2,1,0:T(1,128)S(1)}, u32[]{:S(2)}, u32[]{:S(2)}) async-start(f32[128,1,343]{2,1,0:T(1,128)} %copy.61), calls=%async_computation.2 | async-start | bytes 393216 | tf_op jit(solution)/shard_map/all_to_all | solution.py:170
  125.2 3.1 %slice-start = ((s8[7077888]{0:T(1024)(128)(4,1)}), s8[4194304]{0:T(1024)(128)(4,1)S(1)}, s32[]{:S(2)}) async-start(s8[7077888]{0:T(1024)(128)(4,1)} %bitcast.85), calls=%async_computation.3 | async-start | bytes 8388608
  126.2 2.4 %slice-start.1 = ((s8[7077888]{0:T(1024)(128)(4,1)}), s8[2883584]{0:T(1024)(128)(4,1)S(1)}, s32[]{:S(2)}) async-start(s8[7077888]{0:T(1024)(128)(4,1)} %bitcast.85), calls=%async_computation.4 | async-start | bytes 5767168
